TPU v7x, 128 devices: a whole 4x4x4 slice. The times are simulated.
128 devices in a mesh: chan: 32 (over x, y_lo, z), blk: 4 (over y_hi, core).
Axes of the slice: x: 4, y: 4 (y_hi: 2, y_lo: 2; y = y_hi * 2 + y_lo), z: 4, core: 2. Of those that a mesh axis runs over, the one named last changes fastest.
Arguments:
- voltages: int32 [2048, 134656], P(('chan', 'blk')), may hold values from -128 to 127
- flags: int32 [2048], P(('chan', 'blk')), may hold values 0 or 1
- model_amp: float32 [128, 2048], P('chan'), may hold values from 0.04 to 0.4
- model_phase: float32 [128, 2048], P('chan'), may hold values from -3.140625 to 3.140625
Outputs:
- visibility: bfloat16 [2, 128, 2048, 2048], P(None, 'chan', 'blk')
- gains: float32 [2, 128, 2048], P(None, None, ('chan', 'blk'))
All inputs are finite; a program needn't handle non-finite values. No bound on the sum of `flags` on one device may be relied on, other than what follows from the above.
Results may differ from a plain program's by a relative error of at most 0.0091.
Values may be sent and summed in bfloat16 or wider, within the bound.
No kernel may reach another device: no remote copies, remote signals or barrier semaphores. Data moves between devices by JAX's collectives and lax.ppermute only.
A program may use at most 256 MiB of HBM per device.

v0:
```python
import math

import jax
import jax.numpy as jnp
from jax import lax
from jax.sharding import PartitionSpec as P

CHANS = 128
FRAME = 512
TAPS = 8
BAND_START = 64
SPECTRA = 256
ITERS = 10


def window_table():
    index = jnp.arange(TAPS * FRAME, dtype=jnp.float32)
    offset = (index - TAPS * FRAME / 2 + 0.5) / FRAME
    taper = 0.5 - 0.5 * jnp.cos(2.0 * math.pi * (index + 0.5) / (TAPS * FRAME))
    return (jnp.sinc(offset) * taper).reshape(TAPS, FRAME)


def transform_table():
    sample = jnp.arange(FRAME, dtype=jnp.int32)
    channel = BAND_START + jnp.arange(CHANS, dtype=jnp.int32)
    angle = (sample[:, None] * channel[None, :] % FRAME).astype(jnp.float32) * (
        2.0 * math.pi / FRAME
    )
    return jnp.stack([jnp.cos(angle), -jnp.sin(angle)], axis=1).astype(jnp.bfloat16)


def channelize(voltages, keep):
    window = window_table()
    table = transform_table()
    count = voltages.shape[0]
    samples = voltages.astype(jnp.float32).reshape(count, SPECTRA + TAPS - 1, FRAME)
    frames = window[0] * samples[:, 0:SPECTRA, :]
    for tap in range(1, TAPS):
        frames = frames + window[tap] * samples[:, tap : tap + SPECTRA, :]
    frames = frames.astype(jnp.bfloat16)
    spectra = jnp.einsum("itj,jrc->cirt", frames, table, preferred_element_type=jnp.float32)
    scale = 1.0 / (64.0 * math.sqrt(FRAME))
    return (spectra * (scale * keep)[None, :, None, None]).astype(jnp.bfloat16)


def update_gains(model_re, model_im, power, product_re, product_im):
    denominator = (model_re * model_re + model_im * model_im) * (power[:, None] + 1e-06)
    new_re = (model_re * product_re + model_im * product_im) / denominator
    new_im = (model_re * product_im - model_im * product_re) / denominator
    return (new_re, new_im)


def shards(voltages, flags, model_amp, model_phase):
    keep = (1 - flags).astype(jnp.float32)
    input_count = voltages.shape[0]
    spectra = channelize(voltages, keep)
    blk_count = lax.axis_size("blk")
    block_index = lax.axis_index("blk")
    grouped = lax.all_gather(spectra, "blk", axis=1, tiled=True)
    turned = lax.all_to_all(grouped, "chan", split_axis=0, concat_axis=1, tiled=True)
    local_chans = turned.shape[0]
    all_inputs = turned.shape[1]
    row_count = all_inputs // blk_count
    whole = turned.reshape(local_chans, all_inputs, 2 * SPECTRA)
    rows = lax.dynamic_slice_in_dim(whole, block_index * row_count, row_count, 1)
    rotated = jnp.concatenate([rows[:, :, SPECTRA:], -rows[:, :, :SPECTRA]], axis=2)
    stacked = jnp.stack([rows, rotated])
    correlation = (
        jnp.einsum("rcpk,cqk->rcpq", stacked, whole, preferred_element_type=jnp.float32) / SPECTRA
    )
    visibility = correlation.astype(jnp.bfloat16)
    high = lax.Precision.HIGHEST
    full_re = model_amp * jnp.cos(model_phase)
    full_im = model_amp * jnp.sin(model_phase)
    model_re = lax.dynamic_slice_in_dim(full_re, block_index * row_count, row_count, 1)
    model_im = lax.dynamic_slice_in_dim(full_im, block_index * row_count, row_count, 1)

    def sweep(gain_re, gain_im):
        probe_re = gain_re * model_re - gain_im * model_im
        probe_im = gain_re * model_im + gain_im * model_re
        probes = lax.all_gather(jnp.stack([probe_re, probe_im]), "blk", axis=2, tiled=True)
        power = jnp.sum(probes * probes, axis=(0, 2))
        products = jnp.einsum("rcpq,scq->rscp", correlation, probes, precision=high)
        product_re = products[0, 0] - products[1, 1]
        product_im = products[0, 1] + products[1, 0]
        return update_gains(model_re, model_im, power, product_re, product_im)

    def paired(step_index, carried):
        first_re, first_im = sweep(carried[0], carried[1])
        second_re, second_im = sweep(first_re, first_im)
        return (0.5 * (second_re + first_re), 0.5 * (second_im + first_im))

    start_re = jnp.ones((local_chans, row_count), jnp.float32)
    start_im = jnp.zeros((local_chans, row_count), jnp.float32)
    gain_re, gain_im = lax.fori_loop(0, ITERS // 2, paired, (start_re, start_im))
    solved = lax.all_gather(jnp.stack([gain_re, gain_im]), "blk", axis=2, tiled=True)
    owners = lax.all_to_all(solved, "chan", split_axis=2, concat_axis=1, tiled=True)
    gains = lax.dynamic_slice_in_dim(owners, block_index * input_count, input_count, 2)
    return (visibility, gains)


def solution(mesh):
    return jax.shard_map(
        shards,
        mesh=mesh,
        in_specs=(P(("chan", "blk"), None), P(("chan", "blk")), P("chan", None), P("chan", None)),
        out_specs=(P(None, "chan", "blk", None), P(None, None, ("chan", "blk"))),
        check_vma=False,
    )
```

profile of v0, /device:TPU:1, one launch (start us, length us, event | category | flops | bytes accessed | tf_op | source)
XLA Modules:
  0.0 805.5 jit_solution(235510974840824915)
XLA Ops:
  7.3 1.2 cosine_convert_fusion
  8.6 5.9 convert_element_type.41
  14.5 10.1 %reshape.358 = f32[16,263,512]{2,1,0:T(8,128)} reshape(f32[16,134656]{1,0:T(8,128)} %convert_element_type.41) | data formatting | bytes 17235968 | tf_op jit(solution)/shard_map/reshape | solution.py:36
  24.6 27.3 %fusion.34 = bf16[128,16,2,256]{3,0,1,2:T(8,128)(2,1)} fusion(f32[16]{0:T(128)S(1)} %convert_multiply_fusion, f32[16,263,512]{2,1,0:T(8,128)} %reshape.358, f32[512]{0:T(512)S(1)} %get-tuple-element.223, f32[512]{0:T(512)S(1)} %get-tuple-element.224, f32[512]{0:T(512)S(1)} %get-tuple-element.225, f32[512]{0:T(512)S(1)} %get-tuple-element.226, ...), kind=kOutput, calls=%fused_computation.70 | convolution fusion | flops 1109917696 | bytes 69484608 | tf_op jit(solution)/shard_map/itj,jrc->cirt/dot_general | solution.py:41
  52.0 66.1 %all-gather.2.cloned.1.call-done = bf16[128,64,2,256]{3,0,1,2:T(8,128)(2,1)} async-done(((bf16[128,16,2,256]{3,0,1,2:T(8,128)(2,1)}), bf16[128,64,2,256]{3,0,1,2:T(8,128)(2,1)}) %all-gather.2.cloned.1.call-update) | async-done | bytes 8388624 | tf_op jit(solution)/shard_map/all_gather | solution.py:59
  118.1 11.5 %copy.43 = bf16[128,64,2,256]{3,1,2,0:T(8,128)(2,1)} copy(bf16[128,64,2,256]{3,0,1,2:T(8,128)(2,1)} %all-gather.2.cloned.1.call-done) | data formatting | bytes 16777216 | tf_op jit(solution)/shard_map/all_gather | solution.py:59
  129.7 7.3 all-to-all-start
  137.0 0.8 multiply_add_fusion.2
  137.8 117.2 %all-to-all-done = bf16[128,64,2,256]{3,1,2,0:T(8,128)(2,1)} async-done(((bf16[128,64,2,256]{3,1,2,0:T(8,128)(2,1)}), bf16[128,64,2,256]{3,1,2,0:T(8,128)(2,1)}, u32[]{:S(2)}, u32[]{:S(2)}) %all-to-all-start) | async-done | bytes 8388640 | tf_op jit(solution)/shard_map/all_to_all | solution.py:60
  254.9 16.4 %copy.81 = bf16[32,4,64,2,256]{4,3,2,0,1:T(2,128)(2,1)} copy(bf16[32,4,64,2,256]{4,2,3,1,0:T(8,128)(2,1)} %bitcast.4) | data formatting | bytes 16777216 | tf_op jit(solution)/shard_map/all_to_all | solution.py:60
  271.4 14.1 %reshape.359 = bf16[4,2048,512]{2,1,0:T(8,128)(2,1)} reshape(bf16[4,32,64,2,256]{4,3,2,1,0:T(2,128)(2,1)} %bitcast.199) | data formatting | bytes 16777216 | tf_op jit(solution)/shard_map/reshape | solution.py:64
  285.4 14.1 %reshape.366 = bf16[4,2048,512,1]{2,1,0,3:T(8,128)(2,1)} reshape(bf16[4,32,64,2,256]{4,3,2,1,0:T(2,128)(2,1)} %bitcast.200) | data formatting | bytes 16777216 | tf_op jit(solution)/shard_map/reshape | solution.py:64
  299.5 1.8 constant_dynamic-slice_fusion
  301.3 3.3 maximum_bitcast_fusion
  304.6 22.1 %fusion.78 = (bf16[2,4,512,2048]{2,3,0,1:T(8,128)(2,1)}, f32[2,4,512,2048]{2,3,0,1:T(8,128)}) fusion(bf16[1,4,512,512]{3,2,0,1:T(8,128)(2,1)S(1)} %get-tuple-element.234, bf16[1,4,512,512]{3,2,0,1:T(8,128)(2,1)} %get-tuple-element.235, bf16[4,2048,512,1]{2,1,0,3:T(8,128)(2,1)} %reshape.366), kind=kOutput, calls=%fused_computation.137 | convolution fusion | flops 8615100416 | bytes 62914560 | tf_op jit(solution)/shard_map/rcpk,cqk->rcpq/dot_general | solution.py:69
  326.7 31.8 %copy.45 = f32[2,4,512,2048]{3,2,0,1:T(8,128)} copy(f32[2,4,512,2048]{2,3,0,1:T(8,128)} %get-tuple-element.233) | data formatting | bytes 67108864
  358.5 381.5 %while.16 = (s32[]{:T(128)}, f32[4,512]{1,0:T(4,128)S(1)}, f32[4,512]{1,0:T(4,128)S(1)}, f32[4,512]{1,0:T(4,128)S(1)}, f32[4,512]{1,0:T(4,128)S(1)}, /*index=5*/...) while((s32[]{:T(128)}, f32[4,512]{1,0:T(4,128)S(1)}, ...), condition=%wide.region_3.4_spmd.clone, body=%wide.region_0.3_spmd.clone.sunk | while | flops 402845696 | bytes 68075792 | solution.py:95
  358.6 8.9 %all_gather.24 = f32[2,4,2048]{2,0,1:T(2,128)S(1)} all-gather(f32[2,4,512]{2,0,1:T(2,128)S(1)} %pad_maximum_fusion.5), channel_id=1, replica_groups=mesh['chan'=32,'blk'=4] {'blk'}, dimensions={2}, use_global_device_ids=true | all-gather | bytes 81920 | tf_op jit(solution)/shard_map/while/body/eval_jaxpr/all_gather | solution.py:81
  367.5 30.8 %convolution_bitcast_fusion.2 = f32[2,2,4,512]{3,1,0,2:T(2,128)S(1)} fusion(f32[2,4,512,2048]{3,2,0,1:T(8,128)} %get-tuple-element.328, f32[2,4,2048]{2,0,1:T(2,128)S(1)} %all_gather.24), kind=kOutput, calls=%fused_computation.clone.1 | convolution fusion | flops 201326592 | bytes 33652736 | tf_op jit(solution)/shard_map/while/body/eval_jaxpr/rcpq,scq->rscp/dot_general | solution.py:83
  398.6 6.8 all_gather.25
  405.4 30.8 %fusion.97 = f32[4,2,2,512]{3,1,2,0:T(2,128)S(1)} fusion(f32[2,4,512,2048]{3,2,0,1:T(8,128)} %get-tuple-element.328, f32[2,4,2048,1]{2,1,0,3:T(4,128)S(1)} %bitcast.201), kind=kOutput, calls=%fused_computation.2.clone.1 | convolution fusion | flops 201326592 | bytes 33652736 | tf_op jit(solution)/shard_map/while/body/eval_jaxpr/rcpq,scq->rscp/dot_general | solution.py:83
  436.6 6.8 all_gather.24
  443.3 30.8 %convolution_bitcast_fusion.2 = f32[2,2,4,512]{3,1,0,2:T(2,128)S(1)} fusion(f32[2,4,512,2048]{3,2,0,1:T(8,128)} %get-tuple-element.328, f32[2,4,2048]{2,0,1:T(2,128)S(1)} %all_gather.24), kind=kOutput, calls=%fused_computation.clone.1 | convolution fusion | flops 201326592 | bytes 33652736 | tf_op jit(solution)/shard_map/while/body/eval_jaxpr/rcpq,scq->rscp/dot_general | solution.py:83
  474.5 6.8 all_gather.25
  481.2 30.8 %fusion.97 = f32[4,2,2,512]{3,1,2,0:T(2,128)S(1)} fusion(f32[2,4,512,2048]{3,2,0,1:T(8,128)} %get-tuple-element.328, f32[2,4,2048,1]{2,1,0,3:T(4,128)S(1)} %bitcast.201), kind=kOutput, calls=%fused_computation.2.clone.1 | convolution fusion | flops 201326592 | bytes 33652736 | tf_op jit(solution)/shard_map/while/body/eval_jaxpr/rcpq,scq->rscp/dot_general | solution.py:83
  512.1 0.1 multiply_reduce_fusion.5
  512.4 6.8 all_gather.24
  519.2 30.8 %convolution_bitcast_fusion.2 = f32[2,2,4,512]{3,1,0,2:T(2,128)S(1)} fusion(f32[2,4,512,2048]{3,2,0,1:T(8,128)} %get-tuple-element.328, f32[2,4,2048]{2,0,1:T(2,128)S(1)} %all_gather.24), kind=kOutput, calls=%fused_computation.clone.1 | convolution fusion | flops 201326592 | bytes 33652736 | tf_op jit(solution)/shard_map/while/body/eval_jaxpr/rcpq,scq->rscp/dot_general | solution.py:83
  550.3 6.8 all_gather.25
  557.0 30.8 %fusion.97 = f32[4,2,2,512]{3,1,2,0:T(2,128)S(1)} fusion(f32[2,4,512,2048]{3,2,0,1:T(8,128)} %get-tuple-element.328, f32[2,4,2048,1]{2,1,0,3:T(4,128)S(1)} %bitcast.201), kind=kOutput, calls=%fused_computation.2.clone.1 | convolution fusion | flops 201326592 | bytes 33652736 | tf_op jit(solution)/shard_map/while/body/eval_jaxpr/rcpq,scq->rscp/dot_general | solution.py:83
  588.2 6.8 all_gather.24
  595.0 30.8 %convolution_bitcast_fusion.2 = f32[2,2,4,512]{3,1,0,2:T(2,128)S(1)} fusion(f32[2,4,512,2048]{3,2,0,1:T(8,128)} %get-tuple-element.328, f32[2,4,2048]{2,0,1:T(2,128)S(1)} %all_gather.24), kind=kOutput, calls=%fused_computation.clone.1 | convolution fusion | flops 201326592 | bytes 33652736 | tf_op jit(solution)/shard_map/while/body/eval_jaxpr/rcpq,scq->rscp/dot_general | solution.py:83
  626.1 6.8 all_gather.25
  632.9 30.8 %fusion.97 = f32[4,2,2,512]{3,1,2,0:T(2,128)S(1)} fusion(f32[2,4,512,2048]{3,2,0,1:T(8,128)} %get-tuple-element.328, f32[2,4,2048,1]{2,1,0,3:T(4,128)S(1)} %bitcast.201), kind=kOutput, calls=%fused_computation.2.clone.1 | convolution fusion | flops 201326592 | bytes 33652736 | tf_op jit(solution)/shard_map/while/body/eval_jaxpr/rcpq,scq->rscp/dot_general | solution.py:83
  664.1 6.8 all_gather.24
  670.8 30.8 %convolution_bitcast_fusion.2 = f32[2,2,4,512]{3,1,0,2:T(2,128)S(1)} fusion(f32[2,4,512,2048]{3,2,0,1:T(8,128)} %get-tuple-element.328, f32[2,4,2048]{2,0,1:T(2,128)S(1)} %all_gather.24), kind=kOutput, calls=%fused_computation.clone.1 | convolution fusion | flops 201326592 | bytes 33652736 | tf_op jit(solution)/shard_map/while/body/eval_jaxpr/rcpq,scq->rscp/dot_general | solution.py:83
  701.9 6.8 all_gather.25
  708.7 30.8 %fusion.97 = f32[4,2,2,512]{3,1,2,0:T(2,128)S(1)} fusion(f32[2,4,512,2048]{3,2,0,1:T(8,128)} %get-tuple-element.328, f32[2,4,2048,1]{2,1,0,3:T(4,128)S(1)} %bitcast.201), kind=kOutput, calls=%fused_computation.2.clone.1 | convolution fusion | flops 201326592 | bytes 33652736 | tf_op jit(solution)/shard_map/while/body/eval_jaxpr/rcpq,scq->rscp/dot_general | solution.py:83
  740.0 6.8 all_gather.19
  746.8 1.1 copy.46
  747.9 3.8 reshape.368
  751.7 18.3 %all-to-all-start.1 = ((f32[32,1,512]{2,1,0:T(1,128)}), f32[32,1,512]{2,1,0:T(1,128)S(1)}, u32[]{:S(2)}, u32[]{:S(2)}) async-start(f32[32,1,512]{2,1,0:T(1,128)} %reshape.368), calls=%async_computation.1 | async-start | bytes 131072 | tf_op jit(solution)/shard_map/all_to_all | solution.py:97
  770.0 21.5 %copy.48 = bf16[2,4,512,2048]{3,2,1,0:T(8,128)(2,1)} copy(bf16[2,4,512,2048]{2,3,0,1:T(8,128)(2,1)} %get-tuple-element.232) | data formatting | bytes 33554432
  791.5 0.5 broadcast.226
  792.0 0.8 reduce
  792.8 3.2 reshape.369
  796.1 1.9 copy.47
  798.0 0.7 copy.49
  (82 shorter events, 3.4 us)
Async XLA Ops:
  7.2 111.0 %all-gather.2.cloned.1.call-start = ((), (), s32[]{:S(2)}) async-start(), calls=%async_computation.2 | async-start | bytes 10485760 | tf_op jit(solution)/shard_map/all_gather | solution.py:59
  14.5 10.2 %copy-start = (s32[16]{0:T(128)S(1)}, s32[16]{0:T(128)}, u32[]{:S(2)}) copy-start(s32[16]{0:T(128)} %param.7) | copy-start | bytes 196
  129.7 125.3 %all-to-all-start = ((bf16[128,64,2,256]{3,1,2,0:T(8,128)(2,1)}), bf16[128,64,2,256]{3,1,2,0:T(8,128)(2,1)}, u32[]{:S(2)}, u32[]{:S(2)}) async-start(bf16[128,64,2,256]{3,1,2,0:T(8,128)(2,1)} %copy.43), calls=%async_computation | async-start | bytes 16777216 | tf_op jit(solution)/shard_map/all_to_all | solution.py:60
  751.7 39.8 %all-to-all-start.1 = ((f32[32,1,512]{2,1,0:T(1,128)}), f32[32,1,512]{2,1,0:T(1,128)S(1)}, u32[]{:S(2)}, u32[]{:S(2)}) async-start(f32[32,1,512]{2,1,0:T(1,128)} %reshape.368), calls=%async_computation.1 | async-start | bytes 131072 | tf_op jit(solution)/shard_map/all_to_all | solution.py:97
Sparse Core Ops, SparseCore 0:
  52.1 65.9 all-gather.1
where the time goes:
time: 808 us; the launch traced here: 806 us
  matrix products  357 us (44%)
  waiting for transfers between devices  183 us (23%)
  local copies, waits for them, and re-layouts  131 us (16%)
  blocking collectives  76.4 us (9%)
  starting transfers between devices  25.6 us (3%)
  other arithmetic  17 us (2%)
  between operations  14.2 us (2%)
    dot_general x10, matrix products, sweep(): products = jnp.einsum('rcpq,scq->rscp', correlation, probes, precision=high)  308 us
    all_to_all x1, waiting for transfers between devices, shards(): lax.all_to_all(grouped, 'chan', split_axis=0, concat_axis=1, tiled=True)  117 us
    all_gather x10, blocking collectives, sweep(): lax.all_gather(jnp.stack([probe_re, probe_im]), 'blk', axis=2, tiled=True)  69.7 us
    all_gather x1, waiting for transfers between devices, shards(): grouped = lax.all_gather(spectra, 'blk', axis=1, tiled=True)  66.1 us
    unnamed x7, local copies, waits for them, and re-layouts  61 us
    reshape x2, local copies, waits for them, and re-layouts, shards(): whole = turned.reshape(local_chans, all_inputs, 2 * SPECTRA)  28.1 us
    dot_general x1, matrix products, channelize(): jnp.einsum('itj,jrc->cirt', frames, table, preferred_element_type=jnp.flo...  27.3 us
    dot_general x1, matrix products, shards(): jnp.einsum('rcpk,cqk->rcpq', stacked, whole, preferred_element_type=jnp.f...  22.1 us
  transfers between devices with their start and end apart: 3, of which 2 were waited for; matrix products, arithmetic and copies ran while one was open for 3% of the time, Pallas kernels for 0%

commit v1 on v0

v1 whole, which is shorter than its diff:
```python
import math

import jax
import jax.numpy as jnp
from jax import lax
from jax.sharding import PartitionSpec as P

CHANS = 128
FRAME = 512
TAPS = 8
BAND_START = 64
SPECTRA = 256
ITERS = 10


def window_table():
    index = jnp.arange(TAPS * FRAME, dtype=jnp.float32)
    offset = (index - TAPS * FRAME / 2 + 0.5) / FRAME
    taper = 0.5 - 0.5 * jnp.cos(2.0 * math.pi * (index + 0.5) / (TAPS * FRAME))
    return (jnp.sinc(offset) * taper).reshape(TAPS, FRAME)


def transform_table():
    sample = jnp.arange(FRAME, dtype=jnp.int32)
    channel = BAND_START + jnp.arange(CHANS, dtype=jnp.int32)
    angle = (sample[:, None] * channel[None, :] % FRAME).astype(jnp.float32) * (
        2.0 * math.pi / FRAME
    )
    return jnp.stack([jnp.cos(angle), -jnp.sin(angle)], axis=1).astype(jnp.bfloat16)


def channelize(voltages, keep):
    window = window_table()
    table = transform_table()
    count = voltages.shape[0]
    samples = voltages.astype(jnp.float32).reshape(count, SPECTRA + TAPS - 1, FRAME)
    frames = window[0] * samples[:, 0:SPECTRA, :]
    for tap in range(1, TAPS):
        frames = frames + window[tap] * samples[:, tap : tap + SPECTRA, :]
    frames = frames.astype(jnp.bfloat16)
    spectra = jnp.einsum("itj,jrc->cirt", frames, table, preferred_element_type=jnp.float32)
    scale = 1.0 / (64.0 * math.sqrt(FRAME))
    return (spectra * (scale * keep)[None, :, None, None]).astype(jnp.bfloat16)


def split3(value):
    high = value.astype(jnp.bfloat16)
    rest = value - high.astype(jnp.float32)
    mid = rest.astype(jnp.bfloat16)
    low = (rest - mid.astype(jnp.float32)).astype(jnp.bfloat16)
    return jnp.concatenate([high, mid, low], axis=-1)


def exact_dot(lhs, rhs_f32, dims):
    cols = rhs_f32.shape[-1]
    parts = lax.dot_general(
        lhs, split3(rhs_f32), (dims, ((), ())), preferred_element_type=jnp.float32
    )
    return parts[:, :cols] + parts[:, cols : 2 * cols] + parts[:, 2 * cols :]


def solve_gains(data, model_re, model_im):
    count = data.shape[0]

    def sweep(gain_re, gain_im):
        probe_re = gain_re * model_re - gain_im * model_im
        probe_im = gain_re * model_im + gain_im * model_re
        power = jnp.sum(probe_re * probe_re + probe_im * probe_im)
        half = exact_dot(data, jnp.stack([probe_re, probe_im], axis=1), ((0,), (0,)))
        u_re = half[:SPECTRA, 0] + half[SPECTRA:, 1]
        u_im = half[:SPECTRA, 1] - half[SPECTRA:, 0]
        mix = jnp.concatenate(
            [jnp.stack([u_re, u_im], axis=1), jnp.stack([-u_im, u_re], axis=1)], axis=0
        )
        product = exact_dot(data, mix, ((1,), (0,))) * (1.0 / SPECTRA)
        product_re = product[:, 0]
        product_im = product[:, 1]
        denominator = (model_re * model_re + model_im * model_im) * (power + 1e-06)
        new_re = (model_re * product_re + model_im * product_im) / denominator
        new_im = (model_re * product_im - model_im * product_re) / denominator
        return new_re, new_im

    def paired(step_index, carried):
        first_re, first_im = sweep(carried[0], carried[1])
        second_re, second_im = sweep(first_re, first_im)
        return (0.5 * (second_re + first_re), 0.5 * (second_im + first_im))

    start_re = jnp.ones((count,), jnp.float32)
    start_im = jnp.zeros((count,), jnp.float32)
    return lax.fori_loop(0, ITERS // 2, paired, (start_re, start_im))


def shards(voltages, flags, model_amp, model_phase):
    keep = (1 - flags).astype(jnp.float32)
    input_count = voltages.shape[0]
    spectra = channelize(voltages, keep)
    blk_count = lax.axis_size("blk")
    chan_count = lax.axis_size("chan")
    block_index = lax.axis_index("blk")
    turned = lax.all_to_all(spectra, "chan", split_axis=0, concat_axis=1, tiled=True)
    local_chans = turned.shape[0]
    grouped = lax.all_gather(turned, "blk", axis=1, tiled=False)
    grouped = grouped.reshape(local_chans, blk_count, chan_count, input_count, 2 * SPECTRA)
    whole = jnp.swapaxes(grouped, 1, 2).reshape(local_chans, -1, 2 * SPECTRA)
    all_inputs = whole.shape[1]
    row_count = all_inputs // blk_count
    rows = lax.dynamic_slice_in_dim(whole, block_index * row_count, row_count, 1)
    rotated = jnp.concatenate([rows[:, :, SPECTRA:], -rows[:, :, :SPECTRA]], axis=2)
    stacked = jnp.stack([rows, rotated])
    correlation = (
        jnp.einsum("rcpk,cqk->rcpq", stacked, whole, preferred_element_type=jnp.float32) / SPECTRA
    )
    visibility = correlation.astype(jnp.bfloat16)

    solve_chans = local_chans // blk_count
    data = lax.dynamic_slice_in_dim(whole, block_index * solve_chans, solve_chans, 0)
    amp = lax.dynamic_slice_in_dim(model_amp, block_index * solve_chans, solve_chans, 0)
    phase = lax.dynamic_slice_in_dim(model_phase, block_index * solve_chans, solve_chans, 0)
    full_re = amp * jnp.cos(phase)
    full_im = amp * jnp.sin(phase)
    solved = jax.vmap(solve_gains)(data, full_re, full_im)
    solved = jnp.stack(solved)
    owners = solved.reshape(2, solve_chans, chan_count * blk_count, input_count)
    owners = jnp.swapaxes(owners, 1, 2)
    gains = lax.all_to_all(owners, ("chan", "blk"), split_axis=1, concat_axis=1, tiled=True)
    gains = gains.reshape(2, -1, input_count)
    return (visibility, gains)


def solution(mesh):
    return jax.shard_map(
        shards,
        mesh=mesh,
        in_specs=(P(("chan", "blk"), None), P(("chan", "blk")), P("chan", None), P("chan", None)),
        out_specs=(P(None, "chan", "blk", None), P(None, None, ("chan", "blk"))),
        check_vma=False,
    )
```

time: 808 us -> 280 us (0.35)
  matrix products: 357 us -> 51.3 us
  waiting for transfers between devices: 183 us -> 62.2 us
  local copies, waits for them, and re-layouts: 131 us -> 76.8 us
  blocking collectives: 76.4 us -> 35.5 us
  starting transfers between devices: 25.6 us -> 7.31 us
    dot_general x10 -> x20, matrix products: 308 us -> 10.1 us  [exact_dot(): lax.dot_general(lhs, split3(rhs_f32), (dims, ((), ())), preferred_element...]
    all_to_all x2 -> x1, waiting for transfers between devices: 117 us -> 0.01 us  [shards(): lax.all_to_all(owners, ('chan', 'blk'), split_axis=1, concat_axis=1, tile...]
    all_gather x11 -> x0, blocking collectives: 76.4 us -> none  [the longest x10 69.7 us: sweep(): lax.all_gather(jnp.stack([probe_re, probe_im]), 'blk', axis=2, tiled=True)]
    unnamed x7 -> x2, local copies, waits for them, and re-layouts: 61 us -> 22.2 us
    all_to_all x0 -> x1, blocking collectives: none -> 35.5 us  [shards(): lax.all_to_all(spectra, 'chan', split_axis=0, concat_axis=1, tiled=True)]
    all_to_all x2 -> x1, starting transfers between devices: 25.6 us -> 7.27 us  [shards(): lax.all_to_all(owners, ('chan', 'blk'), split_axis=1, concat_axis=1, tile...]
    all_to_all x3 -> x1, local copies, waits for them, and re-layouts: 18.8 us -> 1.52 us  [shards(): lax.all_to_all(spectra, 'chan', split_axis=0, concat_axis=1, tiled=True)]
    reshape x2 -> x1, local copies, waits for them, and re-layouts: 28.1 us -> 14.1 us  [shards(): grouped.reshape(local_chans, blk_count, chan_count, input_count, 2 * SPEC...]
  transfers between devices with their start and end apart: 3 -> 2, of which waited for: 2 -> 1; matrix products, arithmetic and copies ran while one was open for 3% -> 15% of each run, Pallas kernels for 0% -> 0%
where the time goes in v1:
time: 280 us; the launch traced here: 279 us
  local copies, waits for them, and re-layouts  76.8 us (27%)
  waiting for transfers between devices  62.2 us (22%)
  matrix products  51.3 us (18%)
  blocking collectives  35.5 us (13%)
  other arithmetic  24.3 us (9%)
  between operations  14.1 us (5%)
  starting transfers between devices  7.31 us (3%)
  loops' own time  6.97 us (2%)
    all_gather x1, waiting for transfers between devices, shards(): grouped = lax.all_gather(turned, 'blk', axis=1, tiled=False)  62.1 us
    all_to_all x1, blocking collectives, shards(): lax.all_to_all(spectra, 'chan', split_axis=0, concat_axis=1, tiled=True)  35.5 us
    dot_general x1, matrix products, channelize(): jnp.einsum('itj,jrc->cirt', frames, table, preferred_element_type=jnp.flo...  26 us
    unnamed x2, local copies, waits for them, and re-layouts  22.2 us
    all_gather x1, local copies, waits for them, and re-layouts, shards(): grouped = lax.all_gather(turned, 'blk', axis=1, tiled=False)  16.3 us
    dot_general x1, matrix products, shards(): jnp.einsum('rcpk,cqk->rcpq', stacked, whole, preferred_element_type=jnp.f...  15.2 us
    reshape x1, local copies, waits for them, and re-layouts, shards(): grouped.reshape(local_chans, blk_count, chan_count, input_count, 2 * SPEC...  14.1 us
    reshape x1, local copies, waits for them, and re-layouts, channelize(): voltages.astype(jnp.float32).reshape(count, SPECTRA + TAPS - 1, FRAME)  10.1 us
  transfers between devices with their start and end apart: 2, of which 1 were waited for; matrix products, arithmetic and copies ran while one was open for 15% of the time, Pallas kernels for 0%

profile of v1, /device:TPU:1, one launch (start us, length us, event | category | flops | bytes accessed | tf_op | source)
XLA Modules:
  0.0 278.5 jit_solution(3910800663929175641)
XLA Ops:
  7.3 0.7 convert_multiply_fusion
  8.0 1.2 cosine_convert_fusion
  9.2 5.9 %convert_element_type.436 = f32[16,134656]{1,0:T(8,128)} convert(s32[16,134656]{1,0:T(8,128)} %param.6) | non-fusion elementwise | flops 2154496 | bytes 17235968 | tf_op jit(solution)/shard_map/convert_element_type | solution.py:36
  15.1 10.1 %reshape.1164 = f32[16,263,512]{2,1,0:T(8,128)} reshape(f32[16,134656]{1,0:T(8,128)} %convert_element_type.436) | data formatting | bytes 17235968 | tf_op jit(solution)/shard_map/reshape | solution.py:36
  25.2 26.0 %fusion.65 = bf16[128,16,2,256]{3,0,1,2:T(8,128)(2,1)S(1)} fusion(f32[16]{0:T(128)S(1)} %convert_multiply_fusion, f32[16,263,512]{2,1,0:T(8,128)} %reshape.1164, f32[512]{0:T(512)S(1)} %get-tuple-element.225, f32[512]{0:T(512)S(1)} %get-tuple-element.226, f32[512]{0:T(512)S(1)} %get-tuple-element.227, f32[512]{0:T(512)S(1)} %get-tuple-element.228, ...), kind=kOutput, calls=%fused_computation.122 | convolution fusion | flops 1109917696 | bytes 69484608 | tf_op jit(solution)/shard_map/itj,jrc->cirt/dot_general | solution.py:41
  51.3 1.2 copy.29
  52.5 35.5 %all_to_all.20 = bf16[128,16,2,256]{3,1,2,0:T(8,128)(2,1)S(1)} all-to-all(bf16[128,16,2,256]{3,1,2,0:T(8,128)(2,1)S(1)} %copy.29), channel_id=1, replica_groups=mesh['chan'=32,'blk'=4] {'chan'}, dimensions={0} | all-to-all | bytes 4194304 | tf_op jit(solution)/shard_map/all_to_all | solution.py:100
  87.9 1.5 copy.30
  89.5 1.0 multiply_add_fusion.2
  90.5 62.1 %all-gather.2.cloned.1.call-done = bf16[4,4,512,2,256]{4,2,3,0,1:T(8,128)(2,1)} async-done(((bf16[4,1,512,2,256]{4,2,3,0,1:T(8,128)(2,1)}), bf16[4,4,512,2,256]{4,2,3,0,1:T(8,128)(2,1)}) %all-gather.2.cloned.1.call-update) | async-done | bytes 8388624 | tf_op jit(solution)/shard_map/all_gather | solution.py:102
  152.7 16.3 %copy.31 = bf16[4,4,512,2,256]{4,3,2,1,0:T(2,128)(2,1)} copy(bf16[4,4,512,2,256]{4,2,3,0,1:T(8,128)(2,1)} %all-gather.2.cloned.1.call-done) | data formatting | bytes 16777216 | tf_op jit(solution)/shard_map/all_gather | solution.py:102
  169.0 14.1 %reshape.1165 = bf16[4,4,32,16,512]{4,3,2,1,0:T(8,128)(2,1)} reshape(bf16[4,4,512,2,256]{4,3,2,1,0:T(2,128)(2,1)} %copy.31) | data formatting | bytes 16777216 | tf_op jit(solution)/shard_map/reshape | solution.py:103
  183.1 8.2 %copy.32 = bf16[4,32,4,16,512]{4,3,2,1,0:T(8,128)(2,1)} copy(bf16[4,32,4,16,512]{4,3,1,2,0:T(8,128)(2,1)} %bitcast.178) | data formatting | bytes 16777216 | tf_op jit(solution)/shard_map/transpose | solution.py:104
  191.3 1.7 constant_dynamic-slice_fusion.1
  193.0 25.9 %while.16 = (s32[]{:T(128)}, f32[1,2048]{1,0:T(1,128)S(1)}, f32[1,2048]{1,0:T(1,128)S(1)}, f32[1,2048]{1,0:T(1,128)S(1)}, f32[1,2048]{1,0:T(1,128)S(1)}, /*index...) while((s32[]{:T(128)}, f32[1,2048]{1,0:T(1,128)S(1)}, ...), condition=%wide.region_3.4_spmd.clone, body=%wide.region_0.3_spmd.clone.sunk | while | flops 50787840 | bytes 9187491 | solution.py:90
  193.0 0.7 add_reduce_fusion.4
  194.4 0.4 fusion.143
  194.9 0.6 convolution_bitcast_fusion.4
  195.5 0.7 add_reduce_fusion.5
  197.0 0.4 fusion.152
  197.5 0.6 convolution_bitcast_fusion.5
  198.2 0.7 add_reduce_fusion.4
  199.6 0.4 fusion.143
  200.1 0.6 convolution_bitcast_fusion.4
  200.7 0.7 add_reduce_fusion.5
  202.7 0.6 convolution_bitcast_fusion.5
  203.4 0.7 add_reduce_fusion.4
  205.2 0.6 convolution_bitcast_fusion.4
  205.9 0.7 add_reduce_fusion.5
  207.9 0.6 convolution_bitcast_fusion.5
  208.6 0.7 add_reduce_fusion.4
  210.4 0.6 convolution_bitcast_fusion.4
  211.1 0.7 add_reduce_fusion.5
  213.0 0.6 convolution_bitcast_fusion.5
  213.8 0.7 add_reduce_fusion.4
  215.6 0.6 convolution_bitcast_fusion.4
  216.3 0.7 add_reduce_fusion.5
  218.2 0.6 convolution_bitcast_fusion.5
  219.0 0.5 broadcast.286
  219.5 0.7 reduce.14
  220.2 0.7 reduce.15
  221.0 0.8 copy.33
  221.8 7.3 %all-to-all-start.1 = ((f32[2,128,1,16]{3,2,0,1:T(1,128)}), f32[2,128,1,16]{3,2,0,1:T(1,128)S(1)}, u32[]{:S(2)}, u32[]{:S(2)}) async-start(f32[2,128,1,16]{3,2,0,1:T(1,128)} %copy.33), calls=%async_computation.1 | async-start | bytes 262144 | tf_op jit(solution)/shard_map/all_to_all | solution.py:125
  229.1 1.8 constant_dynamic-slice_fusion
  230.9 3.3 %maximum_bitcast_fusion.8 = (bf16[1,4,512,512]{3,2,0,1:T(8,128)(2,1)S(1)}, bf16[1,4,512,512]{3,2,0,1:T(8,128)(2,1)}) fusion(bf16[4,512,256]{2,1,0:T(8,128)(2,1)S(1)} %get-tuple-element.223, bf16[4,512,256]{2,1,0:T(8,128)(2,1)S(1)} %get-tuple-element.222, bf16[4,2048,512]{2,1,0:T(8,128)(2,1)} %bitcast.181, s32[]{:T(128)S(6)} %select_n.126), kind=kLoop, calls=%fused_computation.123 | loop fusion | flops 4194304 | bytes 8388612 | tf_op jit(solution)/shard_map/stack | solution.py:109
  234.3 15.2 %fusion.50 = bf16[2,4,512,2048]{2,3,0,1:T(8,128)(2,1)} fusion(bf16[4,2048,512,1]{2,1,3,0:T(8,128)(2,1)} %bitcast.182, bf16[1,4,512,512]{3,2,0,1:T(8,128)(2,1)S(1)} %get-tuple-element.234, bf16[1,4,512,512]{3,2,0,1:T(8,128)(2,1)} %get-tuple-element.235), kind=kOutput, calls=%fused_computation.99 | convolution fusion | flops 8615100416 | bytes 29360128 | tf_op jit(solution)/shard_map/rcpk,cqk->rcpq/dot_general | solution.py:111
  249.5 21.5 %copy.34 = bf16[2,4,512,2048]{3,2,1,0:T(8,128)(2,1)} copy(bf16[2,4,512,2048]{2,3,0,1:T(8,128)(2,1)} %fusion.50) | data formatting | bytes 33554432
  271.0 0.7 copy.35
  (103 shorter events, 4.7 us)
Async XLA Ops:
  7.2 145.5 %all-gather.2.cloned.1.call-start = ((), (), s32[]{:S(2)}) async-start(), calls=%async_computation.2 | async-start | bytes 10485760 | tf_op jit(solution)/shard_map/all_gather | solution.py:102
  221.8 49.2 %all-to-all-start.1 = ((f32[2,128,1,16]{3,2,0,1:T(1,128)}), f32[2,128,1,16]{3,2,0,1:T(1,128)S(1)}, u32[]{:S(2)}, u32[]{:S(2)}) async-start(f32[2,128,1,16]{3,2,0,1:T(1,128)} %copy.33), calls=%async_computation.1 | async-start | bytes 262144 | tf_op jit(solution)/shard_map/all_to_all | solution.py:125
Sparse Core Ops, SparseCore 0:
  89.6 63.0 all-gather.1

commit v2 on v1

--- a/solution.py
+++ b/solution.py
@@ -3,6 +3,8 @@
 import jax
 import jax.numpy as jnp
 from jax import lax
+from jax.experimental import pallas as pl
+from jax.experimental.pallas import tpu as pltpu
 from jax.sharding import PartitionSpec as P
 
 CHANS = 128
@@ -90,6 +92,47 @@
     return lax.fori_loop(0, ITERS // 2, paired, (start_re, start_im))
 
 
+def correlate_kernel(block_ref, rows_ref, cols_ref, out_ref):
+    dims = (((1,), (1,)), ((), ()))
+    rows_re = rows_ref[0, :, :SPECTRA]
+    rows_im = rows_ref[0, :, SPECTRA:]
+    cols_re = cols_ref[0, :, :SPECTRA]
+    cols_im = cols_ref[0, :, SPECTRA:]
+
+    def dot(a, b):
+        return lax.dot_general(a, b, dims, preferred_element_type=jnp.float32)
+
+    real = dot(rows_re, cols_re) + dot(rows_im, cols_im)
+    imag = dot(rows_im, cols_re) - dot(rows_re, cols_im)
+    out_ref[0, 0] = (real * (1.0 / SPECTRA)).astype(out_ref.dtype)
+    out_ref[1, 0] = (imag * (1.0 / SPECTRA)).astype(out_ref.dtype)
+
+
+def correlate(whole, block_index, row_count, col_block=512):
+    chans, inputs, width = whole.shape
+    grid = (chans, inputs // col_block)
+    spec = pltpu.PrefetchScalarGridSpec(
+        num_scalar_prefetch=1,
+        grid=grid,
+        in_specs=[
+            pl.BlockSpec((1, row_count, width), lambda c, j, blk: (c, blk[0], 0)),
+            pl.BlockSpec((1, col_block, width), lambda c, j, blk: (c, j, 0)),
+        ],
+        out_specs=pl.BlockSpec((2, 1, row_count, col_block), lambda c, j, blk: (0, c, 0, j)),
+    )
+    flops = 8 * chans * row_count * inputs * (width // 2)
+    return pl.pallas_call(
+        correlate_kernel,
+        grid_spec=spec,
+        out_shape=jax.ShapeDtypeStruct((2, chans, row_count, inputs), jnp.bfloat16),
+        cost_estimate=pl.CostEstimate(
+            flops=flops,
+            transcendentals=0,
+            bytes_accessed=2 * chans * (inputs * width + row_count * width + 2 * row_count * inputs),
+        ),
+    )(jnp.reshape(block_index, (1,)).astype(jnp.int32), whole, whole)
+
+
 def shards(voltages, flags, model_amp, model_phase):
     keep = (1 - flags).astype(jnp.float32)
     input_count = voltages.shape[0]
@@ -97,6 +140,7 @@
     blk_count = lax.axis_size("blk")
     chan_count = lax.axis_size("chan")
     block_index = lax.axis_index("blk")
+    spectra = spectra.reshape(spectra.shape[0], input_count, 2 * SPECTRA)
     turned = lax.all_to_all(spectra, "chan", split_axis=0, concat_axis=1, tiled=True)
     local_chans = turned.shape[0]
     grouped = lax.all_gather(turned, "blk", axis=1, tiled=False)
@@ -104,13 +148,7 @@
     whole = jnp.swapaxes(grouped, 1, 2).reshape(local_chans, -1, 2 * SPECTRA)
     all_inputs = whole.shape[1]
     row_count = all_inputs // blk_count
-    rows = lax.dynamic_slice_in_dim(whole, block_index * row_count, row_count, 1)
-    rotated = jnp.concatenate([rows[:, :, SPECTRA:], -rows[:, :, :SPECTRA]], axis=2)
-    stacked = jnp.stack([rows, rotated])
-    correlation = (
-        jnp.einsum("rcpk,cqk->rcpq", stacked, whole, preferred_element_type=jnp.float32) / SPECTRA
-    )
-    visibility = correlation.astype(jnp.bfloat16)
+    visibility = correlate(whole, block_index, row_count)
 
     solve_chans = local_chans // blk_count
     data = lax.dynamic_slice_in_dim(whole, block_index * solve_chans, solve_chans, 0)

time: 280 us -> 232 us (0.83)
  local copies, waits for them, and re-layouts: 76.8 us -> 29.5 us
  Pallas kernels: 0 us -> 19.5 us
  matrix products: 51.3 us -> 37.4 us
  other arithmetic: 24.3 us -> 18.5 us
    unnamed x2 -> x1, local copies, waits for them, and re-layouts: 22.2 us -> 0.68 us
    pallas_call x0 -> x1, Pallas kernels: none -> 19.5 us  [correlate(): pl.pallas_call(correlate_kernel, grid_spec=spec, out_shape=jax.ShapeDtype...]
    all_gather x1 -> x0, local copies, waits for them, and re-layouts: 16.3 us -> none  [shards(): grouped = lax.all_gather(turned, 'blk', axis=1, tiled=False)]
    dot_general x1 -> x0, matrix products: 15.2 us -> none  [shards(): jnp.einsum('rcpk,cqk->rcpq', stacked, whole, preferred_element_type=jnp.f...]
    reshape x1, local copies, waits for them, and re-layouts: 14.1 us -> 2.9 us  [shards(): spectra = spectra.reshape(spectra.shape[0], input_count, 2 * SPECTRA)]
    another operation x2 -> x1, other arithmetic: 4.56 us -> 1.23 us  [the longest x1 3.34 us: shards(): stacked = jnp.stack([rows, rotated])]
  transfers between devices with their start and end apart: 2 -> 2, of which waited for: 1 -> 1; matrix products, arithmetic and copies ran while one was open for 15% -> 0% of each run, Pallas kernels for 0% -> 8%
where the time goes in v2:
time: 232 us; the launch traced here: 231 us
  waiting for transfers between devices  62.2 us (27%)
  matrix products  37.4 us (16%)
  blocking collectives  35.7 us (15%)
  local copies, waits for them, and re-layouts  29.5 us (13%)
  Pallas kernels  19.5 us (8%)
  other arithmetic  18.5 us (8%)
  between operations  14.1 us (6%)
  starting transfers between devices  7.3 us (3%)
  loops' own time  7.22 us (3%)
    all_gather x1, waiting for transfers between devices, shards(): grouped = lax.all_gather(turned, 'blk', axis=1, tiled=False)  62.1 us
    all_to_all x1, blocking collectives, shards(): lax.all_to_all(spectra, 'chan', split_axis=0, concat_axis=1, tiled=True)  35.7 us
    dot_general x1, matrix products, channelize(): jnp.einsum('itj,jrc->cirt', frames, table, preferred_element_type=jnp.flo...  27.3 us
    pallas_call x1, Pallas kernels, correlate(): pl.pallas_call(correlate_kernel, grid_spec=spec, out_shape=jax.ShapeDtype...  19.5 us
    reshape x1, local copies, waits for them, and re-layouts, channelize(): voltages.astype(jnp.float32).reshape(count, SPECTRA + TAPS - 1, FRAME)  10.1 us
    dot_general x20, matrix products, exact_dot(): lax.dot_general(lhs, split3(rhs_f32), (dims, ((), ())), preferred_element...  10.1 us
    transpose x1, local copies, waits for them, and re-layouts, shards(): whole = jnp.swapaxes(grouped, 1, 2).reshape(local_chans, -1, 2 * SPECTRA)  8.07 us
    all_to_all x1, starting transfers between devices, shards(): lax.all_to_all(owners, ('chan', 'blk'), split_axis=1, concat_axis=1, tile...  7.26 us
  transfers between devices with their start and end apart: 2, of which 1 were waited for; matrix products, arithmetic and copies ran while one was open for 0% of the time, Pallas kernels for 8%

profile of v2, /device:TPU:1, one launch (start us, length us, event | category | flops | bytes accessed | tf_op | source)
XLA Modules:
  0.0 231.4 jit_solution(8283652617891342532)
XLA Ops:
  7.3 0.7 convert_multiply_fusion
  8.0 1.2 cosine_convert_fusion
  9.2 5.9 %convert_element_type.430 = f32[16,134656]{1,0:T(8,128)} convert(s32[16,134656]{1,0:T(8,128)} %param.6) | non-fusion elementwise | flops 2154496 | bytes 17235968 | tf_op jit(solution)/shard_map/convert_element_type | solution.py:38
  15.1 10.1 %reshape.1171 = f32[16,263,512]{2,1,0:T(8,128)} reshape(f32[16,134656]{1,0:T(8,128)} %convert_element_type.430) | data formatting | bytes 17235968 | tf_op jit(solution)/shard_map/reshape | solution.py:38
  25.2 27.3 %fusion.61 = bf16[128,16,2,256]{3,0,1,2:T(8,128)(2,1)} fusion(f32[16]{0:T(128)S(1)} %convert_multiply_fusion, f32[16,263,512]{2,1,0:T(8,128)} %reshape.1171, f32[512]{0:T(512)S(1)} %get-tuple-element.221, f32[512]{0:T(512)S(1)} %get-tuple-element.222, f32[512]{0:T(512)S(1)} %get-tuple-element.223, f32[512]{0:T(512)S(1)} %get-tuple-element.224, ...), kind=kOutput, calls=%fused_computation.117 | convolution fusion | flops 1109917696 | bytes 69484608 | tf_op jit(solution)/shard_map/itj,jrc->cirt/dot_general | solution.py:43
  52.5 3.0 %copy.26 = bf16[128,16,2,256]{0,3,2,1:T(8,128)(2,1)S(1)} copy(bf16[128,16,2,256]{3,0,1,2:T(8,128)(2,1)} %fusion.61) | data formatting | bytes 4194304 | tf_op jit(solution)/shard_map/convert_element_type | solution.py:45
  55.6 2.9 %copy.27 = bf16[128,16,512]{2,1,0:T(8,128)(2,1)} copy(bf16[128,16,512]{0,2,1:T(8,128)(2,1)S(1)} %bitcast.176) | data formatting | bytes 4194304 | tf_op jit(solution)/shard_map/reshape | solution.py:143
  58.5 35.7 %all_to_all.20 = bf16[128,16,512]{2,1,0:T(8,128)(2,1)S(1)} all-to-all(bf16[128,16,512]{2,1,0:T(8,128)(2,1)} %copy.27), channel_id=1, replica_groups=mesh['chan'=32,'blk'=4] {'chan'}, dimensions={0} | all-to-all | bytes 4194304 | tf_op jit(solution)/shard_map/all_to_all | solution.py:144
  94.2 1.5 copy.28
  95.7 1.0 multiply_add_fusion.2
  96.8 62.1 %all-gather.2.cloned.1.call-done = bf16[4,4,512,512]{3,2,0,1:T(8,128)(2,1)} async-done(((bf16[4,1,512,512]{3,2,0,1:T(8,128)(2,1)}), bf16[4,4,512,512]{3,2,0,1:T(8,128)(2,1)}) %all-gather.2.cloned.1.call-update) | async-done | bytes 8388624 | tf_op jit(solution)/shard_map/all_gather | solution.py:146
  158.9 8.1 %copy.30 = bf16[4,32,4,16,512]{4,3,2,1,0:T(8,128)(2,1)} copy(bf16[4,32,4,16,512]{4,3,1,0,2:T(8,128)(2,1)} %bitcast.174) | data formatting | bytes 16777216 | tf_op jit(solution)/shard_map/transpose | solution.py:148
  167.0 1.7 constant_dynamic-slice_fusion
  168.7 25.6 %while.16 = (s32[]{:T(128)}, f32[1,2048]{1,0:T(1,128)S(1)}, f32[1,2048]{1,0:T(1,128)S(1)}, f32[1,2048]{1,0:T(1,128)S(1)}, f32[1,2048]{1,0:T(1,128)S(1)}, /*index...) while((s32[]{:T(128)}, f32[1,2048]{1,0:T(1,128)S(1)}, ...), condition=%wide.region_3.4_spmd.clone, body=%wide.region_0.3_spmd.clone.sunk | while | flops 50787840 | bytes 9187491 | solution.py:92
  168.7 0.6 add_reduce_fusion.4
  170.1 0.4 fusion.137
  170.5 0.6 convolution_bitcast_fusion.4
  171.2 0.7 add_reduce_fusion.5
  172.6 0.4 fusion.146
  173.1 0.6 convolution_bitcast_fusion.5
  173.8 0.6 add_reduce_fusion.4
  175.2 0.4 fusion.137
  175.6 0.6 convolution_bitcast_fusion.4
  176.3 0.7 add_reduce_fusion.5
  178.2 0.6 convolution_bitcast_fusion.5
  178.9 0.6 add_reduce_fusion.4
  180.3 0.4 fusion.137
  180.7 0.6 convolution_bitcast_fusion.4
  181.4 0.7 add_reduce_fusion.5
  183.3 0.6 convolution_bitcast_fusion.5
  184.1 0.6 add_reduce_fusion.4
  185.4 0.4 fusion.137
  185.8 0.6 convolution_bitcast_fusion.4
  186.5 0.7 add_reduce_fusion.5
  188.4 0.6 convolution_bitcast_fusion.5
  189.2 0.6 add_reduce_fusion.4
  190.5 0.4 fusion.137
  191.0 0.6 convolution_bitcast_fusion.4
  191.6 0.7 add_reduce_fusion.5
  193.1 0.4 fusion.146
  193.5 0.6 convolution_bitcast_fusion.5
  194.3 0.5 broadcast.283
  194.8 0.7 reduce.14
  195.5 0.7 reduce.15
  196.3 0.8 copy.31
  197.1 7.3 %all-to-all-start.1 = ((f32[2,128,1,16]{3,2,0,1:T(1,128)}), f32[2,128,1,16]{3,2,0,1:T(1,128)S(1)}, u32[]{:S(2)}, u32[]{:S(2)}) async-start(f32[2,128,1,16]{3,2,0,1:T(1,128)} %copy.31), calls=%async_computation.1 | async-start | bytes 262144 | tf_op jit(solution)/shard_map/all_to_all | solution.py:163
  204.4 19.5 %shard_map.59 = bf16[2,4,512,2048]{3,2,1,0:T(8,128)(2,1)} custom-call(s32[1]{0:T(128)} %bitcast.block_ref, bf16[4,2048,512]{2,1,0:T(8,128)(2,1)} %bitcast.172, bf16[4,2048,512]{2,1,0:T(8,128)(2,1)} %bitcast.173), custom_call_target="tpu_custom_call" | custom-call | flops 8589934592 | bytes 27262976 | tf_op jit(solution)/shard_map/pallas_call | solution.py:124
  223.9 0.7 copy.32
  (99 shorter events, 3.2 us)
Async XLA Ops:
  7.2 151.7 %all-gather.2.cloned.1.call-start = ((), (), s32[]{:S(2)}) async-start(), calls=%async_computation.2 | async-start | bytes 10485760 | tf_op jit(solution)/shard_map/all_gather | solution.py:146
  197.1 26.8 %all-to-all-start.1 = ((f32[2,128,1,16]{3,2,0,1:T(1,128)}), f32[2,128,1,16]{3,2,0,1:T(1,128)S(1)}, u32[]{:S(2)}, u32[]{:S(2)}) async-start(f32[2,128,1,16]{3,2,0,1:T(1,128)} %copy.31), calls=%async_computation.1 | async-start | bytes 262144 | tf_op jit(solution)/shard_map/all_to_all | solution.py:163
Sparse Core Ops, SparseCore 0:
  95.8 63.0 all-gather.1

commit v3 on v2

--- a/solution.py
+++ b/solution.py
@@ -108,29 +108,43 @@
     out_ref[1, 0] = (imag * (1.0 / SPECTRA)).astype(out_ref.dtype)
 
 
-def correlate(whole, block_index, row_count, col_block=512):
-    chans, inputs, width = whole.shape
+def correlate(data, scalars, row_count, out=None, total_chans=None, col_block=512):
+    chans, inputs, width = data.shape
+    total_chans = chans if total_chans is None else total_chans
     grid = (chans, inputs // col_block)
+    in_specs = [
+        pl.BlockSpec((1, row_count, width), lambda c, j, s: (c, s[0], 0)),
+        pl.BlockSpec((1, col_block, width), lambda c, j, s: (c, j, 0)),
+    ]
+    operands = [scalars, data, data]
+    aliases = {}
+    if out is not None:
+        in_specs.append(pl.BlockSpec(memory_space=pl.ANY))
+        operands.append(out)
+        aliases = {3: 0}
     spec = pltpu.PrefetchScalarGridSpec(
         num_scalar_prefetch=1,
         grid=grid,
-        in_specs=[
-            pl.BlockSpec((1, row_count, width), lambda c, j, blk: (c, blk[0], 0)),
-            pl.BlockSpec((1, col_block, width), lambda c, j, blk: (c, j, 0)),
-        ],
-        out_specs=pl.BlockSpec((2, 1, row_count, col_block), lambda c, j, blk: (0, c, 0, j)),
+        in_specs=in_specs,
+        out_specs=pl.BlockSpec((2, 1, row_count, col_block), lambda c, j, s: (0, s[1] + c, 0, j)),
     )
     flops = 8 * chans * row_count * inputs * (width // 2)
+    kernel = correlate_kernel if out is None else correlate_into_kernel
     return pl.pallas_call(
-        correlate_kernel,
+        kernel,
         grid_spec=spec,
-        out_shape=jax.ShapeDtypeStruct((2, chans, row_count, inputs), jnp.bfloat16),
+        out_shape=jax.ShapeDtypeStruct((2, total_chans, row_count, inputs), jnp.bfloat16),
+        input_output_aliases=aliases,
         cost_estimate=pl.CostEstimate(
             flops=flops,
             transcendentals=0,
             bytes_accessed=2 * chans * (inputs * width + row_count * width + 2 * row_count * inputs),
         ),
-    )(jnp.reshape(block_index, (1,)).astype(jnp.int32), whole, whole)
+    )(*operands)
+
+
+def correlate_into_kernel(block_ref, rows_ref, cols_ref, prev_ref, out_ref):
+    correlate_kernel(block_ref, rows_ref, cols_ref, out_ref)
 
 
 def shards(voltages, flags, model_amp, model_phase):
@@ -140,28 +154,36 @@
     blk_count = lax.axis_size("blk")
     chan_count = lax.axis_size("chan")
     block_index = lax.axis_index("blk")
-    spectra = spectra.reshape(spectra.shape[0], input_count, 2 * SPECTRA)
-    turned = lax.all_to_all(spectra, "chan", split_axis=0, concat_axis=1, tiled=True)
-    local_chans = turned.shape[0]
-    grouped = lax.all_gather(turned, "blk", axis=1, tiled=False)
-    grouped = grouped.reshape(local_chans, blk_count, chan_count, input_count, 2 * SPECTRA)
-    whole = jnp.swapaxes(grouped, 1, 2).reshape(local_chans, -1, 2 * SPECTRA)
-    all_inputs = whole.shape[1]
+    spectra = spectra.reshape(chan_count, 2, 2, input_count, 2 * SPECTRA)
+    send = jnp.broadcast_to(
+        spectra[:, None], (chan_count, 2, 2, 2, input_count, 2 * SPECTRA)
+    )
+    send = send.reshape(chan_count * blk_count, 2, input_count, 2 * SPECTRA)
+    send = jnp.swapaxes(send, 0, 1)
+    got = lax.all_to_all(send, ("chan", "blk"), split_axis=1, concat_axis=1, tiled=True)
+    mine = got.reshape(2, -1, 2 * SPECTRA)
+    all_inputs = mine.shape[1]
     row_count = all_inputs // blk_count
-    visibility = correlate(whole, block_index, row_count)
+    core = block_index % 2
+    level = block_index // 2
+    theirs = lax.ppermute(mine, "blk", perm=[(b, b ^ 1) for b in range(blk_count)])
+    local_chans = 4
+    first = jnp.stack([block_index, 2 * core]).astype(jnp.int32)
+    second = jnp.stack([block_index, 2 - 2 * core]).astype(jnp.int32)
+    visibility = correlate(mine, first, row_count, total_chans=local_chans)
+    visibility = correlate(theirs, second, row_count, out=visibility, total_chans=local_chans)
 
-    solve_chans = local_chans // blk_count
-    data = lax.dynamic_slice_in_dim(whole, block_index * solve_chans, solve_chans, 0)
-    amp = lax.dynamic_slice_in_dim(model_amp, block_index * solve_chans, solve_chans, 0)
-    phase = lax.dynamic_slice_in_dim(model_phase, block_index * solve_chans, solve_chans, 0)
+    data = lax.dynamic_index_in_dim(mine, level, 0, keepdims=False)
+    solve = 2 * core + level
+    amp = lax.dynamic_index_in_dim(model_amp, solve, 0, keepdims=False)
+    phase = lax.dynamic_index_in_dim(model_phase, solve, 0, keepdims=False)
     full_re = amp * jnp.cos(phase)
     full_im = amp * jnp.sin(phase)
-    solved = jax.vmap(solve_gains)(data, full_re, full_im)
-    solved = jnp.stack(solved)
-    owners = solved.reshape(2, solve_chans, chan_count * blk_count, input_count)
-    owners = jnp.swapaxes(owners, 1, 2)
+    solved = jnp.stack(solve_gains(data, full_re, full_im))
+    owners = solved.reshape(2, chan_count * blk_count, 1, input_count)
     gains = lax.all_to_all(owners, ("chan", "blk"), split_axis=1, concat_axis=1, tiled=True)
-    gains = gains.reshape(2, -1, input_count)
+    gains = gains.reshape(2, chan_count, 2, 2, input_count)
+    gains = jnp.swapaxes(gains, 2, 3).reshape(2, -1, input_count)
     return (visibility, gains)
 
 

time: 232 us -> 181 us (0.78)
  blocking collectives: 35.7 us -> 0 us
  between operations: 14.1 us -> 0.8 us
  waiting for transfers between devices: 62.2 us -> 51.3 us
  starting transfers between devices: 7.3 us -> 17 us
  Pallas kernels: 19.5 us -> 22.3 us
    all_gather x1 -> x0, waiting for transfers between devices: 62.1 us -> none  [shards(): grouped = lax.all_gather(turned, 'blk', axis=1, tiled=False)]
    all_to_all x0 -> x1, waiting for transfers between devices: none -> 51.3 us  [shards(): lax.all_to_all(send, ('chan', 'blk'), split_axis=1, concat_axis=1, tiled=...]
    all_to_all x1 -> x0, blocking collectives: 35.7 us -> none  [shards(): lax.all_to_all(spectra, 'chan', split_axis=0, concat_axis=1, tiled=True)]
    all_to_all x0 -> x1, starting transfers between devices: none -> 12 us  [shards(): lax.all_to_all(send, ('chan', 'blk'), split_axis=1, concat_axis=1, tiled=...]
    transpose x1, local copies, waits for them, and re-layouts: 8.07 us -> 0.07 us  [shards(): gains = jnp.swapaxes(gains, 2, 3).reshape(2, -1, input_count)]
    broadcast_in_dim x0 -> x2, local copies, waits for them, and re-layouts: none -> 5.79 us  [shards(): jnp.broadcast_to(spectra[:, None], (chan_count, 2, 2, 2, input_count, 2 *...]
    all_to_all x1 -> x2, local copies, waits for them, and re-layouts: 1.51 us -> 4.69 us  [the longest x1 4.68 us: shards(): lax.all_to_all(send, ('chan', 'blk'), split_axis=1, concat_axis=1, tiled=...]
    reshape x1 -> x0, local copies, waits for them, and re-layouts: 2.9 us -> none  [shards(): spectra = spectra.reshape(spectra.shape[0], input_count, 2 * SPECTRA)]
  transfers between devices with their start and end apart: 2 -> 3, of which waited for: 1 -> 1; matrix products, arithmetic and copies ran while one was open for 0% -> 13% of each run, Pallas kernels for 8% -> 6%
where the time goes in v3:
time: 181 us; the launch traced here: 180 us
  waiting for transfers between devices  51.3 us (28%)
  matrix products  36.3 us (20%)
  local copies, waits for them, and re-layouts  27.6 us (15%)
  Pallas kernels  22.3 us (12%)
  other arithmetic  17.9 us (10%)
  starting transfers between devices  17 us (9%)
  loops' own time  7.26 us (4%)
    all_to_all x1, waiting for transfers between devices, shards(): lax.all_to_all(send, ('chan', 'blk'), split_axis=1, concat_axis=1, tiled=...  51.3 us
    dot_general x1, matrix products, channelize(): jnp.einsum('itj,jrc->cirt', frames, table, preferred_element_type=jnp.flo...  26.1 us
    pallas_call x2, Pallas kernels, correlate(): pl.pallas_call(kernel, grid_spec=spec, out_shape=jax.ShapeDtypeStruct((2,...  22.3 us
    all_to_all x1, starting transfers between devices, shards(): lax.all_to_all(send, ('chan', 'blk'), split_axis=1, concat_axis=1, tiled=...  12 us
    reshape x1, local copies, waits for them, and re-layouts, channelize(): voltages.astype(jnp.float32).reshape(count, SPECTRA + TAPS - 1, FRAME)  10.1 us
    dot_general x20, matrix products, exact_dot(): lax.dot_general(lhs, split3(rhs_f32), (dims, ((), ())), preferred_element...  10.1 us
    another operation x1, loops' own time, solve_gains(): return lax.fori_loop(0, ITERS // 2, paired, (start_re, start_im))  7.26 us
    reduce_sum x10, other arithmetic, sweep(): power = jnp.sum(probe_re * probe_re + probe_im * probe_im)  6.12 us
  transfers between devices with their start and end apart: 3, of which 1 were waited for; matrix products, arithmetic and copies ran while one was open for 13% of the time, Pallas kernels for 6%

profile of v3, /device:TPU:1, one launch (start us, length us, event | category | flops | bytes accessed | tf_op | source)
XLA Modules:
  0.0 180.3 jit_solution(4644425067421734622)
XLA Ops:
  0.7 0.7 convert_multiply_fusion
  1.4 1.2 cosine_convert_fusion
  2.6 5.9 %convert_element_type.158 = f32[16,134656]{1,0:T(8,128)} convert(s32[16,134656]{1,0:T(8,128)} %param.6) | non-fusion elementwise | flops 2154496 | bytes 17235968 | tf_op jit(solution)/shard_map/convert_element_type | solution.py:38
  8.5 10.1 %reshape.233 = f32[16,263,512]{2,1,0:T(8,128)} reshape(f32[16,134656]{1,0:T(8,128)} %convert_element_type.158) | data formatting | bytes 17235968 | tf_op jit(solution)/shard_map/reshape | solution.py:38
  18.7 26.1 %fusion.43 = bf16[128,16,2,256]{3,0,1,2:T(8,128)(2,1)S(1)} fusion(f32[16]{0:T(128)S(1)} %convert_multiply_fusion, f32[16,263,512]{2,1,0:T(8,128)} %reshape.233, f32[512]{0:T(512)S(1)} %get-tuple-element.208, f32[512]{0:T(512)S(1)} %get-tuple-element.209, f32[512]{0:T(512)S(1)} %get-tuple-element.210, f32[512]{0:T(512)S(1)} %get-tuple-element.211, ...), kind=kOutput, calls=%fused_computation.91 | convolution fusion | flops 1109917696 | bytes 69484608 | tf_op jit(solution)/shard_map/itj,jrc->cirt/dot_general | solution.py:43
  44.8 3.5 %copy.19 = bf16[128,16,2,256]{3,2,1,0:T(2,128)(2,1)} copy(bf16[128,16,2,256]{3,0,1,2:T(8,128)(2,1)S(1)} %fusion.43) | data formatting | bytes 4194304 | tf_op jit(solution)/shard_map/convert_element_type | solution.py:45
  48.3 3.2 %broadcast_in_dim.21 = bf16[32,2,2,16,512]{4,3,2,1,0:T(8,128)(2,1)S(1)} reshape(bf16[128,16,2,256]{3,2,1,0:T(2,128)(2,1)} %copy.19) | data formatting | bytes 4194304 | tf_op jit(solution)/shard_map/broadcast_in_dim | solution.py:158
  51.5 2.6 %broadcast_in_dim.22 = bf16[32,2,2,2,16,512]{5,4,3,2,1,0:T(8,128)(2,1)} broadcast(bf16[32,2,2,16,512]{4,3,2,1,0:T(8,128)(2,1)S(1)} %broadcast_in_dim.21), dimensions={0,2,3,4,5} | broadcast | bytes 6291456 | tf_op jit(solution)/shard_map/broadcast_in_dim | solution.py:158
  54.1 12.0 %all-to-all-start = ((bf16[2,128,16,512]{3,2,0,1:T(8,128)(2,1)}), bf16[2,128,16,512]{3,2,0,1:T(8,128)(2,1)}, u32[]{:S(2)}, u32[]{:S(2)}) async-start(bf16[2,128,16,512]{3,2,0,1:T(8,128)(2,1)} %bitcast.81), calls=%async_computation | async-start | bytes 8388608 | tf_op jit(solution)/shard_map/all_to_all | solution.py:163
  66.1 0.6 pad_add_fusion.1.block_ref
  66.7 0.6 pad_add_fusion.block_ref
  67.3 1.0 add_bitcast_fusion
  68.4 51.3 %all-to-all-done = bf16[2,128,16,512]{3,2,0,1:T(8,128)(2,1)} async-done(((bf16[2,128,16,512]{3,2,0,1:T(8,128)(2,1)}), bf16[2,128,16,512]{3,2,0,1:T(8,128)(2,1)}, u32[]{:S(2)}, u32[]{:S(2)}) %all-to-all-start) | async-done | bytes 4194336 | tf_op jit(solution)/shard_map/all_to_all | solution.py:163
  119.6 4.7 %copy.20 = bf16[2,128,16,512]{3,2,1,0:T(8,128)(2,1)} copy(bf16[2,128,16,512]{3,2,0,1:T(8,128)(2,1)} %all-to-all-done) | data formatting | bytes 8388608 | tf_op jit(solution)/shard_map/all_to_all | solution.py:163
  124.3 0.5 collective-permute-start
  124.9 1.7 dynamic-slice_bitcast_fusion
  126.6 25.2 %while.16 = (s32[]{:T(128)}, f32[2048]{0:T(1024)S(1)}, f32[2048]{0:T(1024)S(1)}, f32[2048]{0:T(1024)S(1)}, f32[2048]{0:T(1024)S(1)}, /*index=5*/bf16[2048,512]{1...) while((s32[]{:T(128)}, f32[2048]{0:T(1024)S(1)}, ...), condition=%wide.region_3.4_spmd.clone, body=%wide.region_0.3_spmd.clone.sunk | while | flops 50806272 | bytes 9220263 | solution.py:92
  126.6 0.6 add_reduce_fusion.4
  127.9 0.4 convolution_bitcast_fusion.8
  128.4 0.6 convolution_bitcast_fusion.9
  129.1 0.6 add_reduce_fusion.5
  130.5 0.4 convolution_bitcast_fusion.10
  130.9 0.6 convolution_bitcast_fusion.11
  131.6 0.6 add_reduce_fusion.4
  133.4 0.6 convolution_bitcast_fusion.9
  134.1 0.6 add_reduce_fusion.5
  135.5 0.4 convolution_bitcast_fusion.10
  135.9 0.6 convolution_bitcast_fusion.11
  136.7 0.6 add_reduce_fusion.4
  138.4 0.6 convolution_bitcast_fusion.9
  139.2 0.6 add_reduce_fusion.5
  140.5 0.4 convolution_bitcast_fusion.10
  141.0 0.6 convolution_bitcast_fusion.11
  141.7 0.6 add_reduce_fusion.4
  143.5 0.6 convolution_bitcast_fusion.9
  144.2 0.6 add_reduce_fusion.5
  145.6 0.4 convolution_bitcast_fusion.10
  146.0 0.6 convolution_bitcast_fusion.11
  146.8 0.6 add_reduce_fusion.4
  148.5 0.6 convolution_bitcast_fusion.9
  149.2 0.6 add_reduce_fusion.5
  150.6 0.4 convolution_bitcast_fusion.10
  151.0 0.6 convolution_bitcast_fusion.11
  152.0 0.8 copy.21
  152.8 4.5 %all-to-all-start.1 = ((f32[2,128,1,16]{3,2,0,1:T(1,128)}), f32[2,128,1,16]{3,2,0,1:T(1,128)S(1)}, u32[]{:S(2)}, u32[]{:S(2)}) async-start(f32[2,128,1,16]{3,2,0,1:T(1,128)} %copy.21), calls=%async_computation.1 | async-start | bytes 262144 | tf_op jit(solution)/shard_map/all_to_all | solution.py:184
  157.3 11.1 %shard_map.59.prev_ref = bf16[2,4,512,2048]{3,2,1,0:T(8,128)(2,1)} custom-call(s32[2]{0:T(128)} %pad_add_fusion.1.block_ref, bf16[2,2048,512]{2,1,0:T(8,128)(2,1)} %bitcast.8.rows_ref.cols_ref, bf16[2,2048,512]{2,1,0:T(8,128)(2,1)} %bitcast.8.rows_ref.cols_ref), custom_call_target="tpu_custom_call" | custom-call | flops 4294967296 | bytes 13631488 | tf_op jit(solution)/shard_map/pallas_call | solution.py:133
  168.5 0.7 copy.24
  169.2 11.1 %shard_map.60 = bf16[2,4,512,2048]{3,2,1,0:T(8,128)(2,1)} custom-call(s32[2]{0:T(128)} %pad_add_fusion.block_ref, bf16[2,2048,512]{2,1,0:T(8,128)(2,1)} %collective-permute-done.rows_ref.cols_ref, bf16[2,2048,512]{2,1,0:T(8,128)(2,1)} %collective-permute-done.rows_ref.cols_ref, ...), custom_call_target="tpu_custom_call", output_to_operand_aliasing={{}: (3, {})} | custom-call | flops 4294967296 | bytes 13631488 | tf_op jit(solution)/shard_map/pallas_call | solution.py:133
  (107 shorter events, 3.5 us)
Async XLA Ops:
  54.1 65.5 %all-to-all-start = ((bf16[2,128,16,512]{3,2,0,1:T(8,128)(2,1)}), bf16[2,128,16,512]{3,2,0,1:T(8,128)(2,1)}, u32[]{:S(2)}, u32[]{:S(2)}) async-start(bf16[2,128,16,512]{3,2,0,1:T(8,128)(2,1)} %bitcast.81), calls=%async_computation | async-start | bytes 8388608 | tf_op jit(solution)/shard_map/all_to_all | solution.py:163
  124.3 44.9 %collective-permute-start = (bf16[2,2048,512]{2,1,0:T(8,128)(2,1)}, bf16[2,2048,512]{2,1,0:T(8,128)(2,1)}, u32[]{:S(2)}, u32[]{:S(2)}) collective-permute-start(bf16[2,2048,512]{2,1,0:T(8,128)(2,1)} %bitcast.8.rows_ref.cols_ref), channel_id=1, source_target_pairs={{0,1},{1,0},{2,3},{3,2},{4,5},{5,4},{6,7},{7,6},{8,9},{9,8},{10,11... | collective-permute-start | bytes 12582920 | tf_op jit(solution)/shard_map/ppermute | solution.py:169
  152.8 15.7 %all-to-all-start.1 = ((f32[2,128,1,16]{3,2,0,1:T(1,128)}), f32[2,128,1,16]{3,2,0,1:T(1,128)S(1)}, u32[]{:S(2)}, u32[]{:S(2)}) async-start(f32[2,128,1,16]{3,2,0,1:T(1,128)} %copy.21), calls=%async_computation.1 | async-start | bytes 262144 | tf_op jit(solution)/shard_map/all_to_all | solution.py:184

commit v4 on v3

--- a/solution.py
+++ b/solution.py
@@ -31,18 +31,47 @@
     return jnp.stack([jnp.cos(angle), -jnp.sin(angle)], axis=1).astype(jnp.bfloat16)
 
 
+def transform_kernel(keep_ref, table_ref, frames_ref, out_ref):
+    group = frames_ref.shape[0]
+    base = pl.program_id(0) * group
+    scale = 1.0 / (64.0 * math.sqrt(FRAME))
+    for item in range(group):
+        result = lax.dot_general(
+            table_ref[...], frames_ref[item], (((1,), (1,)), ((), ())),
+            preferred_element_type=jnp.float32,
+        )
+        result = result * (scale * keep_ref[base + item])
+        out_ref[:, item, :SPECTRA] = result[:CHANS].astype(out_ref.dtype)
+        out_ref[:, item, SPECTRA:] = result[CHANS:].astype(out_ref.dtype)
+
+
 def channelize(voltages, keep):
     window = window_table()
     table = transform_table()
     count = voltages.shape[0]
-    samples = voltages.astype(jnp.float32).reshape(count, SPECTRA + TAPS - 1, FRAME)
-    frames = window[0] * samples[:, 0:SPECTRA, :]
+    samples = voltages.astype(jnp.bfloat16).reshape(count, SPECTRA + TAPS - 1, FRAME)
+    frames = window[0] * samples[:, 0:SPECTRA, :].astype(jnp.float32)
     for tap in range(1, TAPS):
-        frames = frames + window[tap] * samples[:, tap : tap + SPECTRA, :]
+        frames = frames + window[tap] * samples[:, tap : tap + SPECTRA, :].astype(jnp.float32)
     frames = frames.astype(jnp.bfloat16)
-    spectra = jnp.einsum("itj,jrc->cirt", frames, table, preferred_element_type=jnp.float32)
-    scale = 1.0 / (64.0 * math.sqrt(FRAME))
-    return (spectra * (scale * keep)[None, :, None, None]).astype(jnp.bfloat16)
+    table_t = jnp.transpose(table.reshape(FRAME, 2 * CHANS))
+    group = 8
+    return pl.pallas_call(
+        transform_kernel,
+        grid=(count // group,),
+        in_specs=[
+            pl.BlockSpec(memory_space=pltpu.SMEM),
+            pl.BlockSpec((2 * CHANS, FRAME), lambda g: (0, 0)),
+            pl.BlockSpec((group, SPECTRA, FRAME), lambda g: (g, 0, 0)),
+        ],
+        out_specs=pl.BlockSpec((CHANS, group, 2 * SPECTRA), lambda g: (0, g, 0)),
+        out_shape=jax.ShapeDtypeStruct((CHANS, count, 2 * SPECTRA), jnp.bfloat16),
+        cost_estimate=pl.CostEstimate(
+            flops=2 * count * SPECTRA * FRAME * 2 * CHANS,
+            transcendentals=0,
+            bytes_accessed=2 * count * SPECTRA * FRAME + 2 * CHANS * count * 2 * SPECTRA,
+        ),
+    )(keep, table_t, frames)
 
 
 def split3(value):

time: 181 us -> 175 us (0.967)
  matrix products: 36.3 us -> 10.1 us
  other arithmetic: 17.9 us -> 41.3 us
  local copies, waits for them, and re-layouts: 27.6 us -> 17.4 us
  Pallas kernels: 22.3 us -> 28.7 us
    dot_general x1 -> x0, matrix products: 26.1 us -> none  [channelize(): jnp.einsum('itj,jrc->cirt', frames, table, preferred_element_type=jnp.flo...]
    convert_element_type x1 -> x3, other arithmetic: 5.91 us -> 29.2 us  [the longest x1 22.8 us: channelize(): frames = frames.astype(jnp.bfloat16)]
    pallas_call x0 -> x1, Pallas kernels: none -> 6.44 us  [channelize(): pl.pallas_call(transform_kernel, grid=(count // group,), in_specs=[pl.Blo...]
    reshape x1, local copies, waits for them, and re-layouts: 10.1 us -> 5.03 us  [channelize(): voltages.astype(jnp.bfloat16).reshape(count, SPECTRA + TAPS - 1, FRAME)]
    convert_element_type x1 -> x0, local copies, waits for them, and re-layouts: 3.48 us -> none  [channelize(): return (spectra * (scale * keep)[None, :, None, None]).astype(jnp.bfloat16)]
    broadcast_in_dim x2 -> x1, local copies, waits for them, and re-layouts: 5.79 us -> 4.19 us  [shards(): jnp.broadcast_to(spectra[:, None], (chan_count, 2, 2, 2, input_count, 2 *...]
  transfers between devices with their start and end apart: 3 -> 3, of which waited for: 1 -> 1; matrix products, arithmetic and copies ran while one was open for 13% -> 14% of each run, Pallas kernels for 6% -> 6%
where the time goes in v4:
time: 175 us; the launch traced here: 174 us
  waiting for transfers between devices  51.3 us (29%)
  other arithmetic  41.3 us (24%)
  Pallas kernels  28.7 us (16%)
  local copies, waits for them, and re-layouts  17.4 us (10%)
  starting transfers between devices  17 us (10%)
  matrix products  10.1 us (6%)
  loops' own time  7.26 us (4%)
    all_to_all x1, waiting for transfers between devices, shards(): lax.all_to_all(send, ('chan', 'blk'), split_axis=1, concat_axis=1, tiled=...  51.3 us
    convert_element_type x1, other arithmetic, channelize(): frames = frames.astype(jnp.bfloat16)  22.8 us
    pallas_call x2, Pallas kernels, correlate(): pl.pallas_call(kernel, grid_spec=spec, out_shape=jax.ShapeDtypeStruct((2,...  22.3 us
    all_to_all x1, starting transfers between devices, shards(): lax.all_to_all(send, ('chan', 'blk'), split_axis=1, concat_axis=1, tiled=...  12 us
    dot_general x20, matrix products, exact_dot(): lax.dot_general(lhs, split3(rhs_f32), (dims, ((), ())), preferred_element...  10.1 us
    another operation x1, loops' own time, solve_gains(): return lax.fori_loop(0, ITERS // 2, paired, (start_re, start_im))  7.26 us
    pallas_call x1, Pallas kernels, channelize(): pl.pallas_call(transform_kernel, grid=(count // group,), in_specs=[pl.Blo...  6.44 us
    reduce_sum x10, other arithmetic, sweep(): power = jnp.sum(probe_re * probe_re + probe_im * probe_im)  6.12 us
  transfers between devices with their start and end apart: 3, of which 1 were waited for; matrix products, arithmetic and copies ran while one was open for 14% of the time, Pallas kernels for 6%

profile of v4, /device:TPU:1, one launch (start us, length us, event | category | flops | bytes accessed | tf_op | source)
XLA Modules:
  0.0 173.8 jit_solution(1095188039699993781)
XLA Ops:
  0.7 1.2 subtract_convert_fusion.4.keep_ref
  1.9 1.2 cosine_convert_fusion
  3.1 5.3 %convert_element_type.182 = bf16[16,134656]{1,0:T(8,128)(2,1)} convert(s32[16,134656]{1,0:T(8,128)} %param.6) | non-fusion elementwise | flops 2154496 | bytes 12926976 | tf_op jit(solution)/shard_map/convert_element_type | solution.py:52
  8.4 5.0 %reshape.235 = bf16[16,263,512]{2,1,0:T(8,128)(2,1)} reshape(bf16[16,134656]{1,0:T(8,128)(2,1)} %convert_element_type.182) | data formatting | bytes 8617984 | tf_op jit(solution)/shard_map/reshape | solution.py:52
  13.5 0.7 pad_maximum_fusion.2
  14.2 22.8 %add_convert_fusion.frames_ref = bf16[16,256,512]{2,1,0:T(8,128)(2,1)} fusion(bf16[16,263,512]{2,1,0:T(8,128)(2,1)} %reshape.235, f32[512]{0:T(512)S(1)} %get-tuple-element.208, f32[512]{0:T(512)S(1)} %get-tuple-element.209, f32[512]{0:T(512)S(1)} %get-tuple-element.210, f32[512]{0:T(512)S(1)} %get-tuple-element.211, f32[512]{0:T(512)S(1)} %get-tuple-element.212, ...), kind=kLoop, calls=%fused_computation.72 | loop fusion | flops 50331648 | bytes 37765120 | tf_op jit(solution)/shard_map/convert_element_type | solution.py:56
  37.0 6.4 %shard_map.59 = bf16[128,16,512]{2,1,0:T(8,128)(2,1)} custom-call(f32[16]{0:T(128)} %subtract_convert_fusion.4.keep_ref, bf16[256,512]{1,0:T(8,128)(2,1)} %bitcast.91, bf16[16,256,512]{2,1,0:T(8,128)(2,1)} %add_convert_fusion.frames_ref), custom_call_target="tpu_custom_call" | custom-call | flops 1073741824 | bytes 6291456 | tf_op jit(solution)/shard_map/pallas_call | solution.py:59
  43.4 4.2 %broadcast_in_dim.21 = bf16[32,2,2,2,16,512]{5,4,3,2,1,0:T(8,128)(2,1)} broadcast(bf16[32,2,2,16,512]{4,3,2,1,0:T(8,128)(2,1)} %bitcast.74), dimensions={0,2,3,4,5} | broadcast | bytes 6291456 | tf_op jit(solution)/shard_map/broadcast_in_dim | solution.py:187
  47.6 12.0 %all-to-all-start = ((bf16[2,128,16,512]{3,2,0,1:T(8,128)(2,1)}), bf16[2,128,16,512]{3,2,0,1:T(8,128)(2,1)}, u32[]{:S(2)}, u32[]{:S(2)}) async-start(bf16[2,128,16,512]{3,2,0,1:T(8,128)(2,1)} %bitcast.73), calls=%async_computation | async-start | bytes 8388608 | tf_op jit(solution)/shard_map/all_to_all | solution.py:192
  59.6 0.6 pad_add_fusion.1.block_ref
  60.2 0.6 pad_add_fusion.block_ref
  60.8 1.0 add_bitcast_fusion
  61.9 51.3 %all-to-all-done = bf16[2,128,16,512]{3,2,0,1:T(8,128)(2,1)} async-done(((bf16[2,128,16,512]{3,2,0,1:T(8,128)(2,1)}), bf16[2,128,16,512]{3,2,0,1:T(8,128)(2,1)}, u32[]{:S(2)}, u32[]{:S(2)}) %all-to-all-start) | async-done | bytes 4194336 | tf_op jit(solution)/shard_map/all_to_all | solution.py:192
  113.1 4.7 %copy.18 = bf16[2,128,16,512]{3,2,1,0:T(8,128)(2,1)} copy(bf16[2,128,16,512]{3,2,0,1:T(8,128)(2,1)} %all-to-all-done) | data formatting | bytes 8388608 | tf_op jit(solution)/shard_map/all_to_all | solution.py:192
  117.8 0.5 collective-permute-start
  118.3 1.7 dynamic-slice_bitcast_fusion
  120.1 25.2 %while.16 = (s32[]{:T(128)}, f32[2048]{0:T(1024)S(1)}, f32[2048]{0:T(1024)S(1)}, f32[2048]{0:T(1024)S(1)}, f32[2048]{0:T(1024)S(1)}, /*index=5*/bf16[2048,512]{1...) while((s32[]{:T(128)}, f32[2048]{0:T(1024)S(1)}, ...), condition=%wide.region_3.4_spmd.clone, body=%wide.region_0.3_spmd.clone.sunk | while | flops 50806272 | bytes 9220263 | solution.py:121
  120.1 0.6 add_reduce_fusion.4
  121.9 0.6 convolution_bitcast_fusion.9
  122.6 0.6 add_reduce_fusion.5
  123.9 0.4 convolution_bitcast_fusion.10
  124.4 0.6 convolution_bitcast_fusion.11
  125.1 0.6 add_reduce_fusion.4
  126.4 0.4 convolution_bitcast_fusion.8
  126.9 0.6 convolution_bitcast_fusion.9
  127.6 0.6 add_reduce_fusion.5
  129.0 0.4 convolution_bitcast_fusion.10
  129.4 0.6 convolution_bitcast_fusion.11
  130.2 0.6 add_reduce_fusion.4
  131.9 0.6 convolution_bitcast_fusion.9
  132.7 0.6 add_reduce_fusion.5
  134.0 0.4 convolution_bitcast_fusion.10
  134.5 0.6 convolution_bitcast_fusion.11
  135.2 0.6 add_reduce_fusion.4
  137.0 0.6 convolution_bitcast_fusion.9
  137.7 0.6 add_reduce_fusion.5
  139.1 0.4 convolution_bitcast_fusion.10
  139.5 0.6 convolution_bitcast_fusion.11
  140.2 0.6 add_reduce_fusion.4
  142.0 0.6 convolution_bitcast_fusion.9
  142.7 0.6 add_reduce_fusion.5
  144.1 0.4 convolution_bitcast_fusion.10
  144.5 0.6 convolution_bitcast_fusion.11
  145.5 0.8 copy.19
  146.2 4.5 %all-to-all-start.1 = ((f32[2,128,1,16]{3,2,0,1:T(1,128)}), f32[2,128,1,16]{3,2,0,1:T(1,128)S(1)}, u32[]{:S(2)}, u32[]{:S(2)}) async-start(f32[2,128,1,16]{3,2,0,1:T(1,128)} %copy.19), calls=%async_computation.1 | async-start | bytes 262144 | tf_op jit(solution)/shard_map/all_to_all | solution.py:213
  150.8 11.1 %shard_map.60.prev_ref = bf16[2,4,512,2048]{3,2,1,0:T(8,128)(2,1)} custom-call(s32[2]{0:T(128)} %pad_add_fusion.1.block_ref, bf16[2,2048,512]{2,1,0:T(8,128)(2,1)} %bitcast.7.rows_ref.cols_ref, bf16[2,2048,512]{2,1,0:T(8,128)(2,1)} %bitcast.7.rows_ref.cols_ref), custom_call_target="tpu_custom_call" | custom-call | flops 4294967296 | bytes 13631488 | tf_op jit(solution)/shard_map/pallas_call | solution.py:162
  162.0 0.7 copy.22
  162.7 11.1 %shard_map.61 = bf16[2,4,512,2048]{3,2,1,0:T(8,128)(2,1)} custom-call(s32[2]{0:T(128)} %pad_add_fusion.block_ref, bf16[2,2048,512]{2,1,0:T(8,128)(2,1)} %collective-permute-done.rows_ref.cols_ref, bf16[2,2048,512]{2,1,0:T(8,128)(2,1)} %collective-permute-done.rows_ref.cols_ref, ...), custom_call_target="tpu_custom_call", output_to_operand_aliasing={{}: (3, {})} | custom-call | flops 4294967296 | bytes 13631488 | tf_op jit(solution)/shard_map/pallas_call | solution.py:162
  (107 shorter events, 3.5 us)
Async XLA Ops:
  47.6 65.5 %all-to-all-start = ((bf16[2,128,16,512]{3,2,0,1:T(8,128)(2,1)}), bf16[2,128,16,512]{3,2,0,1:T(8,128)(2,1)}, u32[]{:S(2)}, u32[]{:S(2)}) async-start(bf16[2,128,16,512]{3,2,0,1:T(8,128)(2,1)} %bitcast.73), calls=%async_computation | async-start | bytes 8388608 | tf_op jit(solution)/shard_map/all_to_all | solution.py:192
  117.8 44.9 %collective-permute-start = (bf16[2,2048,512]{2,1,0:T(8,128)(2,1)}, bf16[2,2048,512]{2,1,0:T(8,128)(2,1)}, u32[]{:S(2)}, u32[]{:S(2)}) collective-permute-start(bf16[2,2048,512]{2,1,0:T(8,128)(2,1)} %bitcast.7.rows_ref.cols_ref), channel_id=1, source_target_pairs={{0,1},{1,0},{2,3},{3,2},{4,5},{5,4},{6,7},{7,6},{8,9},{9,8},{10,11... | collective-permute-start | bytes 12582920 | tf_op jit(solution)/shard_map/ppermute | solution.py:198
  146.2 15.7 %all-to-all-start.1 = ((f32[2,128,1,16]{3,2,0,1:T(1,128)}), f32[2,128,1,16]{3,2,0,1:T(1,128)S(1)}, u32[]{:S(2)}, u32[]{:S(2)}) async-start(f32[2,128,1,16]{3,2,0,1:T(1,128)} %copy.19), calls=%async_computation.1 | async-start | bytes 262144 | tf_op jit(solution)/shard_map/all_to_all | solution.py:213

commit v5 on v3

--- a/solution.py
+++ b/solution.py
@@ -31,18 +31,53 @@
     return jnp.stack([jnp.cos(angle), -jnp.sin(angle)], axis=1).astype(jnp.bfloat16)
 
 
+def transform_kernel(frames_ref, table_ref, keep_ref, out_ref):
+    count, width = frames_ref.shape
+    steps = width // FRAME
+    stacked = jnp.concatenate(
+        [frames_ref[:, step * FRAME : (step + 1) * FRAME] for step in range(steps)], axis=0
+    )
+    result = jnp.dot(stacked, table_ref[...], preferred_element_type=jnp.float32)
+    result = result * keep_ref[...]
+    out_ref[...] = result.astype(out_ref.dtype).reshape(out_ref.shape)
+
+
 def channelize(voltages, keep):
     window = window_table()
     table = transform_table()
     count = voltages.shape[0]
-    samples = voltages.astype(jnp.float32).reshape(count, SPECTRA + TAPS - 1, FRAME)
-    frames = window[0] * samples[:, 0:SPECTRA, :]
+    span = SPECTRA * FRAME
+    def weight(tap):
+        return jnp.broadcast_to(window[tap][None, None, :], (count, SPECTRA, FRAME)).reshape(
+            count, span
+        )
+
+    frames = weight(0) * voltages[:, 0:span].astype(jnp.float32)
     for tap in range(1, TAPS):
-        frames = frames + window[tap] * samples[:, tap : tap + SPECTRA, :]
+        frames = frames + weight(tap) * voltages[:, tap * FRAME : tap * FRAME + span].astype(
+            jnp.float32
+        )
     frames = frames.astype(jnp.bfloat16)
-    spectra = jnp.einsum("itj,jrc->cirt", frames, table, preferred_element_type=jnp.float32)
+    table = table.reshape(FRAME, 2 * CHANS)
     scale = 1.0 / (64.0 * math.sqrt(FRAME))
-    return (spectra * (scale * keep)[None, :, None, None]).astype(jnp.bfloat16)
+    chunk = 32
+    keep_rows = jnp.tile(scale * keep, chunk)[:, None]
+    return pl.pallas_call(
+        transform_kernel,
+        grid=(SPECTRA // chunk,),
+        in_specs=[
+            pl.BlockSpec((count, chunk * FRAME), lambda g: (0, g)),
+            pl.BlockSpec((FRAME, 2 * CHANS), lambda g: (0, 0)),
+            pl.BlockSpec((chunk * count, 1), lambda g: (0, 0)),
+        ],
+        out_specs=pl.BlockSpec((chunk, count, 2 * CHANS), lambda g: (g, 0, 0)),
+        out_shape=jax.ShapeDtypeStruct((SPECTRA, count, 2 * CHANS), jnp.bfloat16),
+        cost_estimate=pl.CostEstimate(
+            flops=2 * count * SPECTRA * FRAME * 2 * CHANS,
+            transcendentals=0,
+            bytes_accessed=2 * count * SPECTRA * FRAME + 2 * CHANS * count * 2 * SPECTRA,
+        ),
+    )(frames, table, keep_rows)
 
 
 def split3(value):
@@ -154,12 +189,12 @@
     blk_count = lax.axis_size("blk")
     chan_count = lax.axis_size("chan")
     block_index = lax.axis_index("blk")
-    spectra = spectra.reshape(chan_count, 2, 2, input_count, 2 * SPECTRA)
+    spectra = spectra.reshape(SPECTRA, input_count, 2, chan_count, 2, 2)
+    spectra = jnp.transpose(spectra, (5, 3, 4, 1, 2, 0))
     send = jnp.broadcast_to(
-        spectra[:, None], (chan_count, 2, 2, 2, input_count, 2 * SPECTRA)
-    )
-    send = send.reshape(chan_count * blk_count, 2, input_count, 2 * SPECTRA)
-    send = jnp.swapaxes(send, 0, 1)
+        spectra[:, :, None], (2, chan_count, 2, 2, input_count, 2, SPECTRA)
+    )
+    send = send.reshape(2, chan_count * blk_count, input_count, 2 * SPECTRA)
     got = lax.all_to_all(send, ("chan", "blk"), split_axis=1, concat_axis=1, tiled=True)
     mine = got.reshape(2, -1, 2 * SPECTRA)
     all_inputs = mine.shape[1]

time: 181 us -> 191 us (1.055)
  matrix products: 36.3 us -> 10.1 us
  other arithmetic: 17.9 us -> 38.6 us
  local copies, waits for them, and re-layouts: 27.6 us -> 35.1 us
  Pallas kernels: 22.3 us -> 29.6 us
    dot_general x1 -> x0, matrix products: 26.1 us -> none  [channelize(): jnp.einsum('itj,jrc->cirt', frames, table, preferred_element_type=jnp.flo...]
    convert_element_type x1 -> x2, other arithmetic: 5.91 us -> 26.7 us  [the longest x1 25.9 us: channelize(): frames = frames.astype(jnp.bfloat16)]
    pallas_call x0 -> x1, Pallas kernels: none -> 7.29 us  [channelize(): pl.pallas_call(transform_kernel, grid=(SPECTRA // chunk,), in_specs=[pl.B...]
    transpose x0 -> x1, local copies, waits for them, and re-layouts: none -> 5.53 us  [shards(): spectra = jnp.transpose(spectra, (5, 3, 4, 1, 2, 0))]
    pallas_call x0 -> x1, local copies, waits for them, and re-layouts: none -> 4.82 us  [channelize(): pl.pallas_call(transform_kernel, grid=(SPECTRA // chunk,), in_specs=[pl.B...]
    convert_element_type x1 -> x0, local copies, waits for them, and re-layouts: 3.48 us -> none  [channelize(): return (spectra * (scale * keep)[None, :, None, None]).astype(jnp.bfloat16)]
    reshape x1, local copies, waits for them, and re-layouts: 10.1 us -> 7.59 us  [shards(): send = send.reshape(2, chan_count * blk_count, input_count, 2 * SPECTRA)]
    broadcast_in_dim x2 -> x1, local copies, waits for them, and re-layouts: 5.79 us -> 6.56 us  [shards(): jnp.broadcast_to(spectra[:, :, None], (2, chan_count, 2, 2, input_count,...]
  transfers between devices with their start and end apart: 3 -> 3, of which waited for: 1 -> 1; matrix products, arithmetic and copies ran while one was open for 13% -> 12% of each run, Pallas kernels for 6% -> 6%
where the time goes in v5:
time: 191 us; the launch traced here: 190 us
  waiting for transfers between devices  51.2 us (27%)
  other arithmetic  38.6 us (20%)
  local copies, waits for them, and re-layouts  35.1 us (18%)
  Pallas kernels  29.6 us (15%)
  starting transfers between devices  17 us (9%)
  matrix products  10.1 us (5%)
  loops' own time  7.26 us (4%)
    all_to_all x1, waiting for transfers between devices, shards(): lax.all_to_all(send, ('chan', 'blk'), split_axis=1, concat_axis=1, tiled=...  51.2 us
    convert_element_type x1, other arithmetic, channelize(): frames = frames.astype(jnp.bfloat16)  25.9 us
    pallas_call x2, Pallas kernels, correlate(): pl.pallas_call(kernel, grid_spec=spec, out_shape=jax.ShapeDtypeStruct((2,...  22.3 us
    all_to_all x1, starting transfers between devices, shards(): lax.all_to_all(send, ('chan', 'blk'), split_axis=1, concat_axis=1, tiled=...  12 us
    dot_general x20, matrix products, exact_dot(): lax.dot_general(lhs, split3(rhs_f32), (dims, ((), ())), preferred_element...  10.1 us
    reshape x1, local copies, waits for them, and re-layouts, shards(): send = send.reshape(2, chan_count * blk_count, input_count, 2 * SPECTRA)  7.59 us
    pallas_call x1, Pallas kernels, channelize(): pl.pallas_call(transform_kernel, grid=(SPECTRA // chunk,), in_specs=[pl.B...  7.29 us
    another operation x1, loops' own time, solve_gains(): return lax.fori_loop(0, ITERS // 2, paired, (start_re, start_im))  7.26 us
  transfers between devices with their start and end apart: 3, of which 1 were waited for; matrix products, arithmetic and copies ran while one was open for 12% of the time, Pallas kernels for 6%

profile of v5, /device:TPU:1, one launch (start us, length us, event | category | flops | bytes accessed | tf_op | source)
XLA Modules:
  0.0 189.7 jit_solution(10647188808834556760)
XLA Ops:
  0.7 0.7 convert_multiply_fusion
  1.4 0.9 broadcast_in_dim_tile.4.keep_ref
  2.3 1.1 cosine_convert_fusion
  5.0 0.7 copy_bitcast_fusion.table_ref
  5.8 25.9 %add_convert_fusion.frames_ref = bf16[16,131072]{1,0:T(8,128)(2,1)} fusion(s32[16,134656]{1,0:T(8,128)} %param.6, f32[131072]{0:T(1024)S(1)} %bitcast.111, f32[131072]{0:T(1024)S(1)} %bitcast.112, f32[131072]{0:T(1024)S(1)} %bitcast.113, f32[131072]{0:T(1024)S(1)} %bitcast.114, f32[131072]{0:T(1024)S(1)} %bitcast.115, f32[131072]{0:T(1024)S(1)} %bitcast.116, ...), kind=kLoop, calls=%fused_computation.72 | loop fusion | flops 50331648 | bytes 75497472 | tf_op jit(solution)/shard_map/convert_element_type | solution.py:60
  31.7 7.3 %shard_map.59 = bf16[256,16,256]{2,1,0:T(8,128)(2,1)} custom-call(bf16[16,131072]{1,0:T(8,128)(2,1)} %add_convert_fusion.frames_ref, bf16[512,256]{1,0:T(8,128)(2,1)} %copy_bitcast_fusion.table_ref, f32[512,1]{1,0:T(8,128)} %broadcast_in_dim_tile.4.keep_ref), custom_call_target="tpu_custom_call" | custom-call | flops 1073741824 | bytes 6291456 | tf_op jit(solution)/shard_map/pallas_call | solution.py:65
  39.0 4.8 %copy.33 = bf16[256,16,256]{0,1,2:T(8,128)(2,1)} copy(bf16[256,16,256]{2,1,0:T(8,128)(2,1)} %shard_map.59) | data formatting | bytes 4194304 | tf_op jit(solution)/shard_map/pallas_call | solution.py:65
  43.8 5.5 %copy.34 = bf16[2,32,2,16,2,256]{5,4,3,0,2,1:T(2,128)(2,1)S(1)} copy(bf16[2,32,2,16,2,256]{5,3,0,2,1,4:T(8,128)(2,1)} %bitcast.100) | data formatting | bytes 4194304 | tf_op jit(solution)/shard_map/transpose | solution.py:193
  49.3 6.6 %broadcast_in_dim.115 = bf16[2,32,2,2,16,2,256]{6,5,4,0,3,2,1:T(2,128)(2,1)} broadcast(bf16[2,32,2,16,2,256]{5,4,3,0,2,1:T(2,128)(2,1)S(1)} %copy.34), dimensions={0,1,3,4,5,6} | broadcast | bytes 6291456 | tf_op jit(solution)/shard_map/broadcast_in_dim | solution.py:194
  55.9 7.6 %reshape.253 = bf16[2,128,16,512]{3,2,0,1:T(8,128)(2,1)} reshape(bf16[2,32,2,2,16,2,256]{6,5,4,0,3,2,1:T(2,128)(2,1)} %broadcast_in_dim.115) | data formatting | bytes 8388608 | tf_op jit(solution)/shard_map/reshape | solution.py:197
  63.5 12.0 %all-to-all-start = ((bf16[2,128,16,512]{3,2,0,1:T(8,128)(2,1)}), bf16[2,128,16,512]{3,2,0,1:T(8,128)(2,1)}, u32[]{:S(2)}, u32[]{:S(2)}) async-start(bf16[2,128,16,512]{3,2,0,1:T(8,128)(2,1)} %reshape.253), calls=%async_computation | async-start | bytes 8388608 | tf_op jit(solution)/shard_map/all_to_all | solution.py:198
  75.5 0.6 pad_add_fusion.1.block_ref
  76.1 0.7 pad_add_fusion.block_ref
  76.8 1.0 add_bitcast_fusion
  77.8 51.2 %all-to-all-done = bf16[2,128,16,512]{3,2,0,1:T(8,128)(2,1)} async-done(((bf16[2,128,16,512]{3,2,0,1:T(8,128)(2,1)}), bf16[2,128,16,512]{3,2,0,1:T(8,128)(2,1)}, u32[]{:S(2)}, u32[]{:S(2)}) %all-to-all-start) | async-done | bytes 4194336 | tf_op jit(solution)/shard_map/all_to_all | solution.py:198
  129.0 4.7 %copy.35 = bf16[2,128,16,512]{3,2,1,0:T(8,128)(2,1)} copy(bf16[2,128,16,512]{3,2,0,1:T(8,128)(2,1)} %all-to-all-done) | data formatting | bytes 8388608 | tf_op jit(solution)/shard_map/all_to_all | solution.py:198
  133.7 0.5 collective-permute-start
  134.2 1.7 dynamic-slice_bitcast_fusion
  136.0 25.2 %while.16 = (s32[]{:T(128)}, f32[2048]{0:T(1024)S(1)}, f32[2048]{0:T(1024)S(1)}, f32[2048]{0:T(1024)S(1)}, f32[2048]{0:T(1024)S(1)}, /*index=5*/bf16[2048,512]{1...) while((s32[]{:T(128)}, f32[2048]{0:T(1024)S(1)}, ...), condition=%wide.region_3.4_spmd.clone, body=%wide.region_0.3_spmd.clone.sunk | while | flops 50806272 | bytes 9220263 | solution.py:127
  136.0 0.6 add_reduce_fusion.4
  137.7 0.6 convolution_bitcast_fusion.9
  138.5 0.6 add_reduce_fusion.5
  140.3 0.6 convolution_bitcast_fusion.11
  141.0 0.6 add_reduce_fusion.4
  142.8 0.6 convolution_bitcast_fusion.9
  143.5 0.6 add_reduce_fusion.5
  144.9 0.4 convolution_bitcast_fusion.10
  145.3 0.6 convolution_bitcast_fusion.11
  146.0 0.6 add_reduce_fusion.4
  147.8 0.6 convolution_bitcast_fusion.9
  148.5 0.6 add_reduce_fusion.5
  149.9 0.4 convolution_bitcast_fusion.10
  150.3 0.6 convolution_bitcast_fusion.11
  151.1 0.6 add_reduce_fusion.4
  152.9 0.6 convolution_bitcast_fusion.9
  153.6 0.6 add_reduce_fusion.5
  154.9 0.4 convolution_bitcast_fusion.10
  155.4 0.6 convolution_bitcast_fusion.11
  156.1 0.6 add_reduce_fusion.4
  157.9 0.6 convolution_bitcast_fusion.9
  158.6 0.6 add_reduce_fusion.5
  160.0 0.4 convolution_bitcast_fusion.10
  160.4 0.6 convolution_bitcast_fusion.11
  161.3 0.8 copy.36
  162.1 4.5 %all-to-all-start.1 = ((f32[2,128,1,16]{3,2,0,1:T(1,128)}), f32[2,128,1,16]{3,2,0,1:T(1,128)S(1)}, u32[]{:S(2)}, u32[]{:S(2)}) async-start(f32[2,128,1,16]{3,2,0,1:T(1,128)} %copy.36), calls=%async_computation.1 | async-start | bytes 262144 | tf_op jit(solution)/shard_map/all_to_all | solution.py:219
  166.7 11.1 %shard_map.60.prev_ref = bf16[2,4,512,2048]{3,2,1,0:T(8,128)(2,1)} custom-call(s32[2]{0:T(128)} %pad_add_fusion.1.block_ref, bf16[2,2048,512]{2,1,0:T(8,128)(2,1)} %bitcast.4.rows_ref.cols_ref, bf16[2,2048,512]{2,1,0:T(8,128)(2,1)} %bitcast.4.rows_ref.cols_ref), custom_call_target="tpu_custom_call" | custom-call | flops 4294967296 | bytes 13631488 | tf_op jit(solution)/shard_map/pallas_call | solution.py:168
  177.9 0.7 copy.39
  178.6 11.1 %shard_map.61 = bf16[2,4,512,2048]{3,2,1,0:T(8,128)(2,1)} custom-call(s32[2]{0:T(128)} %pad_add_fusion.block_ref, bf16[2,2048,512]{2,1,0:T(8,128)(2,1)} %collective-permute-done.rows_ref.cols_ref, bf16[2,2048,512]{2,1,0:T(8,128)(2,1)} %collective-permute-done.rows_ref.cols_ref, ...), custom_call_target="tpu_custom_call", output_to_operand_aliasing={{}: (3, {})} | custom-call | flops 4294967296 | bytes 13631488 | tf_op jit(solution)/shard_map/pallas_call | solution.py:168
  (122 shorter events, 5.9 us)
Async XLA Ops:
  63.5 65.5 %all-to-all-start = ((bf16[2,128,16,512]{3,2,0,1:T(8,128)(2,1)}), bf16[2,128,16,512]{3,2,0,1:T(8,128)(2,1)}, u32[]{:S(2)}, u32[]{:S(2)}) async-start(bf16[2,128,16,512]{3,2,0,1:T(8,128)(2,1)} %reshape.253), calls=%async_computation | async-start | bytes 8388608 | tf_op jit(solution)/shard_map/all_to_all | solution.py:198
  133.7 44.9 %collective-permute-start = (bf16[2,2048,512]{2,1,0:T(8,128)(2,1)}, bf16[2,2048,512]{2,1,0:T(8,128)(2,1)}, u32[]{:S(2)}, u32[]{:S(2)}) collective-permute-start(bf16[2,2048,512]{2,1,0:T(8,128)(2,1)} %bitcast.4.rows_ref.cols_ref), channel_id=1, source_target_pairs={{0,1},{1,0},{2,3},{3,2},{4,5},{5,4},{6,7},{7,6},{8,9},{9,8},{10,11... | collective-permute-start | bytes 12582920 | tf_op jit(solution)/shard_map/ppermute | solution.py:204
  162.1 15.7 %all-to-all-start.1 = ((f32[2,128,1,16]{3,2,0,1:T(1,128)}), f32[2,128,1,16]{3,2,0,1:T(1,128)S(1)}, u32[]{:S(2)}, u32[]{:S(2)}) async-start(f32[2,128,1,16]{3,2,0,1:T(1,128)} %copy.36), calls=%async_computation.1 | async-start | bytes 262144 | tf_op jit(solution)/shard_map/all_to_all | solution.py:219

commit v6 on v4

--- a/solution.py
+++ b/solution.py
@@ -31,13 +31,17 @@
     return jnp.stack([jnp.cos(angle), -jnp.sin(angle)], axis=1).astype(jnp.bfloat16)
 
 
-def transform_kernel(keep_ref, table_ref, frames_ref, out_ref):
-    group = frames_ref.shape[0]
+def transform_kernel(keep_ref, window_ref, table_ref, samples_ref, out_ref, wide_ref):
+    group = samples_ref.shape[0]
     base = pl.program_id(0) * group
     scale = 1.0 / (64.0 * math.sqrt(FRAME))
     for item in range(group):
+        wide_ref[0 : SPECTRA + TAPS - 1, :] = samples_ref[item].astype(jnp.float32)
+        frames = window_ref[0:1, :] * wide_ref[0:SPECTRA, :]
+        for tap in range(1, TAPS):
+            frames = frames + window_ref[tap : tap + 1, :] * wide_ref[tap : tap + SPECTRA, :]
         result = lax.dot_general(
-            table_ref[...], frames_ref[item], (((1,), (1,)), ((), ())),
+            table_ref[...], frames.astype(jnp.bfloat16), (((1,), (1,)), ((), ())),
             preferred_element_type=jnp.float32,
         )
         result = result * (scale * keep_ref[base + item])
@@ -50,10 +54,6 @@
     table = transform_table()
     count = voltages.shape[0]
     samples = voltages.astype(jnp.bfloat16).reshape(count, SPECTRA + TAPS - 1, FRAME)
-    frames = window[0] * samples[:, 0:SPECTRA, :].astype(jnp.float32)
-    for tap in range(1, TAPS):
-        frames = frames + window[tap] * samples[:, tap : tap + SPECTRA, :].astype(jnp.float32)
-    frames = frames.astype(jnp.bfloat16)
     table_t = jnp.transpose(table.reshape(FRAME, 2 * CHANS))
     group = 8
     return pl.pallas_call(
@@ -61,17 +61,19 @@
         grid=(count // group,),
         in_specs=[
             pl.BlockSpec(memory_space=pltpu.SMEM),
+            pl.BlockSpec((TAPS, FRAME), lambda g: (0, 0)),
             pl.BlockSpec((2 * CHANS, FRAME), lambda g: (0, 0)),
-            pl.BlockSpec((group, SPECTRA, FRAME), lambda g: (g, 0, 0)),
+            pl.BlockSpec((group, SPECTRA + TAPS - 1, FRAME), lambda g: (g, 0, 0)),
         ],
         out_specs=pl.BlockSpec((CHANS, group, 2 * SPECTRA), lambda g: (0, g, 0)),
         out_shape=jax.ShapeDtypeStruct((CHANS, count, 2 * SPECTRA), jnp.bfloat16),
+        scratch_shapes=[pltpu.VMEM((SPECTRA + 2 * TAPS, FRAME), jnp.float32)],
         cost_estimate=pl.CostEstimate(
-            flops=2 * count * SPECTRA * FRAME * 2 * CHANS,
+            flops=2 * count * SPECTRA * FRAME * (2 * CHANS + TAPS),
             transcendentals=0,
-            bytes_accessed=2 * count * SPECTRA * FRAME + 2 * CHANS * count * 2 * SPECTRA,
+            bytes_accessed=2 * count * (SPECTRA + TAPS) * FRAME + 2 * CHANS * count * 2 * SPECTRA,
         ),
-    )(keep, table_t, frames)
+    )(keep, window, table_t, samples)
 
 
 def split3(value):

time: 175 us -> 161 us (0.920)
  other arithmetic: 41.3 us -> 19.2 us
  Pallas kernels: 28.7 us -> 37.1 us
    convert_element_type x1 -> x0, other arithmetic: 22.8 us -> none  [channelize(): frames = frames.astype(jnp.bfloat16)]
    pallas_call x1, Pallas kernels: 6.44 us -> 14.8 us  [channelize(): pl.pallas_call(transform_kernel, grid=(count // group,), in_specs=[pl.Blo...]
  transfers between devices with their start and end apart: 3 -> 3, of which waited for: 1 -> 1; matrix products, arithmetic and copies ran while one was open for 14% -> 15% of each run, Pallas kernels for 6% -> 7%
where the time goes in v6:
time: 161 us; the launch traced here: 160 us
  waiting for transfers between devices  51.3 us (32%)
  Pallas kernels  37.1 us (23%)
  other arithmetic  19.2 us (12%)
  local copies, waits for them, and re-layouts  17.4 us (11%)
  starting transfers between devices  17 us (11%)
  matrix products  10.1 us (6%)
  loops' own time  7.26 us (5%)
    all_to_all x1, waiting for transfers between devices, shards(): lax.all_to_all(send, ('chan', 'blk'), split_axis=1, concat_axis=1, tiled=...  51.3 us
    pallas_call x2, Pallas kernels, correlate(): pl.pallas_call(kernel, grid_spec=spec, out_shape=jax.ShapeDtypeStruct((2,...  22.3 us
    pallas_call x1, Pallas kernels, channelize(): pl.pallas_call(transform_kernel, grid=(count // group,), in_specs=[pl.Blo...  14.8 us
    all_to_all x1, starting transfers between devices, shards(): lax.all_to_all(send, ('chan', 'blk'), split_axis=1, concat_axis=1, tiled=...  12 us
    dot_general x20, matrix products, exact_dot(): lax.dot_general(lhs, split3(rhs_f32), (dims, ((), ())), preferred_element...  10.1 us
    another operation x1, loops' own time, solve_gains(): return lax.fori_loop(0, ITERS // 2, paired, (start_re, start_im))  7.26 us
    reduce_sum x10, other arithmetic, sweep(): power = jnp.sum(probe_re * probe_re + probe_im * probe_im)  6.12 us
    convert_element_type x1, other arithmetic, channelize(): voltages.astype(jnp.bfloat16).reshape(count, SPECTRA + TAPS - 1, FRAME)  5.3 us
  transfers between devices with their start and end apart: 3, of which 1 were waited for; matrix products, arithmetic and copies ran while one was open for 15% of the time, Pallas kernels for 7%

profile of v6, /device:TPU:1, one launch (start us, length us, event | category | flops | bytes accessed | tf_op | source)
XLA Modules:
  0.0 160.1 jit_solution(3933194895757415277)
XLA Ops:
  0.6 0.7 fusion.42.window_ref
  1.3 1.2 subtract_convert_fusion.4.keep_ref
  2.6 1.2 cosine_convert_fusion
  3.8 5.3 %convert_element_type.155 = bf16[16,134656]{1,0:T(8,128)(2,1)} convert(s32[16,134656]{1,0:T(8,128)} %param.6) | non-fusion elementwise | flops 2154496 | bytes 12926976 | tf_op jit(solution)/shard_map/convert_element_type | solution.py:56
  9.1 5.0 %reshape.213.samples_ref = bf16[16,263,512]{2,1,0:T(8,128)(2,1)} reshape(bf16[16,134656]{1,0:T(8,128)(2,1)} %convert_element_type.155) | data formatting | bytes 8617984 | tf_op jit(solution)/shard_map/reshape | solution.py:56
  14.1 0.7 pad_maximum_fusion.2
  14.9 14.8 %shard_map.59 = bf16[128,16,512]{2,1,0:T(8,128)(2,1)} custom-call(f32[16]{0:T(128)} %subtract_convert_fusion.4.keep_ref, f32[8,512]{1,0:T(8,128)} %fusion.42.window_ref, bf16[256,512]{1,0:T(8,128)(2,1)} %bitcast.91, bf16[16,263,512]{2,1,0:T(8,128)(2,1)} %reshape.213.samples_ref), custom_call_target="tpu_custom_call" | custom-call | flops 1107296256 | bytes 6422528 | tf_op jit(solution)/shard_map/pallas_call | solution.py:59
  29.7 4.2 %broadcast_in_dim.21 = bf16[32,2,2,2,16,512]{5,4,3,2,1,0:T(8,128)(2,1)} broadcast(bf16[32,2,2,16,512]{4,3,2,1,0:T(8,128)(2,1)} %bitcast.74), dimensions={0,2,3,4,5} | broadcast | bytes 6291456 | tf_op jit(solution)/shard_map/broadcast_in_dim | solution.py:189
  33.9 12.0 %all-to-all-start = ((bf16[2,128,16,512]{3,2,0,1:T(8,128)(2,1)}), bf16[2,128,16,512]{3,2,0,1:T(8,128)(2,1)}, u32[]{:S(2)}, u32[]{:S(2)}) async-start(bf16[2,128,16,512]{3,2,0,1:T(8,128)(2,1)} %bitcast.73), calls=%async_computation | async-start | bytes 8388608 | tf_op jit(solution)/shard_map/all_to_all | solution.py:194
  45.9 0.6 pad_add_fusion.1.block_ref
  46.5 0.6 pad_add_fusion.block_ref
  47.1 1.0 add_bitcast_fusion
  48.2 51.3 %all-to-all-done = bf16[2,128,16,512]{3,2,0,1:T(8,128)(2,1)} async-done(((bf16[2,128,16,512]{3,2,0,1:T(8,128)(2,1)}), bf16[2,128,16,512]{3,2,0,1:T(8,128)(2,1)}, u32[]{:S(2)}, u32[]{:S(2)}) %all-to-all-start) | async-done | bytes 4194336 | tf_op jit(solution)/shard_map/all_to_all | solution.py:194
  99.4 4.7 %copy.18 = bf16[2,128,16,512]{3,2,1,0:T(8,128)(2,1)} copy(bf16[2,128,16,512]{3,2,0,1:T(8,128)(2,1)} %all-to-all-done) | data formatting | bytes 8388608 | tf_op jit(solution)/shard_map/all_to_all | solution.py:194
  104.1 0.5 collective-permute-start
  104.6 1.7 %dynamic-slice_bitcast_fusion = bf16[2048,512]{1,0:T(8,128)(2,1)S(1)} fusion(bf16[2,2048,512]{2,1,0:T(8,128)(2,1)} %bitcast.7.rows_ref.cols_ref, s32[]{:T(128)S(6)} %select_n.75), kind=kLoop, calls=%fused_computation.72 | loop fusion | bytes 4194308 | tf_op jit(solution)/shard_map/jit(dynamic_index_in_dim)/squeeze | solution.py:207
  106.4 25.2 %while.16 = (s32[]{:T(128)}, f32[2048]{0:T(1024)S(1)}, f32[2048]{0:T(1024)S(1)}, f32[2048]{0:T(1024)S(1)}, f32[2048]{0:T(1024)S(1)}, /*index=5*/bf16[2048,512]{1...) while((s32[]{:T(128)}, f32[2048]{0:T(1024)S(1)}, ...), condition=%wide.region_3.4_spmd.clone, body=%wide.region_0.3_spmd.clone.sunk | while | flops 50806272 | bytes 9220263 | solution.py:123
  106.4 0.6 add_reduce_fusion.4
  107.7 0.4 convolution_bitcast_fusion.8
  108.1 0.6 convolution_bitcast_fusion.9
  108.9 0.6 add_reduce_fusion.5
  110.2 0.4 convolution_bitcast_fusion.10
  110.7 0.6 convolution_bitcast_fusion.11
  111.4 0.6 add_reduce_fusion.4
  113.2 0.6 convolution_bitcast_fusion.9
  113.9 0.6 add_reduce_fusion.5
  115.3 0.4 convolution_bitcast_fusion.10
  115.7 0.6 convolution_bitcast_fusion.11
  116.5 0.6 add_reduce_fusion.4
  118.2 0.6 convolution_bitcast_fusion.9
  119.0 0.6 add_reduce_fusion.5
  120.3 0.4 convolution_bitcast_fusion.10
  120.8 0.6 convolution_bitcast_fusion.11
  121.5 0.6 add_reduce_fusion.4
  123.3 0.6 convolution_bitcast_fusion.9
  124.0 0.6 add_reduce_fusion.5
  125.3 0.4 convolution_bitcast_fusion.10
  125.8 0.6 convolution_bitcast_fusion.11
  126.5 0.6 add_reduce_fusion.4
  128.3 0.6 convolution_bitcast_fusion.9
  129.0 0.6 add_reduce_fusion.5
  130.4 0.4 convolution_bitcast_fusion.10
  130.8 0.6 convolution_bitcast_fusion.11
  131.8 0.8 copy.19
  132.5 4.5 %all-to-all-start.1 = ((f32[2,128,1,16]{3,2,0,1:T(1,128)}), f32[2,128,1,16]{3,2,0,1:T(1,128)S(1)}, u32[]{:S(2)}, u32[]{:S(2)}) async-start(f32[2,128,1,16]{3,2,0,1:T(1,128)} %copy.19), calls=%async_computation.1 | async-start | bytes 262144 | tf_op jit(solution)/shard_map/all_to_all | solution.py:215
  137.1 11.1 %shard_map.60.prev_ref = bf16[2,4,512,2048]{3,2,1,0:T(8,128)(2,1)} custom-call(s32[2]{0:T(128)} %pad_add_fusion.1.block_ref, bf16[2,2048,512]{2,1,0:T(8,128)(2,1)} %bitcast.7.rows_ref.cols_ref, bf16[2,2048,512]{2,1,0:T(8,128)(2,1)} %bitcast.7.rows_ref.cols_ref), custom_call_target="tpu_custom_call" | custom-call | flops 4294967296 | bytes 13631488 | tf_op jit(solution)/shard_map/pallas_call | solution.py:164
  148.3 0.7 copy.22
  149.0 11.1 %shard_map.61 = bf16[2,4,512,2048]{3,2,1,0:T(8,128)(2,1)} custom-call(s32[2]{0:T(128)} %pad_add_fusion.block_ref, bf16[2,2048,512]{2,1,0:T(8,128)(2,1)} %collective-permute-done.rows_ref.cols_ref, bf16[2,2048,512]{2,1,0:T(8,128)(2,1)} %collective-permute-done.rows_ref.cols_ref, ...), custom_call_target="tpu_custom_call", output_to_operand_aliasing={{}: (3, {})} | custom-call | flops 4294967296 | bytes 13631488 | tf_op jit(solution)/shard_map/pallas_call | solution.py:164
  (105 shorter events, 3.4 us)
Async XLA Ops:
  33.9 65.5 %all-to-all-start = ((bf16[2,128,16,512]{3,2,0,1:T(8,128)(2,1)}), bf16[2,128,16,512]{3,2,0,1:T(8,128)(2,1)}, u32[]{:S(2)}, u32[]{:S(2)}) async-start(bf16[2,128,16,512]{3,2,0,1:T(8,128)(2,1)} %bitcast.73), calls=%async_computation | async-start | bytes 8388608 | tf_op jit(solution)/shard_map/all_to_all | solution.py:194
  104.1 44.9 %collective-permute-start = (bf16[2,2048,512]{2,1,0:T(8,128)(2,1)}, bf16[2,2048,512]{2,1,0:T(8,128)(2,1)}, u32[]{:S(2)}, u32[]{:S(2)}) collective-permute-start(bf16[2,2048,512]{2,1,0:T(8,128)(2,1)} %bitcast.7.rows_ref.cols_ref), channel_id=1, source_target_pairs={{0,1},{1,0},{2,3},{3,2},{4,5},{5,4},{6,7},{7,6},{8,9},{9,8},{10,11... | collective-permute-start | bytes 12582920 | tf_op jit(solution)/shard_map/ppermute | solution.py:200
  132.5 15.7 %all-to-all-start.1 = ((f32[2,128,1,16]{3,2,0,1:T(1,128)}), f32[2,128,1,16]{3,2,0,1:T(1,128)S(1)}, u32[]{:S(2)}, u32[]{:S(2)}) async-start(f32[2,128,1,16]{3,2,0,1:T(1,128)} %copy.19), calls=%async_computation.1 | async-start | bytes 262144 | tf_op jit(solution)/shard_map/all_to_all | solution.py:215

commit v7 on v6

--- a/solution.py
+++ b/solution.py
@@ -181,17 +181,26 @@
 def shards(voltages, flags, model_amp, model_phase):
     keep = (1 - flags).astype(jnp.float32)
     input_count = voltages.shape[0]
-    spectra = channelize(voltages, keep)
     blk_count = lax.axis_size("blk")
     chan_count = lax.axis_size("chan")
     block_index = lax.axis_index("blk")
-    spectra = spectra.reshape(chan_count, 2, 2, input_count, 2 * SPECTRA)
-    send = jnp.broadcast_to(
-        spectra[:, None], (chan_count, 2, 2, 2, input_count, 2 * SPECTRA)
-    )
-    send = send.reshape(chan_count * blk_count, 2, input_count, 2 * SPECTRA)
-    send = jnp.swapaxes(send, 0, 1)
-    got = lax.all_to_all(send, ("chan", "blk"), split_axis=1, concat_axis=1, tiled=True)
+    pieces = 2
+    part = input_count // pieces
+    received = []
+    for piece in range(pieces):
+        spectra = channelize(
+            voltages[piece * part : (piece + 1) * part], keep[piece * part : (piece + 1) * part]
+        )
+        spectra = spectra.reshape(chan_count, 2, 2, part, 2 * SPECTRA)
+        send = jnp.broadcast_to(
+            spectra[:, None], (chan_count, 2, 2, 2, part, 2 * SPECTRA)
+        )
+        send = send.reshape(chan_count * blk_count, 2, part, 2 * SPECTRA)
+        send = jnp.swapaxes(send, 0, 1)
+        received.append(
+            lax.all_to_all(send, ("chan", "blk"), split_axis=1, concat_axis=1, tiled=True)
+        )
+    got = jnp.concatenate(received, axis=2)
     mine = got.reshape(2, -1, 2 * SPECTRA)
     all_inputs = mine.shape[1]
     row_count = all_inputs // blk_count

time: 161 us -> 162 us (level)
  waiting for transfers between devices: 51.3 us -> 46.1 us
  starting transfers between devices: 17 us -> 21.8 us
  Pallas kernels: 37.1 us -> 39.8 us
    convert_element_type x1 -> x0, other arithmetic: 5.3 us -> none  [channelize(): voltages.astype(jnp.bfloat16).reshape(count, SPECTRA + TAPS - 1, FRAME)]
    all_to_all x1 -> x2, waiting for transfers between devices: 51.3 us -> 46.1 us  [shards(): lax.all_to_all(send, ('chan', 'blk'), split_axis=1, concat_axis=1, tiled=...]
    all_to_all x1 -> x2, starting transfers between devices: 12 us -> 16.8 us  [shards(): lax.all_to_all(send, ('chan', 'blk'), split_axis=1, concat_axis=1, tiled=...]
    all_to_all x1 -> x0, local copies, waits for them, and re-layouts: 4.67 us -> none  [shards(): lax.all_to_all(send, ('chan', 'blk'), split_axis=1, concat_axis=1, tiled=...]
    another operation x2, other arithmetic: 1.83 us -> 5 us
    pallas_call x1 -> x2, Pallas kernels: 14.8 us -> 17.5 us  [channelize(): pl.pallas_call(transform_kernel, grid=(count // group,), in_specs=[pl.Blo...]
    concatenate x0 -> x1, local copies, waits for them, and re-layouts: none -> 2.44 us  [shards(): got = jnp.concatenate(received, axis=2)]
    concatenate x0 -> x1, other arithmetic: none -> 2.12 us  [shards(): got = jnp.concatenate(received, axis=2)]
  transfers between devices with their start and end apart: 3 -> 4, of which waited for: 1 -> 2; matrix products, arithmetic and copies ran while one was open for 15% -> 16% of each run, Pallas kernels for 7% -> 12%
where the time goes in v7:
time: 162 us; the launch traced here: 161 us
  waiting for transfers between devices  46.1 us (28%)
  Pallas kernels  39.8 us (25%)
  starting transfers between devices  21.8 us (13%)
  other arithmetic  18.1 us (11%)
  local copies, waits for them, and re-layouts  17.3 us (11%)
  matrix products  10.1 us (6%)
  loops' own time  7.26 us (4%)
    all_to_all x2, waiting for transfers between devices, shards(): lax.all_to_all(send, ('chan', 'blk'), split_axis=1, concat_axis=1, tiled=...  46.1 us
    pallas_call x2, Pallas kernels, correlate(): pl.pallas_call(kernel, grid_spec=spec, out_shape=jax.ShapeDtypeStruct((2,...  22.3 us
    pallas_call x2, Pallas kernels, channelize(): pl.pallas_call(transform_kernel, grid=(count // group,), in_specs=[pl.Blo...  17.5 us
    all_to_all x2, starting transfers between devices, shards(): lax.all_to_all(send, ('chan', 'blk'), split_axis=1, concat_axis=1, tiled=...  16.8 us
    dot_general x20, matrix products, exact_dot(): lax.dot_general(lhs, split3(rhs_f32), (dims, ((), ())), preferred_element...  10.1 us
    another operation x1, loops' own time, solve_gains(): return lax.fori_loop(0, ITERS // 2, paired, (start_re, start_im))  7.26 us
    reduce_sum x10, other arithmetic, sweep(): power = jnp.sum(probe_re * probe_re + probe_im * probe_im)  6.12 us
    broadcast_in_dim x2, local copies, waits for them, and re-layouts, shards(): jnp.broadcast_to(spectra[:, None], (chan_count, 2, 2, 2, part, 2 * SPECTRA))  5.66 us
  transfers between devices with their start and end apart: 4, of which 2 were waited for; matrix products, arithmetic and copies ran while one was open for 16% of the time, Pallas kernels for 12%

profile of v7, /device:TPU:1, one launch (start us, length us, event | category | flops | bytes accessed | tf_op | source)
XLA Modules:
  0.0 161.3 jit_solution(10667289939065460886)
XLA Ops:
  0.7 0.7 subtract_convert_fusion.4
  1.4 0.6 fusion.73
  2.1 0.6 reshape.224.window_ref
  2.7 1.2 cosine_convert_fusion
  3.9 3.8 %convert.12 = bf16[16,134656]{1,0:T(8,128)(2,1)S(1)} convert(s32[16,134656]{1,0:T(8,128)} %param.7) | non-fusion elementwise | flops 2154496 | bytes 12926976 | tf_op jit(solution)/shard_map/convert.1
  8.0 2.1 %copy.24.samples_ref = bf16[8,263,512]{2,1,0:T(8,128)(2,1)} copy(bf16[8,263,512]{2,0,1:T(8,128)(2,1)S(1)} %bitcast.80) | data formatting | bytes 4308992 | tf_op jit(solution)/shard_map/reshape | solution.py:56
  10.1 0.8 pad_maximum_fusion.3
  10.8 8.8 %shard_map.59 = bf16[128,8,512]{2,1,0:T(8,128)(2,1)} custom-call(f32[8]{0:T(128)} %get-tuple-element.210.keep_ref, f32[8,512]{1,0:T(8,128)} %reshape.224.window_ref, bf16[256,512]{1,0:T(8,128)(2,1)} %bitcast.92, bf16[8,263,512]{2,1,0:T(8,128)(2,1)} %copy.24.samples_ref), custom_call_target="tpu_custom_call" | custom-call | flops 553648128 | bytes 3211264 | tf_op jit(solution)/shard_map/pallas_call | solution.py:59
  19.6 2.8 %broadcast_in_dim.28 = bf16[32,2,2,2,8,512]{5,4,3,2,1,0:T(8,128)(2,1)} broadcast(bf16[32,2,2,8,512]{4,3,2,1,0:T(8,128)(2,1)} %bitcast.91), dimensions={0,2,3,4,5} | broadcast | bytes 3145728 | tf_op jit(solution)/shard_map/broadcast_in_dim | solution.py:195
  22.4 12.0 %all-to-all-start = ((bf16[2,128,8,512]{3,2,0,1:T(8,128)(2,1)}), bf16[2,128,8,512]{3,2,0,1:T(8,128)(2,1)}, u32[]{:S(2)}, u32[]{:S(2)}) async-start(bf16[2,128,8,512]{3,2,0,1:T(8,128)(2,1)} %bitcast.81), calls=%async_computation | async-start | bytes 4194304 | tf_op jit(solution)/shard_map/all_to_all | solution.py:201
  34.4 2.1 %copy.25.samples_ref = bf16[8,263,512]{2,1,0:T(8,128)(2,1)} copy(bf16[8,263,512]{2,0,1:T(8,128)(2,1)S(1)} %bitcast.79) | data formatting | bytes 4308992 | tf_op jit(solution)/shard_map/reshape | solution.py:56
  36.5 8.8 %shard_map.60 = bf16[128,8,512]{2,1,0:T(8,128)(2,1)} custom-call(f32[8]{0:T(128)} %get-tuple-element.211.keep_ref, f32[8,512]{1,0:T(8,128)} %reshape.224.window_ref, bf16[256,512]{1,0:T(8,128)(2,1)} %bitcast.93, bf16[8,263,512]{2,1,0:T(8,128)(2,1)} %copy.25.samples_ref), custom_call_target="tpu_custom_call" | custom-call | flops 553648128 | bytes 3211264 | tf_op jit(solution)/shard_map/pallas_call | solution.py:59
  45.2 18.3 %all-to-all-done = bf16[2,128,8,512]{3,2,0,1:T(8,128)(2,1)} async-done(((bf16[2,128,8,512]{3,2,0,1:T(8,128)(2,1)}), bf16[2,128,8,512]{3,2,0,1:T(8,128)(2,1)}, u32[]{:S(2)}, u32[]{:S(2)}) %all-to-all-start) | async-done | bytes 2097184 | tf_op jit(solution)/shard_map/all_to_all | solution.py:201
  63.6 2.8 %broadcast_in_dim.30 = bf16[32,2,2,2,8,512]{5,4,3,2,1,0:T(8,128)(2,1)} broadcast(bf16[32,2,2,8,512]{4,3,2,1,0:T(8,128)(2,1)} %bitcast.90), dimensions={0,2,3,4,5} | broadcast | bytes 3145728 | tf_op jit(solution)/shard_map/broadcast_in_dim | solution.py:195
  66.4 4.9 %all-to-all-start.1 = ((bf16[2,128,8,512]{3,2,0,1:T(8,128)(2,1)}), bf16[2,128,8,512]{3,2,0,1:T(8,128)(2,1)S(1)}, u32[]{:S(2)}, u32[]{:S(2)}) async-start(bf16[2,128,8,512]{3,2,0,1:T(8,128)(2,1)} %bitcast.12), calls=%async_computation.1 | async-start | bytes 4194304 | tf_op jit(solution)/shard_map/all_to_all | solution.py:201
  71.3 0.7 pad_add_fusion
  72.0 1.0 add_bitcast_fusion
  73.0 27.7 %all-to-all-done.1 = bf16[2,128,8,512]{3,2,0,1:T(8,128)(2,1)S(1)} async-done(((bf16[2,128,8,512]{3,2,0,1:T(8,128)(2,1)}), bf16[2,128,8,512]{3,2,0,1:T(8,128)(2,1)S(1)}, u32[]{:S(2)}, u32[]{:S(2)}) %all-to-all-start.1) | async-done | bytes 2097184 | tf_op jit(solution)/shard_map/all_to_all | solution.py:201
  100.8 2.1 %pad_maximum_fusion.2 = bf16[2,128,16,512]{3,2,0,1:T(8,128)(2,1)S(1)} fusion(bf16[2,128,8,512]{3,2,0,1:T(8,128)(2,1)S(1)} %all-to-all-done.1, bf16[2,128,8,512]{3,2,0,1:T(8,128)(2,1)} %all-to-all-done), kind=kLoop, calls=%fused_computation.72 | loop fusion | flops 8388608 | bytes 8388608 | tf_op jit(solution)/shard_map/concatenate | solution.py:203
  102.9 2.4 %copy.26 = bf16[2,128,16,512]{3,2,1,0:T(8,128)(2,1)} copy(bf16[2,128,16,512]{3,2,0,1:T(8,128)(2,1)S(1)} %pad_maximum_fusion.2) | data formatting | bytes 8388608 | tf_op jit(solution)/shard_map/concatenate | solution.py:203
  105.3 1.3 collective-permute-start
  106.6 1.7 %dynamic-slice_bitcast_fusion = bf16[2048,512]{1,0:T(8,128)(2,1)S(1)} fusion(bf16[2,2048,512]{2,1,0:T(8,128)(2,1)} %bitcast.13.rows_ref.cols_ref, s32[]{:T(128)S(6)} %select_n.62), kind=kLoop, calls=%fused_computation.73 | loop fusion | bytes 4194308 | tf_op jit(solution)/shard_map/jit(dynamic_index_in_dim)/squeeze | solution.py:216
  108.3 25.2 %while.16 = (s32[]{:T(128)}, f32[2048]{0:T(1024)S(1)}, f32[2048]{0:T(1024)S(1)}, f32[2048]{0:T(1024)S(1)}, f32[2048]{0:T(1024)S(1)}, /*index=5*/bf16[2048,512]{1...) while((s32[]{:T(128)}, f32[2048]{0:T(1024)S(1)}, ...), condition=%wide.region_3.5_spmd.clone, body=%wide.region_0.4_spmd.clone.sunk | while | flops 50806272 | bytes 9220263 | solution.py:123
  108.3 0.6 add_reduce_fusion.4
  110.1 0.6 convolution_bitcast_fusion.9
  110.8 0.6 add_reduce_fusion.5
  112.6 0.6 convolution_bitcast_fusion.11
  113.4 0.6 add_reduce_fusion.4
  115.1 0.6 convolution_bitcast_fusion.9
  115.9 0.6 add_reduce_fusion.5
  117.7 0.6 convolution_bitcast_fusion.11
  118.4 0.6 add_reduce_fusion.4
  120.2 0.6 convolution_bitcast_fusion.9
  120.9 0.6 add_reduce_fusion.5
  122.7 0.6 convolution_bitcast_fusion.11
  123.5 0.6 add_reduce_fusion.4
  125.2 0.6 convolution_bitcast_fusion.9
  126.0 0.6 add_reduce_fusion.5
  127.8 0.6 convolution_bitcast_fusion.11
  128.5 0.6 add_reduce_fusion.4
  130.3 0.6 convolution_bitcast_fusion.9
  131.0 0.6 add_reduce_fusion.5
  132.8 0.6 convolution_bitcast_fusion.11
  133.7 0.8 copy.27
  134.5 3.7 %all-to-all-start.2 = ((f32[2,128,1,16]{3,2,0,1:T(1,128)}), f32[2,128,1,16]{3,2,0,1:T(1,128)S(1)}, u32[]{:S(2)}, u32[]{:S(2)}) async-start(f32[2,128,1,16]{3,2,0,1:T(1,128)} %copy.27), calls=%async_computation.2 | async-start | bytes 262144 | tf_op jit(solution)/shard_map/all_to_all | solution.py:224
  138.2 11.1 %shard_map.61.prev_ref = bf16[2,4,512,2048]{3,2,1,0:T(8,128)(2,1)} custom-call(s32[2]{0:T(128)} %get-tuple-element.215.block_ref, bf16[2,2048,512]{2,1,0:T(8,128)(2,1)} %bitcast.13.rows_ref.cols_ref, bf16[2,2048,512]{2,1,0:T(8,128)(2,1)} %bitcast.13.rows_ref.cols_ref), custom_call_target="tpu_custom_call" | custom-call | flops 4294967296 | bytes 13631488 | tf_op jit(solution)/shard_map/pallas_call | solution.py:164
  149.4 0.7 copy.30
  150.1 11.1 %shard_map.62 = bf16[2,4,512,2048]{3,2,1,0:T(8,128)(2,1)} custom-call(s32[2]{0:T(128)} %get-tuple-element.214.block_ref, bf16[2,2048,512]{2,1,0:T(8,128)(2,1)} %collective-permute-done.rows_ref.cols_ref, bf16[2,2048,512]{2,1,0:T(8,128)(2,1)} %collective-permute-done.rows_ref.cols_ref, ...), custom_call_target="tpu_custom_call", output_to_operand_aliasing={{}: (3, {})} | custom-call | flops 4294967296 | bytes 13631488 | tf_op jit(solution)/shard_map/pallas_call | solution.py:164
  (113 shorter events, 6.1 us)
Async XLA Ops:
  22.4 41.1 %all-to-all-start = ((bf16[2,128,8,512]{3,2,0,1:T(8,128)(2,1)}), bf16[2,128,8,512]{3,2,0,1:T(8,128)(2,1)}, u32[]{:S(2)}, u32[]{:S(2)}) async-start(bf16[2,128,8,512]{3,2,0,1:T(8,128)(2,1)} %bitcast.81), calls=%async_computation | async-start | bytes 4194304 | tf_op jit(solution)/shard_map/all_to_all | solution.py:201
  66.4 34.4 %all-to-all-start.1 = ((bf16[2,128,8,512]{3,2,0,1:T(8,128)(2,1)}), bf16[2,128,8,512]{3,2,0,1:T(8,128)(2,1)S(1)}, u32[]{:S(2)}, u32[]{:S(2)}) async-start(bf16[2,128,8,512]{3,2,0,1:T(8,128)(2,1)} %bitcast.12), calls=%async_computation.1 | async-start | bytes 4194304 | tf_op jit(solution)/shard_map/all_to_all | solution.py:201
  105.3 44.8 %collective-permute-start = (bf16[2,2048,512]{2,1,0:T(8,128)(2,1)}, bf16[2,2048,512]{2,1,0:T(8,128)(2,1)}, u32[]{:S(2)}, u32[]{:S(2)}) collective-permute-start(bf16[2,2048,512]{2,1,0:T(8,128)(2,1)} %bitcast.13.rows_ref.cols_ref), channel_id=1, source_target_pairs={{0,1},{1,0},{2,3},{3,2},{4,5},{5,4},{6,7},{7,6},{8,9},{9,8},{10,11... | collective-permute-start | bytes 12582920 | tf_op jit(solution)/shard_map/ppermute | solution.py:209
  134.5 14.9 %all-to-all-start.2 = ((f32[2,128,1,16]{3,2,0,1:T(1,128)}), f32[2,128,1,16]{3,2,0,1:T(1,128)S(1)}, u32[]{:S(2)}, u32[]{:S(2)}) async-start(f32[2,128,1,16]{3,2,0,1:T(1,128)} %copy.27), calls=%async_computation.2 | async-start | bytes 262144 | tf_op jit(solution)/shard_map/all_to_all | solution.py:224

commit v8 on v6

--- a/solution.py
+++ b/solution.py
@@ -123,29 +123,37 @@
     return lax.fori_loop(0, ITERS // 2, paired, (start_re, start_im))
 
 
-def correlate_kernel(block_ref, rows_ref, cols_ref, out_ref):
+def correlate_kernel(block_ref, rows_ref, cols_ref, out_ref, turned_ref):
+    width = rows_ref.shape[-1]
+    rows = rows_ref[:, 0].reshape(-1, width)
+
+    @pl.when(pl.program_id(1) == 0)
+    def _():
+        turned_ref[:, :SPECTRA] = rows[:, SPECTRA:]
+        turned_ref[:, SPECTRA:] = -rows[:, :SPECTRA]
+
+    cols = cols_ref[:, 0].reshape(-1, width)
     dims = (((1,), (1,)), ((), ()))
-    rows_re = rows_ref[0, :, :SPECTRA]
-    rows_im = rows_ref[0, :, SPECTRA:]
-    cols_re = cols_ref[0, :, :SPECTRA]
-    cols_im = cols_ref[0, :, SPECTRA:]
-
-    def dot(a, b):
-        return lax.dot_general(a, b, dims, preferred_element_type=jnp.float32)
-
-    real = dot(rows_re, cols_re) + dot(rows_im, cols_im)
-    imag = dot(rows_im, cols_re) - dot(rows_re, cols_im)
+    real = lax.dot_general(rows, cols, dims, preferred_element_type=jnp.float32)
+    imag = lax.dot_general(turned_ref[...], cols, dims, preferred_element_type=jnp.float32)
     out_ref[0, 0] = (real * (1.0 / SPECTRA)).astype(out_ref.dtype)
     out_ref[1, 0] = (imag * (1.0 / SPECTRA)).astype(out_ref.dtype)
 
 
+def correlate_into_kernel(block_ref, rows_ref, cols_ref, prev_ref, out_ref, turned_ref):
+    correlate_kernel(block_ref, rows_ref, cols_ref, out_ref, turned_ref)
+
+
 def correlate(data, scalars, row_count, out=None, total_chans=None, col_block=512):
-    chans, inputs, width = data.shape
+    devices, chans, per, width = data.shape
+    inputs = devices * per
     total_chans = chans if total_chans is None else total_chans
     grid = (chans, inputs // col_block)
+    row_devices = row_count // per
+    col_devices = col_block // per
     in_specs = [
-        pl.BlockSpec((1, row_count, width), lambda c, j, s: (c, s[0], 0)),
-        pl.BlockSpec((1, col_block, width), lambda c, j, s: (c, j, 0)),
+        pl.BlockSpec((row_devices, 1, per, width), lambda c, j, s: (s[0], c, 0, 0)),
+        pl.BlockSpec((col_devices, 1, per, width), lambda c, j, s: (j, c, 0, 0)),
     ]
     operands = [scalars, data, data]
     aliases = {}
@@ -158,6 +166,7 @@
         grid=grid,
         in_specs=in_specs,
         out_specs=pl.BlockSpec((2, 1, row_count, col_block), lambda c, j, s: (0, s[1] + c, 0, j)),
+        scratch_shapes=[pltpu.VMEM((row_count, width), data.dtype)],
     )
     flops = 8 * chans * row_count * inputs * (width // 2)
     kernel = correlate_kernel if out is None else correlate_into_kernel
@@ -174,10 +183,6 @@
     )(*operands)
 
 
-def correlate_into_kernel(block_ref, rows_ref, cols_ref, prev_ref, out_ref):
-    correlate_kernel(block_ref, rows_ref, cols_ref, out_ref)
-
-
 def shards(voltages, flags, model_amp, model_phase):
     keep = (1 - flags).astype(jnp.float32)
     input_count = voltages.shape[0]
@@ -190,10 +195,8 @@
         spectra[:, None], (chan_count, 2, 2, 2, input_count, 2 * SPECTRA)
     )
     send = send.reshape(chan_count * blk_count, 2, input_count, 2 * SPECTRA)
-    send = jnp.swapaxes(send, 0, 1)
-    got = lax.all_to_all(send, ("chan", "blk"), split_axis=1, concat_axis=1, tiled=True)
-    mine = got.reshape(2, -1, 2 * SPECTRA)
-    all_inputs = mine.shape[1]
+    mine = lax.all_to_all(send, ("chan", "blk"), split_axis=0, concat_axis=0, tiled=True)
+    all_inputs = mine.shape[0] * input_count
     row_count = all_inputs // blk_count
     core = block_index % 2
     level = block_index // 2
@@ -204,7 +207,7 @@
     visibility = correlate(mine, first, row_count, total_chans=local_chans)
     visibility = correlate(theirs, second, row_count, out=visibility, total_chans=local_chans)
 
-    data = lax.dynamic_index_in_dim(mine, level, 0, keepdims=False)
+    data = lax.dynamic_index_in_dim(mine, level, 1, keepdims=False).reshape(all_inputs, -1)
     solve = 2 * core + level
     amp = lax.dynamic_index_in_dim(model_amp, solve, 0, keepdims=False)
     phase = lax.dynamic_index_in_dim(model_phase, solve, 0, keepdims=False)

time: 161 us -> 157 us (0.975)
  local copies, waits for them, and re-layouts: 17.4 us -> 12.8 us
    all_to_all x1 -> x0, local copies, waits for them, and re-layouts: 4.67 us -> none  [shards(): lax.all_to_all(send, ('chan', 'blk'), split_axis=1, concat_axis=1, tiled=...]
    dynamic_slice x0 -> x1, local copies, waits for them, and re-layouts: none -> 1.78 us  [shards(): lax.dynamic_index_in_dim(mine, level, 1, keepdims=False)]
    squeeze x1 -> x0, local copies, waits for them, and re-layouts: 1.73 us -> none  [shards(): data = lax.dynamic_index_in_dim(mine, level, 0, keepdims=False)]
where the time goes in v8:
time: 157 us; the launch traced here: 156 us
  waiting for transfers between devices  51.8 us (33%)
  Pallas kernels  37.6 us (24%)
  other arithmetic  18.6 us (12%)
  starting transfers between devices  17 us (11%)
  local copies, waits for them, and re-layouts  12.8 us (8%)
  matrix products  10.1 us (6%)
  loops' own time  7.26 us (5%)
    all_to_all x1, waiting for transfers between devices, shards(): lax.all_to_all(send, ('chan', 'blk'), split_axis=0, concat_axis=0, tiled=...  51.8 us
    pallas_call x2, Pallas kernels, correlate(): pl.pallas_call(kernel, grid_spec=spec, out_shape=jax.ShapeDtypeStruct((2,...  22.8 us
    pallas_call x1, Pallas kernels, channelize(): pl.pallas_call(transform_kernel, grid=(count // group,), in_specs=[pl.Blo...  14.8 us
    all_to_all x1, starting transfers between devices, shards(): lax.all_to_all(send, ('chan', 'blk'), split_axis=0, concat_axis=0, tiled=...  12 us
    dot_general x20, matrix products, exact_dot(): lax.dot_general(lhs, split3(rhs_f32), (dims, ((), ())), preferred_element...  10.1 us
    another operation x1, loops' own time, solve_gains(): return lax.fori_loop(0, ITERS // 2, paired, (start_re, start_im))  7.26 us
    reduce_sum x10, other arithmetic, sweep(): power = jnp.sum(probe_re * probe_re + probe_im * probe_im)  6.12 us
    convert_element_type x1, other arithmetic, channelize(): voltages.astype(jnp.bfloat16).reshape(count, SPECTRA + TAPS - 1, FRAME)  5.29 us
  transfers between devices with their start and end apart: 3, of which 1 were waited for; matrix products, arithmetic and copies ran while one was open for 15% of the time, Pallas kernels for 7%

profile of v8, /device:TPU:1, one launch (start us, length us, event | category | flops | bytes accessed | tf_op | source)
XLA Modules:
  0.0 156.0 jit_solution(13684086154211988654)
XLA Ops:
  0.6 0.7 fusion.42.window_ref
  1.3 1.3 subtract_convert_fusion.4.keep_ref
  2.6 1.2 cosine_convert_fusion
  3.8 5.3 %convert_element_type.155 = bf16[16,134656]{1,0:T(8,128)(2,1)} convert(s32[16,134656]{1,0:T(8,128)} %param.6) | non-fusion elementwise | flops 2154496 | bytes 12926976 | tf_op jit(solution)/shard_map/convert_element_type | solution.py:56
  9.1 5.0 %reshape.214.samples_ref = bf16[16,263,512]{2,1,0:T(8,128)(2,1)} reshape(bf16[16,134656]{1,0:T(8,128)(2,1)} %convert_element_type.155) | data formatting | bytes 8617984 | tf_op jit(solution)/shard_map/reshape | solution.py:56
  14.2 0.7 pad_maximum_fusion.2
  14.9 14.8 %shard_map.59 = bf16[128,16,512]{2,1,0:T(8,128)(2,1)} custom-call(f32[16]{0:T(128)} %subtract_convert_fusion.4.keep_ref, f32[8,512]{1,0:T(8,128)} %fusion.42.window_ref, bf16[256,512]{1,0:T(8,128)(2,1)} %bitcast.88, bf16[16,263,512]{2,1,0:T(8,128)(2,1)} %reshape.214.samples_ref), custom_call_target="tpu_custom_call" | custom-call | flops 1107296256 | bytes 6422528 | tf_op jit(solution)/shard_map/pallas_call | solution.py:59
  29.7 4.2 %broadcast_in_dim.21 = bf16[32,2,2,2,16,512]{5,4,3,2,1,0:T(8,128)(2,1)} broadcast(bf16[32,2,2,16,512]{4,3,2,1,0:T(8,128)(2,1)} %bitcast.71), dimensions={0,2,3,4,5} | broadcast | bytes 6291456 | tf_op jit(solution)/shard_map/broadcast_in_dim | solution.py:194
  33.9 12.0 %all-to-all-start = ((bf16[128,2,16,512]{3,2,1,0:T(8,128)(2,1)}), bf16[128,2,16,512]{3,2,1,0:T(8,128)(2,1)}, u32[]{:S(2)}, u32[]{:S(2)}) async-start(bf16[128,2,16,512]{3,2,1,0:T(8,128)(2,1)} %bitcast.70), calls=%async_computation | async-start | bytes 8388608 | tf_op jit(solution)/shard_map/all_to_all | solution.py:198
  45.9 0.6 pad_add_fusion
  46.6 1.0 add_bitcast_fusion
  47.6 51.8 %all-to-all-done.rows_ref.cols_ref = bf16[128,2,16,512]{3,2,1,0:T(8,128)(2,1)} async-done(((bf16[128,2,16,512]{3,2,1,0:T(8,128)(2,1)}), bf16[128,2,16,512]{3,2,1,0:T(8,128)(2,1)}, u32[]{:S(2)}, u32[]{:S(2)}) %all-to-all-start) | async-done | bytes 4194336 | tf_op jit(solution)/shard_map/all_to_all | solution.py:198
  99.4 0.5 collective-permute-start
  100.0 1.8 %constant_dynamic-slice_fusion = bf16[128,1,16,512]{3,2,1,0:T(8,128)(2,1)S(1)} fusion(bf16[128,2,16,512]{3,2,1,0:T(8,128)(2,1)} %all-to-all-done.rows_ref.cols_ref, s32[]{:T(128)S(6)} %select_n.75), kind=kLoop, calls=%fused_computation.113 | loop fusion | bytes 4194308 | tf_op jit(solution)/shard_map/jit(dynamic_index_in_dim)/dynamic_slice | solution.py:210
  101.8 25.2 %while.16 = (s32[]{:T(128)}, f32[2048]{0:T(1024)S(1)}, f32[2048]{0:T(1024)S(1)}, f32[2048]{0:T(1024)S(1)}, f32[2048]{0:T(1024)S(1)}, /*index=5*/bf16[2048,512]{1...) while((s32[]{:T(128)}, f32[2048]{0:T(1024)S(1)}, ...), condition=%wide.region_3.4_spmd.clone, body=%wide.region_0.3_spmd.clone.sunk | while | flops 50806272 | bytes 9220263 | solution.py:123
  101.8 0.6 add_reduce_fusion.4
  103.1 0.4 convolution_bitcast_fusion.8
  103.5 0.6 convolution_bitcast_fusion.9
  104.3 0.6 add_reduce_fusion.5
  105.6 0.4 convolution_bitcast_fusion.10
  106.1 0.6 convolution_bitcast_fusion.11
  106.8 0.6 add_reduce_fusion.4
  108.1 0.4 convolution_bitcast_fusion.8
  108.6 0.6 convolution_bitcast_fusion.9
  109.3 0.6 add_reduce_fusion.5
  110.7 0.4 convolution_bitcast_fusion.10
  111.1 0.6 convolution_bitcast_fusion.11
  111.8 0.6 add_reduce_fusion.4
  113.6 0.6 convolution_bitcast_fusion.9
  114.3 0.6 add_reduce_fusion.5
  115.7 0.4 convolution_bitcast_fusion.10
  116.1 0.6 convolution_bitcast_fusion.11
  116.9 0.6 add_reduce_fusion.4
  118.2 0.4 convolution_bitcast_fusion.8
  118.6 0.6 convolution_bitcast_fusion.9
  119.4 0.6 add_reduce_fusion.5
  120.7 0.4 convolution_bitcast_fusion.10
  121.2 0.6 convolution_bitcast_fusion.11
  121.9 0.6 add_reduce_fusion.4
  123.7 0.6 convolution_bitcast_fusion.9
  124.4 0.6 add_reduce_fusion.5
  125.8 0.4 convolution_bitcast_fusion.10
  126.2 0.6 convolution_bitcast_fusion.11
  127.1 0.8 copy.15
  127.9 4.5 %all-to-all-start.1 = ((f32[2,128,1,16]{3,2,0,1:T(1,128)}), f32[2,128,1,16]{3,2,0,1:T(1,128)S(1)}, u32[]{:S(2)}, u32[]{:S(2)}) async-start(f32[2,128,1,16]{3,2,0,1:T(1,128)} %copy.15), calls=%async_computation.1 | async-start | bytes 262144 | tf_op jit(solution)/shard_map/all_to_all | solution.py:218
  132.5 11.4 %shard_map.60.prev_ref = bf16[2,4,512,2048]{3,2,1,0:T(8,128)(2,1)} custom-call(s32[2]{0:T(128)} %get-tuple-element.210.block_ref, bf16[128,2,16,512]{3,2,1,0:T(8,128)(2,1)} %all-to-all-done.rows_ref.cols_ref, bf16[128,2,16,512]{3,2,1,0:T(8,128)(2,1)} %all-to-all-done.rows_ref.cols_ref), custom_call_target="tpu_custom_call" | custom-call | flops 4294967296 | bytes 13631488 | tf_op jit(solution)/shard_map/pallas_call | solution.py:173
  143.9 0.7 copy.18
  144.6 11.4 %shard_map.61 = bf16[2,4,512,2048]{3,2,1,0:T(8,128)(2,1)} custom-call(s32[2]{0:T(128)} %get-tuple-element.209.block_ref, bf16[128,2,16,512]{3,2,1,0:T(8,128)(2,1)} %collective-permute-done.rows_ref.cols_ref, bf16[128,2,16,512]{3,2,1,0:T(8,128)(2,1)} %collective-permute-done.rows_ref.cols_ref, ...), custom_call_target="tpu_custom_call", output_to_operand_aliasing={{}: (3, {})} | custom-call | flops 4294967296 | bytes 13631488 | tf_op jit(solution)/shard_map/pallas_call | solution.py:173
  (103 shorter events, 2.7 us)
Async XLA Ops:
  33.9 65.5 %all-to-all-start = ((bf16[128,2,16,512]{3,2,1,0:T(8,128)(2,1)}), bf16[128,2,16,512]{3,2,1,0:T(8,128)(2,1)}, u32[]{:S(2)}, u32[]{:S(2)}) async-start(bf16[128,2,16,512]{3,2,1,0:T(8,128)(2,1)} %bitcast.70), calls=%async_computation | async-start | bytes 8388608 | tf_op jit(solution)/shard_map/all_to_all | solution.py:198
  99.4 45.2 %collective-permute-start = (bf16[128,2,16,512]{3,2,1,0:T(8,128)(2,1)}, bf16[128,2,16,512]{3,2,1,0:T(8,128)(2,1)}, u32[]{:S(2)}, u32[]{:S(2)}) collective-permute-start(bf16[128,2,16,512]{3,2,1,0:T(8,128)(2,1)} %all-to-all-done.rows_ref.cols_ref), channel_id=1, source_target_pairs={{0,1},{1,0},{2,3},{3,2},{4,5},{5,4},{6,7},{7,6},{8,9},{9,8},{10,11... | collective-permute-start | bytes 12582920 | tf_op jit(solution)/shard_map/ppermute | solution.py:203
  127.9 15.9 %all-to-all-start.1 = ((f32[2,128,1,16]{3,2,0,1:T(1,128)}), f32[2,128,1,16]{3,2,0,1:T(1,128)S(1)}, u32[]{:S(2)}, u32[]{:S(2)}) async-start(f32[2,128,1,16]{3,2,0,1:T(1,128)} %copy.15), calls=%async_computation.1 | async-start | bytes 262144 | tf_op jit(solution)/shard_map/all_to_all | solution.py:218

commit v9 on v8

--- a/solution.py
+++ b/solution.py
@@ -53,7 +53,7 @@
     window = window_table()
     table = transform_table()
     count = voltages.shape[0]
-    samples = voltages.astype(jnp.bfloat16).reshape(count, SPECTRA + TAPS - 1, FRAME)
+    samples = voltages.reshape(count, SPECTRA + TAPS - 1, FRAME)
     table_t = jnp.transpose(table.reshape(FRAME, 2 * CHANS))
     group = 8
     return pl.pallas_call(
@@ -71,7 +71,7 @@
         cost_estimate=pl.CostEstimate(
             flops=2 * count * SPECTRA * FRAME * (2 * CHANS + TAPS),
             transcendentals=0,
-            bytes_accessed=2 * count * (SPECTRA + TAPS) * FRAME + 2 * CHANS * count * 2 * SPECTRA,
+            bytes_accessed=4 * count * (SPECTRA + TAPS) * FRAME + 2 * CHANS * count * 2 * SPECTRA,
         ),
     )(keep, window, table_t, samples)
 
@@ -120,7 +120,7 @@
 
     start_re = jnp.ones((count,), jnp.float32)
     start_im = jnp.zeros((count,), jnp.float32)
-    return lax.fori_loop(0, ITERS // 2, paired, (start_re, start_im))
+    return lax.fori_loop(0, ITERS // 2, paired, (start_re, start_im), unroll=True)
 
 
 def correlate_kernel(block_ref, rows_ref, cols_ref, out_ref, turned_ref):

time: 157 us -> 156 us (level)
  loops' own time: 7.26 us -> 0 us
  between operations: 0.78 us -> 7.93 us
  local copies, waits for them, and re-layouts: 12.8 us -> 17.8 us
  other arithmetic: 18.6 us -> 13.8 us
    another operation x1 -> x0, loops' own time: 7.26 us -> none  [solve_gains(): return lax.fori_loop(0, ITERS // 2, paired, (start_re, start_im))]
    convert_element_type x1 -> x0, other arithmetic: 5.29 us -> none  [channelize(): voltages.astype(jnp.bfloat16).reshape(count, SPECTRA + TAPS - 1, FRAME)]
    reshape x1, local copies, waits for them, and re-layouts: 5.03 us -> 10.1 us  [channelize(): samples = voltages.reshape(count, SPECTRA + TAPS - 1, FRAME)]
  transfers between devices with their start and end apart: 3 -> 3, of which waited for: 1 -> 1; matrix products, arithmetic and copies ran while one was open for 15% -> 4% of each run, Pallas kernels for 7% -> 7%
where the time goes in v9:
time: 156 us
  waiting for transfers between devices  50.4 us (32%)
  Pallas kernels  38.4 us (25%)
  local copies, waits for them, and re-layouts  17.8 us (11%)
  starting transfers between devices  17 us (11%)
  other arithmetic  13.8 us (9%)
  matrix products  10.1 us (6%)
  between operations  7.93 us (5%)
    all_to_all x1, waiting for transfers between devices, shards(): lax.all_to_all(send, ('chan', 'blk'), split_axis=0, concat_axis=0, tiled=...  50.4 us
    pallas_call x2, Pallas kernels, correlate(): pl.pallas_call(kernel, grid_spec=spec, out_shape=jax.ShapeDtypeStruct((2,...  22.8 us
    pallas_call x1, Pallas kernels, channelize(): pl.pallas_call(transform_kernel, grid=(count // group,), in_specs=[pl.Blo...  15.6 us
    all_to_all x1, starting transfers between devices, shards(): lax.all_to_all(send, ('chan', 'blk'), split_axis=0, concat_axis=0, tiled=...  12 us
    reshape x1, local copies, waits for them, and re-layouts, channelize(): samples = voltages.reshape(count, SPECTRA + TAPS - 1, FRAME)  10.1 us
    dot_general x20, matrix products, exact_dot(): lax.dot_general(lhs, split3(rhs_f32), (dims, ((), ())), preferred_element...  10.1 us
    reduce_sum x10, other arithmetic, sweep(): power = jnp.sum(probe_re * probe_re + probe_im * probe_im)  6.25 us
    all_to_all x1, starting transfers between devices, shards(): lax.all_to_all(owners, ('chan', 'blk'), split_axis=1, concat_axis=1, tile...  4.56 us
  transfers between devices with their start and end apart: 3, of which 1 were waited for; matrix products, arithmetic and copies ran while one was open for 4% of the time, Pallas kernels for 7%

profile of v9, /device:TPU:1, one launch (start us, length us, event | category | flops | bytes accessed | tf_op | source)
XLA Modules:
  0.0 155.5 jit_solution(6497528056533051836)
XLA Ops:
  0.6 0.7 fusion.70.window_ref
  1.3 1.2 subtract_convert_fusion.20.keep_ref
  2.6 1.2 cosine_convert_fusion
  3.8 10.1 %reshape.402.samples_ref = s32[16,263,512]{2,1,0:T(8,128)} reshape(s32[16,134656]{1,0:T(8,128)} %param.4) | data formatting | bytes 17235968 | tf_op jit(solution)/shard_map/reshape | solution.py:56
  14.0 0.7 pad_maximum_fusion
  14.7 15.6 %shard_map.59 = bf16[128,16,512]{2,1,0:T(8,128)(2,1)} custom-call(f32[16]{0:T(128)} %subtract_convert_fusion.20.keep_ref, f32[8,512]{1,0:T(8,128)} %fusion.70.window_ref, bf16[256,512]{1,0:T(8,128)(2,1)} %bitcast.541, s32[16,263,512]{2,1,0:T(8,128)} %reshape.402.samples_ref), custom_call_target="tpu_custom_call" | custom-call | flops 1107296256 | bytes 10747904 | tf_op jit(solution)/shard_map/pallas_call | solution.py:59
  30.3 4.2 %broadcast_in_dim.20 = bf16[32,2,2,2,16,512]{5,4,3,2,1,0:T(8,128)(2,1)} broadcast(bf16[32,2,2,16,512]{4,3,2,1,0:T(8,128)(2,1)} %bitcast.520), dimensions={0,2,3,4,5} | broadcast | bytes 6291456 | tf_op jit(solution)/shard_map/broadcast_in_dim | solution.py:194
  34.5 12.0 %all-to-all-start = ((bf16[128,2,16,512]{3,2,1,0:T(8,128)(2,1)}), bf16[128,2,16,512]{3,2,1,0:T(8,128)(2,1)}, u32[]{:S(2)}, u32[]{:S(2)}) async-start(bf16[128,2,16,512]{3,2,1,0:T(8,128)(2,1)} %bitcast.519), calls=%async_computation | async-start | bytes 8388608 | tf_op jit(solution)/shard_map/all_to_all | solution.py:198
  46.5 1.0 fusion.163
  47.6 0.7 add_reduce_fusion.9
  48.9 0.6 pad_add_fusion
  49.6 50.4 %all-to-all-done.rows_ref.cols_ref = bf16[128,2,16,512]{3,2,1,0:T(8,128)(2,1)} async-done(((bf16[128,2,16,512]{3,2,1,0:T(8,128)(2,1)}), bf16[128,2,16,512]{3,2,1,0:T(8,128)(2,1)}, u32[]{:S(2)}, u32[]{:S(2)}) %all-to-all-start) | async-done | bytes 4194336 | tf_op jit(solution)/shard_map/all_to_all | solution.py:198
  100.0 1.8 %constant_dynamic-slice_fusion = bf16[128,1,16,512]{3,2,1,0:T(8,128)(2,1)S(1)} fusion(bf16[128,2,16,512]{3,2,1,0:T(8,128)(2,1)} %all-to-all-done.rows_ref.cols_ref, s32[]{:T(128)S(6)} %select_n.75), kind=kLoop, calls=%fused_computation.483 | loop fusion | bytes 4194308 | tf_op jit(solution)/shard_map/jit(dynamic_index_in_dim)/dynamic_slice | solution.py:210
  101.8 0.4 fusion.6
  102.2 0.6 fusion.99
  103.1 0.6 add_reduce_fusion.8
  104.3 0.4 fusion.12
  104.8 0.6 fusion.105
  105.6 0.6 add_reduce_fusion.7
  106.9 0.4 fusion.18
  107.3 0.6 fusion.111
  108.2 0.6 add_reduce_fusion.6
  109.4 0.4 fusion.24
  109.9 0.6 fusion.117
  110.7 0.6 add_reduce_fusion.5
  112.0 0.4 fusion.30
  112.4 0.6 fusion.123
  113.2 0.6 add_reduce_fusion.4
  114.5 0.4 fusion.36
  115.0 0.6 fusion.129
  115.8 0.6 add_reduce_fusion.3
  117.1 0.4 fusion.42
  117.5 0.6 fusion.135
  118.3 0.6 add_reduce_fusion.2
  119.6 0.4 fusion.48
  120.0 0.6 fusion.141
  120.9 0.6 add_reduce_fusion.1
  122.2 0.4 fusion.54
  122.6 0.6 fusion.147
  123.2 0.5 collective-permute-start
  123.8 0.6 add_reduce_fusion
  125.2 0.4 fusion.60
  125.6 0.6 fusion.153
  126.6 0.8 copy.15
  127.4 4.6 %all-to-all-start.1 = ((f32[2,128,1,16]{3,2,0,1:T(1,128)}), f32[2,128,1,16]{3,2,0,1:T(1,128)S(1)}, u32[]{:S(2)}, u32[]{:S(2)}) async-start(f32[2,128,1,16]{3,2,0,1:T(1,128)} %copy.15), calls=%async_computation.1 | async-start | bytes 262144 | tf_op jit(solution)/shard_map/all_to_all | solution.py:218
  131.9 11.4 %shard_map.60.prev_ref = bf16[2,4,512,2048]{3,2,1,0:T(8,128)(2,1)} custom-call(s32[2]{0:T(128)} %get-tuple-element.151.block_ref, bf16[128,2,16,512]{3,2,1,0:T(8,128)(2,1)} %all-to-all-done.rows_ref.cols_ref, bf16[128,2,16,512]{3,2,1,0:T(8,128)(2,1)} %all-to-all-done.rows_ref.cols_ref), custom_call_target="tpu_custom_call" | custom-call | flops 4294967296 | bytes 13631488 | tf_op jit(solution)/shard_map/pallas_call | solution.py:173
  143.4 0.7 copy.18
  144.1 11.4 %shard_map.61 = bf16[2,4,512,2048]{3,2,1,0:T(8,128)(2,1)} custom-call(s32[2]{0:T(128)} %get-tuple-element.150.block_ref, bf16[128,2,16,512]{3,2,1,0:T(8,128)(2,1)} %collective-permute-done.rows_ref.cols_ref, bf16[128,2,16,512]{3,2,1,0:T(8,128)(2,1)} %collective-permute-done.rows_ref.cols_ref, ...), custom_call_target="tpu_custom_call", output_to_operand_aliasing={{}: (3, {})} | custom-call | flops 4294967296 | bytes 13631488 | tf_op jit(solution)/shard_map/pallas_call | solution.py:173
  (98 shorter events, 2.2 us)
Async XLA Ops:
  34.5 65.5 %all-to-all-start = ((bf16[128,2,16,512]{3,2,1,0:T(8,128)(2,1)}), bf16[128,2,16,512]{3,2,1,0:T(8,128)(2,1)}, u32[]{:S(2)}, u32[]{:S(2)}) async-start(bf16[128,2,16,512]{3,2,1,0:T(8,128)(2,1)} %bitcast.519), calls=%async_computation | async-start | bytes 8388608 | tf_op jit(solution)/shard_map/all_to_all | solution.py:198
  123.2 20.9 %collective-permute-start = (bf16[128,2,16,512]{3,2,1,0:T(8,128)(2,1)}, bf16[128,2,16,512]{3,2,1,0:T(8,128)(2,1)}, u32[]{:S(2)}, u32[]{:S(2)}) collective-permute-start(bf16[128,2,16,512]{3,2,1,0:T(8,128)(2,1)} %all-to-all-done.rows_ref.cols_ref), channel_id=1, source_target_pairs={{0,1},{1,0},{2,3},{3,2},{4,5},{5,4},{6,7},{7,6},{8,9},{9,8},{10,11... | collective-permute-start | bytes 12582920 | tf_op jit(solution)/shard_map/ppermute | solution.py:203
  127.4 16.0 %all-to-all-start.1 = ((f32[2,128,1,16]{3,2,0,1:T(1,128)}), f32[2,128,1,16]{3,2,0,1:T(1,128)S(1)}, u32[]{:S(2)}, u32[]{:S(2)}) async-start(f32[2,128,1,16]{3,2,0,1:T(1,128)} %copy.15), calls=%async_computation.1 | async-start | bytes 262144 | tf_op jit(solution)/shard_map/all_to_all | solution.py:218

commit v10 on v9

--- a/solution.py
+++ b/solution.py
@@ -191,33 +191,48 @@
     chan_count = lax.axis_size("chan")
     block_index = lax.axis_index("blk")
     spectra = spectra.reshape(chan_count, 2, 2, input_count, 2 * SPECTRA)
-    send = jnp.broadcast_to(
-        spectra[:, None], (chan_count, 2, 2, 2, input_count, 2 * SPECTRA)
-    )
-    send = send.reshape(chan_count * blk_count, 2, input_count, 2 * SPECTRA)
-    mine = lax.all_to_all(send, ("chan", "blk"), split_axis=0, concat_axis=0, tiled=True)
-    all_inputs = mine.shape[0] * input_count
+    first_send = jnp.swapaxes(spectra, 1, 2)
+    second_send = jnp.swapaxes(spectra[:, :, ::-1], 1, 2)
+    devices = chan_count * blk_count
+
+    def turn(send):
+        send = send.reshape(devices, input_count, 2 * SPECTRA)
+        return lax.all_to_all(send, ("chan", "blk"), split_axis=0, concat_axis=0, tiled=True)
+
+    own = turn(first_send)
+    all_inputs = devices * input_count
     row_count = all_inputs // blk_count
     core = block_index % 2
     level = block_index // 2
-    theirs = lax.ppermute(mine, "blk", perm=[(b, b ^ 1) for b in range(blk_count)])
-    local_chans = 4
-    first = jnp.stack([block_index, 2 * core]).astype(jnp.int32)
-    second = jnp.stack([block_index, 2 - 2 * core]).astype(jnp.int32)
-    visibility = correlate(mine, first, row_count, total_chans=local_chans)
-    visibility = correlate(theirs, second, row_count, out=visibility, total_chans=local_chans)
-
-    data = lax.dynamic_index_in_dim(mine, level, 1, keepdims=False).reshape(all_inputs, -1)
+    swap = [(b, b ^ 1) for b in range(blk_count)]
+    own_partner = lax.ppermute(own, "blk", perm=swap)
+
     solve = 2 * core + level
     amp = lax.dynamic_index_in_dim(model_amp, solve, 0, keepdims=False)
     phase = lax.dynamic_index_in_dim(model_phase, solve, 0, keepdims=False)
     full_re = amp * jnp.cos(phase)
     full_im = amp * jnp.sin(phase)
-    solved = jnp.stack(solve_gains(data, full_re, full_im))
-    owners = solved.reshape(2, chan_count * blk_count, 1, input_count)
+    other = turn(second_send)
+    other_partner = lax.ppermute(other, "blk", perm=swap)
+    solved = jnp.stack(solve_gains(own.reshape(all_inputs, -1), full_re, full_im))
+    owners = solved.reshape(2, devices, 1, input_count)
     gains = lax.all_to_all(owners, ("chan", "blk"), split_axis=1, concat_axis=1, tiled=True)
     gains = gains.reshape(2, chan_count, 2, 2, input_count)
     gains = jnp.swapaxes(gains, 2, 3).reshape(2, -1, input_count)
+
+    local_chans = 4
+    shape = (devices, 1, input_count, 2 * SPECTRA)
+    visibility = None
+    for data, chan in (
+        (own, 2 * core + level),
+        (other, 2 * core + 1 - level),
+        (own_partner, 2 - 2 * core + level),
+        (other_partner, 3 - 2 * core - level),
+    ):
+        scalars = jnp.stack([block_index, chan]).astype(jnp.int32)
+        visibility = correlate(
+            data.reshape(shape), scalars, row_count, out=visibility, total_chans=local_chans
+        )
     return (visibility, gains)
 
 

time: 156 us -> 144 us (0.923)
  waiting for transfers between devices: 50.4 us -> 25.9 us
  starting transfers between devices: 17 us -> 23.8 us
  Pallas kernels: 38.4 us -> 42.4 us
    all_to_all x1 -> x2, waiting for transfers between devices: 50.4 us -> 25.9 us  [turn(): lax.all_to_all(send, ('chan', 'blk'), split_axis=0, concat_axis=0, tiled=...]
    all_to_all x1 -> x2, starting transfers between devices: 12 us -> 17.3 us  [turn(): lax.all_to_all(send, ('chan', 'blk'), split_axis=0, concat_axis=0, tiled=...]
    broadcast_in_dim x1 -> x0, local copies, waits for them, and re-layouts: 4.19 us -> none  [shards(): jnp.broadcast_to(spectra[:, None], (chan_count, 2, 2, 2, input_count, 2 *...]
    pallas_call x2 -> x4, Pallas kernels: 22.8 us -> 26.8 us  [correlate(): pl.pallas_call(kernel, grid_spec=spec, out_shape=jax.ShapeDtypeStruct((2,...]
    rev x0 -> x1, local copies, waits for them, and re-layouts: none -> 3.27 us  [shards(): second_send = jnp.swapaxes(spectra[:, :, ::-1], 1, 2)]
    reshape x0 -> x1, local copies, waits for them, and re-layouts: none -> 3.18 us  [shards(): spectra = spectra.reshape(chan_count, 2, 2, input_count, 2 * SPECTRA)]
    ppermute x1 -> x2, starting transfers between devices: 0.49 us -> 2.8 us  [the longest x1 1.53 us: shards(): own_partner = lax.ppermute(own, 'blk', perm=swap)]
    dynamic_slice x1 -> x0, local copies, waits for them, and re-layouts: 1.78 us -> none  [shards(): lax.dynamic_index_in_dim(mine, level, 1, keepdims=False)]
  transfers between devices with their start and end apart: 3 -> 5, of which waited for: 1 -> 2; matrix products, arithmetic and copies ran while one was open for 4% -> 19% of each run, Pallas kernels for 7% -> 14%
where the time goes in v10:
time: 144 us; the launch traced here: 143 us
  Pallas kernels  42.4 us (29%)
  waiting for transfers between devices  25.9 us (18%)
  starting transfers between devices  23.8 us (17%)
  local copies, waits for them, and re-layouts  18.3 us (13%)
  other arithmetic  14.8 us (10%)
  matrix products  10.1 us (7%)
  between operations  7.94 us (6%)
    pallas_call x4, Pallas kernels, correlate(): pl.pallas_call(kernel, grid_spec=spec, out_shape=jax.ShapeDtypeStruct((2,...  26.8 us
    all_to_all x2, waiting for transfers between devices, turn(): lax.all_to_all(send, ('chan', 'blk'), split_axis=0, concat_axis=0, tiled=...  25.9 us
    all_to_all x2, starting transfers between devices, turn(): lax.all_to_all(send, ('chan', 'blk'), split_axis=0, concat_axis=0, tiled=...  17.3 us
    pallas_call x1, Pallas kernels, channelize(): pl.pallas_call(transform_kernel, grid=(count // group,), in_specs=[pl.Blo...  15.6 us
    reshape x1, local copies, waits for them, and re-layouts, channelize(): samples = voltages.reshape(count, SPECTRA + TAPS - 1, FRAME)  10.1 us
    dot_general x20, matrix products, exact_dot(): lax.dot_general(lhs, split3(rhs_f32), (dims, ((), ())), preferred_element...  10.1 us
    reduce_sum x10, other arithmetic, sweep(): power = jnp.sum(probe_re * probe_re + probe_im * probe_im)  6.27 us
    all_to_all x1, starting transfers between devices, shards(): lax.all_to_all(owners, ('chan', 'blk'), split_axis=1, concat_axis=1, tile...  3.7 us
  transfers between devices with their start and end apart: 5, of which 2 were waited for; matrix products, arithmetic and copies ran while one was open for 19% of the time, Pallas kernels for 14%

profile of v10, /device:TPU:1, one launch (start us, length us, event | category | flops | bytes accessed | tf_op | source)
XLA Modules:
  0.0 143.3 jit_solution(5573060945631776579)
XLA Ops:
  0.6 0.7 fusion.70.window_ref
  1.3 1.2 cosine_convert_fusion
  2.6 10.1 %reshape.418.samples_ref = s32[16,263,512]{2,1,0:T(8,128)} reshape(s32[16,134656]{1,0:T(8,128)} %param.4) | data formatting | bytes 17235968 | tf_op jit(solution)/shard_map/reshape | solution.py:56
  12.7 0.5 subtract_convert_fusion.20.keep_ref
  13.3 0.7 pad_maximum_fusion
  14.0 15.6 %shard_map.59 = bf16[128,16,512]{2,1,0:T(8,128)(2,1)} custom-call(f32[16]{0:T(128)} %subtract_convert_fusion.20.keep_ref, f32[8,512]{1,0:T(8,128)} %fusion.70.window_ref, bf16[256,512]{1,0:T(8,128)(2,1)} %bitcast.561, s32[16,263,512]{2,1,0:T(8,128)} %reshape.418.samples_ref), custom_call_target="tpu_custom_call" | custom-call | flops 1107296256 | bytes 10747904 | tf_op jit(solution)/shard_map/pallas_call | solution.py:59
  29.6 3.2 %copy.35 = bf16[32,2,2,16,512]{4,3,1,2,0:T(8,128)(2,1)} copy(bf16[32,2,2,16,512]{4,3,2,1,0:T(8,128)(2,1)} %bitcast.540) | data formatting | bytes 4194304 | tf_op jit(solution)/shard_map/reshape | solution.py:193
  32.8 11.5 %all-to-all-start.1 = ((bf16[128,16,512]{2,1,0:T(8,128)(2,1)}), bf16[128,16,512]{2,1,0:T(8,128)(2,1)S(1)}, u32[]{:S(2)}, u32[]{:S(2)}) async-start(bf16[128,16,512]{2,1,0:T(8,128)(2,1)} %bitcast.538), calls=%async_computation.1 | async-start | bytes 4194304 | tf_op jit(solution)/shard_map/all_to_all | solution.py:200
  44.3 3.3 %rev.3 = bf16[32,2,2,16,512]{4,3,1,2,0:T(8,128)(2,1)} reverse(bf16[32,2,2,16,512]{4,3,1,2,0:T(8,128)(2,1)} %copy.35), dimensions={2} | reverse | bytes 4194304 | tf_op jit(solution)/shard_map/rev | solution.py:195
  47.6 1.0 fusion.163
  48.6 0.7 add_reduce_fusion.9
  50.0 0.6 pad_add_fusion.3.block_ref
  50.6 0.6 pad_add_fusion.2.block_ref
  51.1 0.6 pad_add_fusion.1.block_ref
  51.7 0.6 pad_add_fusion.block_ref
  52.4 21.4 %all-to-all-done.1 = bf16[128,16,512]{2,1,0:T(8,128)(2,1)S(1)} async-done(((bf16[128,16,512]{2,1,0:T(8,128)(2,1)}), bf16[128,16,512]{2,1,0:T(8,128)(2,1)S(1)}, u32[]{:S(2)}, u32[]{:S(2)}) %all-to-all-start.1) | async-done | bytes 2097184 | tf_op jit(solution)/shard_map/all_to_all | solution.py:200
  73.8 5.8 %all-to-all-start = ((bf16[128,16,512]{2,1,0:T(8,128)(2,1)}), bf16[128,16,512]{2,1,0:T(8,128)(2,1)}, u32[]{:S(2)}, u32[]{:S(2)}) async-start(bf16[128,16,512]{2,1,0:T(8,128)(2,1)} %bitcast.539), calls=%async_computation | async-start | bytes 4194304 | tf_op jit(solution)/shard_map/all_to_all | solution.py:200
  80.1 0.6 fusion.99
  80.9 0.4 fusion.12
  81.3 0.6 fusion.105
  82.0 0.6 add_reduce_fusion.8
  83.4 0.4 fusion.18
  83.9 0.6 fusion.111
  84.6 0.6 add_reduce_fusion.7
  86.4 0.6 fusion.117
  87.1 0.6 add_reduce_fusion.6
  89.0 0.6 fusion.123
  89.7 0.6 add_reduce_fusion.5
  91.5 0.6 fusion.129
  92.2 0.6 add_reduce_fusion.4
  94.1 0.6 fusion.135
  94.7 0.6 add_reduce_fusion.3
  96.6 0.6 fusion.141
  97.3 0.6 add_reduce_fusion.2
  99.2 0.6 add_reduce_fusion.1
  100.4 0.6 fusion.147
  101.2 0.6 add_reduce_fusion
  102.4 1.5 %collective-permute-start.1 = (bf16[128,16,512]{2,1,0:T(8,128)(2,1)S(1)}, bf16[128,16,512]{2,1,0:T(8,128)(2,1)}, u32[]{:S(2)}, u32[]{:S(2)}) collective-permute-start(bf16[128,16,512]{2,1,0:T(8,128)(2,1)S(1)} %all-to-all-done.1), channel_id=1, source_target_pairs={{0,1},{1,0},{2,3},{3,2},{4,5},{5,4},{6,7},{7,6},{8,9},{9,8},{10,11... | collective-permute-start | bytes 6291464 | tf_op jit(solution)/shard_map/ppermute | solution.py:208
  104.4 4.5 %all-to-all-done = bf16[128,16,512]{2,1,0:T(8,128)(2,1)} async-done(((bf16[128,16,512]{2,1,0:T(8,128)(2,1)}), bf16[128,16,512]{2,1,0:T(8,128)(2,1)}, u32[]{:S(2)}, u32[]{:S(2)}) %all-to-all-start) | async-done | bytes 2097184 | tf_op jit(solution)/shard_map/all_to_all | solution.py:200
  108.9 1.3 collective-permute-start
  110.2 0.6 fusion.153
  111.2 0.8 copy.41
  112.0 3.7 %all-to-all-start.2 = ((f32[2,128,1,16]{3,2,0,1:T(1,128)}), f32[2,128,1,16]{3,2,0,1:T(1,128)S(1)}, u32[]{:S(2)}, u32[]{:S(2)}) async-start(f32[2,128,1,16]{3,2,0,1:T(1,128)} %copy.41), calls=%async_computation.2 | async-start | bytes 262144 | tf_op jit(solution)/shard_map/all_to_all | solution.py:219
  115.7 6.7 %shard_map.60.prev_ref = bf16[2,4,512,2048]{3,2,1,0:T(8,128)(2,1)} custom-call(s32[2]{0:T(128)} %pad_add_fusion.3.block_ref, bf16[128,1,16,512]{3,2,1,0:T(8,128)(2,1)} %bitcast.536, bf16[128,1,16,512]{3,2,1,0:T(8,128)(2,1)} %bitcast.537), custom_call_target="tpu_custom_call" | custom-call | flops 2147483648 | bytes 6815744 | tf_op jit(solution)/shard_map/pallas_call | solution.py:173
  122.4 6.7 %shard_map.61.prev_ref = bf16[2,4,512,2048]{3,2,1,0:T(8,128)(2,1)} custom-call(s32[2]{0:T(128)} %pad_add_fusion.2.block_ref, bf16[128,1,16,512]{3,2,1,0:T(8,128)(2,1)} %bitcast.14.rows_ref.cols_ref, bf16[128,1,16,512]{3,2,1,0:T(8,128)(2,1)} %bitcast.14.rows_ref.cols_ref, bf16[2,4,512,2048]{3,2,1,0:T(8,128)(2,1)} %shard_map.60.prev_ref), custom_call_target="tpu_custom_call", output_to_operand_aliasing={{}: (3, {})} | custom-call | flops 2147483648 | bytes 6815744 | tf_op jit(solution)/shard_map/pallas_call | solution.py:173
  129.2 0.7 copy.44
  129.9 6.7 %shard_map.62.prev_ref = bf16[2,4,512,2048]{3,2,1,0:T(8,128)(2,1)} custom-call(s32[2]{0:T(128)} %pad_add_fusion.1.block_ref, bf16[128,1,16,512]{3,2,1,0:T(8,128)(2,1)} %bitcast.11.rows_ref.cols_ref, bf16[128,1,16,512]{3,2,1,0:T(8,128)(2,1)} %bitcast.11.rows_ref.cols_ref, bf16[2,4,512,2048]{3,2,1,0:T(8,128)(2,1)} %shard_map.61.prev_ref), custom_call_target="tpu_custom_call", output_to_operand_aliasing={{}: (3, {})} | custom-call | flops 2147483648 | bytes 6815744 | tf_op jit(solution)/shard_map/pallas_call | solution.py:173
  136.6 6.7 %shard_map.63 = bf16[2,4,512,2048]{3,2,1,0:T(8,128)(2,1)} custom-call(s32[2]{0:T(128)} %pad_add_fusion.block_ref, bf16[128,1,16,512]{3,2,1,0:T(8,128)(2,1)} %bitcast.7.rows_ref.cols_ref, bf16[128,1,16,512]{3,2,1,0:T(8,128)(2,1)} %bitcast.7.rows_ref.cols_ref, bf16[2,4,512,2048]{3,2,1,0:T(8,128)(2,1)} %shard_map.62.prev_ref), custom_call_target="tpu_custom_call", output_to_operand_aliasing={{}: (3, {})} | custom-call | flops 2147483648 | bytes 6815744 | tf_op jit(solution)/shard_map/pallas_call | solution.py:173
  (111 shorter events, 5.2 us)
Async XLA Ops:
  2.6 10.2 %copy-start.1 = (s32[16]{0:T(128)S(1)}, s32[16]{0:T(128)}, u32[]{:S(2)}) copy-start(s32[16]{0:T(128)} %param.5) | copy-start | bytes 196
  32.8 41.0 %all-to-all-start.1 = ((bf16[128,16,512]{2,1,0:T(8,128)(2,1)}), bf16[128,16,512]{2,1,0:T(8,128)(2,1)S(1)}, u32[]{:S(2)}, u32[]{:S(2)}) async-start(bf16[128,16,512]{2,1,0:T(8,128)(2,1)} %bitcast.538), calls=%async_computation.1 | async-start | bytes 4194304 | tf_op jit(solution)/shard_map/all_to_all | solution.py:200
  73.8 36.4 %copy-start = (bf16[128,16,512]{2,1,0:T(8,128)(2,1)}, bf16[128,16,512]{2,1,0:T(8,128)(2,1)S(1)}, u32[]{:S(2)}) copy-start(bf16[128,16,512]{2,1,0:T(8,128)(2,1)S(1)} %all-to-all-done.1) | copy-start | bytes 6291460
  73.8 35.1 %all-to-all-start = ((bf16[128,16,512]{2,1,0:T(8,128)(2,1)}), bf16[128,16,512]{2,1,0:T(8,128)(2,1)}, u32[]{:S(2)}, u32[]{:S(2)}) async-start(bf16[128,16,512]{2,1,0:T(8,128)(2,1)} %bitcast.539), calls=%async_computation | async-start | bytes 4194304 | tf_op jit(solution)/shard_map/all_to_all | solution.py:200
  102.4 27.5 %collective-permute-start.1 = (bf16[128,16,512]{2,1,0:T(8,128)(2,1)S(1)}, bf16[128,16,512]{2,1,0:T(8,128)(2,1)}, u32[]{:S(2)}, u32[]{:S(2)}) collective-permute-start(bf16[128,16,512]{2,1,0:T(8,128)(2,1)S(1)} %all-to-all-done.1), channel_id=1, source_target_pairs={{0,1},{1,0},{2,3},{3,2},{4,5},{5,4},{6,7},{7,6},{8,9},{9,8},{10,11... | collective-permute-start | bytes 6291464 | tf_op jit(solution)/shard_map/ppermute | solution.py:208
  108.9 27.7 %collective-permute-start = (bf16[128,16,512]{2,1,0:T(8,128)(2,1)}, bf16[128,16,512]{2,1,0:T(8,128)(2,1)}, u32[]{:S(2)}, u32[]{:S(2)}) collective-permute-start(bf16[128,16,512]{2,1,0:T(8,128)(2,1)} %all-to-all-done), channel_id=1, source_target_pairs={{0,1},{1,0},{2,3},{3,2},{4,5},{5,4},{6,7},{7,6},{8,9},{9,8},{10,11... | collective-permute-start | bytes 6291464 | tf_op jit(solution)/shard_map/ppermute | solution.py:216
  112.0 17.1 %all-to-all-start.2 = ((f32[2,128,1,16]{3,2,0,1:T(1,128)}), f32[2,128,1,16]{3,2,0,1:T(1,128)S(1)}, u32[]{:S(2)}, u32[]{:S(2)}) async-start(f32[2,128,1,16]{3,2,0,1:T(1,128)} %copy.41), calls=%async_computation.2 | async-start | bytes 262144 | tf_op jit(solution)/shard_map/all_to_all | solution.py:219

commit v11 on v10

--- a/solution.py
+++ b/solution.py
@@ -54,7 +54,8 @@
     table = transform_table()
     count = voltages.shape[0]
     samples = voltages.reshape(count, SPECTRA + TAPS - 1, FRAME)
-    table_t = jnp.transpose(table.reshape(FRAME, 2 * CHANS))
+    order = jnp.arange(CHANS).reshape(-1, 2, 2).transpose(0, 2, 1).reshape(-1)
+    table_t = jnp.transpose(table[:, :, order].reshape(FRAME, 2 * CHANS))
     group = 8
     return pl.pallas_call(
         transform_kernel,
@@ -191,8 +192,8 @@
     chan_count = lax.axis_size("chan")
     block_index = lax.axis_index("blk")
     spectra = spectra.reshape(chan_count, 2, 2, input_count, 2 * SPECTRA)
-    first_send = jnp.swapaxes(spectra, 1, 2)
-    second_send = jnp.swapaxes(spectra[:, :, ::-1], 1, 2)
+    first_send = spectra
+    second_send = spectra[:, ::-1]
     devices = chan_count * blk_count
 
     def turn(send):
@@ -215,10 +216,11 @@
     other = turn(second_send)
     other_partner = lax.ppermute(other, "blk", perm=swap)
     solved = jnp.stack(solve_gains(own.reshape(all_inputs, -1), full_re, full_im))
-    owners = solved.reshape(2, devices, 1, input_count)
-    gains = lax.all_to_all(owners, ("chan", "blk"), split_axis=1, concat_axis=1, tiled=True)
-    gains = gains.reshape(2, chan_count, 2, 2, input_count)
-    gains = jnp.swapaxes(gains, 2, 3).reshape(2, -1, input_count)
+    everyone = lax.all_gather(solved, ("chan", "blk"), axis=0, tiled=False)
+    me = lax.axis_index("chan") * blk_count + block_index
+    gains = lax.dynamic_slice_in_dim(everyone, me * input_count, input_count, 2)
+    gains = gains.reshape(chan_count, 2, 2, 2, input_count)
+    gains = jnp.transpose(gains, (3, 0, 2, 1, 4)).reshape(2, -1, input_count)
 
     local_chans = 4
     shape = (devices, 1, input_count, 2 * SPECTRA)

time: 144 us -> 315 us (2.19)
  waiting for transfers between devices: 25.9 us -> 188 us
  between operations: 7.94 us -> 21.3 us
  starting transfers between devices: 23.8 us -> 20.2 us
    all_gather x0 -> x1, waiting for transfers between devices: none -> 161 us  [shards(): everyone = lax.all_gather(solved, ('chan', 'blk'), axis=0, tiled=False)]
    all_to_all x1 -> x0, starting transfers between devices: 3.7 us -> none  [shards(): lax.all_to_all(owners, ('chan', 'blk'), split_axis=1, concat_axis=1, tile...]
  transfers between devices with their start and end apart: 5 -> 5, of which waited for: 2 -> 3; matrix products, arithmetic and copies ran while one was open for 19% -> 8% of each run, Pallas kernels for 14% -> 9%
where the time goes in v11:
time: 315 us; the launch traced here: 314 us
  waiting for transfers between devices  188 us (60%)
  Pallas kernels  42.4 us (13%)
  between operations  21.3 us (7%)
  starting transfers between devices  20.2 us (6%)
  local copies, waits for them, and re-layouts  17.5 us (6%)
  other arithmetic  14.7 us (5%)
  matrix products  10.1 us (3%)
    all_gather x1, waiting for transfers between devices, shards(): everyone = lax.all_gather(solved, ('chan', 'blk'), axis=0, tiled=False)  161 us
    pallas_call x4, Pallas kernels, correlate(): pl.pallas_call(kernel, grid_spec=spec, out_shape=jax.ShapeDtypeStruct((2,...  26.8 us
    all_to_all x2, waiting for transfers between devices, turn(): lax.all_to_all(send, ('chan', 'blk'), split_axis=0, concat_axis=0, tiled=...  26.8 us
    all_to_all x2, starting transfers between devices, turn(): lax.all_to_all(send, ('chan', 'blk'), split_axis=0, concat_axis=0, tiled=...  17.3 us
    pallas_call x1, Pallas kernels, channelize(): pl.pallas_call(transform_kernel, grid=(count // group,), in_specs=[pl.Blo...  15.6 us
    reshape x1, local copies, waits for them, and re-layouts, channelize(): samples = voltages.reshape(count, SPECTRA + TAPS - 1, FRAME)  10.1 us
    dot_general x20, matrix products, exact_dot(): lax.dot_general(lhs, split3(rhs_f32), (dims, ((), ())), preferred_element...  10.1 us
  transfers between devices with their start and end apart: 5, of which 3 were waited for; matrix products, arithmetic and copies ran while one was open for 8% of the time, Pallas kernels for 9%

profile of v11, /device:TPU:1, one launch (start us, length us, event | category | flops | bytes accessed | tf_op | source)
XLA Modules:
  0.0 314.0 jit_solution(16569254464785014274)
XLA Ops:
  7.2 0.7 fusion.70.window_ref
  7.9 1.1 cosine_convert_fusion
  9.4 1.1 gather_fusion
  10.6 0.7 copy.30
  11.3 10.1 %reshape.487.samples_ref = s32[16,263,512]{2,1,0:T(8,128)} reshape(s32[16,134656]{1,0:T(8,128)} %param.4) | data formatting | bytes 17235968 | tf_op jit(solution)/shard_map/reshape | solution.py:56
  21.4 0.6 subtract_convert_fusion.20.keep_ref
  22.0 15.6 %shard_map.59 = bf16[128,16,512]{2,1,0:T(8,128)(2,1)} custom-call(f32[16]{0:T(128)} %subtract_convert_fusion.20.keep_ref, f32[8,512]{1,0:T(8,128)} %fusion.70.window_ref, bf16[256,512]{1,0:T(8,128)(2,1)} %bitcast.560, s32[16,263,512]{2,1,0:T(8,128)} %reshape.487.samples_ref), custom_call_target="tpu_custom_call" | custom-call | flops 1107296256 | bytes 10747904 | tf_op jit(solution)/shard_map/pallas_call | solution.py:60
  37.6 11.5 %all-to-all-start.1 = ((bf16[128,16,512]{2,1,0:T(8,128)(2,1)}), bf16[128,16,512]{2,1,0:T(8,128)(2,1)S(1)}, u32[]{:S(2)}, u32[]{:S(2)}) async-start(bf16[128,16,512]{2,1,0:T(8,128)(2,1)} %shard_map.59), calls=%async_computation.1 | async-start | bytes 4194304 | tf_op jit(solution)/shard_map/all_to_all | solution.py:201
  49.2 3.3 %rev.3 = bf16[32,2,2,16,512]{4,3,2,1,0:T(8,128)(2,1)} reverse(bf16[32,2,2,16,512]{4,3,2,1,0:T(8,128)(2,1)} %bitcast.538), dimensions={1} | reverse | bytes 4194304 | tf_op jit(solution)/shard_map/rev | solution.py:196
  52.4 1.0 fusion.163
  53.5 0.6 add_reduce_fusion.9
  54.8 23.8 %all-to-all-done.1 = bf16[128,16,512]{2,1,0:T(8,128)(2,1)S(1)} async-done(((bf16[128,16,512]{2,1,0:T(8,128)(2,1)}), bf16[128,16,512]{2,1,0:T(8,128)(2,1)S(1)}, u32[]{:S(2)}, u32[]{:S(2)}) %all-to-all-start.1) | async-done | bytes 2097184 | tf_op jit(solution)/shard_map/all_to_all | solution.py:201
  78.7 5.8 %all-to-all-start = ((bf16[128,16,512]{2,1,0:T(8,128)(2,1)}), bf16[128,16,512]{2,1,0:T(8,128)(2,1)}, u32[]{:S(2)}, u32[]{:S(2)}) async-start(bf16[128,16,512]{2,1,0:T(8,128)(2,1)} %bitcast.539), calls=%async_computation | async-start | bytes 4194304 | tf_op jit(solution)/shard_map/all_to_all | solution.py:201
  85.2 0.6 fusion.99
  86.4 0.6 fusion.105
  87.1 0.6 add_reduce_fusion.8
  88.5 0.4 fusion.18
  89.0 0.6 fusion.111
  89.6 0.6 add_reduce_fusion.7
  91.5 0.6 fusion.117
  92.2 0.6 add_reduce_fusion.6
  94.1 0.6 fusion.123
  94.7 0.6 add_reduce_fusion.5
  96.6 0.6 fusion.129
  97.3 0.6 add_reduce_fusion.4
  99.1 0.6 fusion.135
  99.8 0.6 add_reduce_fusion.3
  101.7 0.6 fusion.141
  102.4 0.6 add_reduce_fusion.2
  104.2 0.6 fusion.147
  104.9 0.6 add_reduce_fusion.1
  106.3 0.6 add_reduce_fusion
  108.0 0.6 fusion.153
  108.8 0.6 maximum_bitcast_fusion
  109.5 1.4 collective-permute-start.1
  110.8 3.0 all-to-all-done
  113.8 1.3 collective-permute-start
  115.0 0.6 pad_add_fusion.3.block_ref
  115.6 0.6 pad_add_fusion.2.block_ref
  116.2 0.6 pad_add_fusion.1.block_ref
  116.8 0.6 pad_add_fusion.block_ref
  117.5 6.7 %shard_map.60.prev_ref = bf16[2,4,512,2048]{3,2,1,0:T(8,128)(2,1)} custom-call(s32[2]{0:T(128)} %pad_add_fusion.3.block_ref, bf16[128,1,16,512]{3,2,1,0:T(8,128)(2,1)} %bitcast.536, bf16[128,1,16,512]{3,2,1,0:T(8,128)(2,1)} %bitcast.537), custom_call_target="tpu_custom_call" | custom-call | flops 2147483648 | bytes 6815744 | tf_op jit(solution)/shard_map/pallas_call | solution.py:174
  124.2 6.7 %shard_map.61.prev_ref = bf16[2,4,512,2048]{3,2,1,0:T(8,128)(2,1)} custom-call(s32[2]{0:T(128)} %pad_add_fusion.2.block_ref, bf16[128,1,16,512]{3,2,1,0:T(8,128)(2,1)} %bitcast.13.rows_ref.cols_ref, bf16[128,1,16,512]{3,2,1,0:T(8,128)(2,1)} %bitcast.13.rows_ref.cols_ref, bf16[2,4,512,2048]{3,2,1,0:T(8,128)(2,1)} %shard_map.60.prev_ref), custom_call_target="tpu_custom_call", output_to_operand_aliasing={{}: (3, {})} | custom-call | flops 2147483648 | bytes 6815744 | tf_op jit(solution)/shard_map/pallas_call | solution.py:174
  130.9 6.7 %shard_map.62.prev_ref = bf16[2,4,512,2048]{3,2,1,0:T(8,128)(2,1)} custom-call(s32[2]{0:T(128)} %pad_add_fusion.1.block_ref, bf16[128,1,16,512]{3,2,1,0:T(8,128)(2,1)} %bitcast.10.rows_ref.cols_ref, bf16[128,1,16,512]{3,2,1,0:T(8,128)(2,1)} %bitcast.10.rows_ref.cols_ref, bf16[2,4,512,2048]{3,2,1,0:T(8,128)(2,1)} %shard_map.61.prev_ref), custom_call_target="tpu_custom_call", output_to_operand_aliasing={{}: (3, {})} | custom-call | flops 2147483648 | bytes 6815744 | tf_op jit(solution)/shard_map/pallas_call | solution.py:174
  137.6 6.7 %shard_map.63 = bf16[2,4,512,2048]{3,2,1,0:T(8,128)(2,1)} custom-call(s32[2]{0:T(128)} %pad_add_fusion.block_ref, bf16[128,1,16,512]{3,2,1,0:T(8,128)(2,1)} %bitcast.8.rows_ref.cols_ref, bf16[128,1,16,512]{3,2,1,0:T(8,128)(2,1)} %bitcast.8.rows_ref.cols_ref, bf16[2,4,512,2048]{3,2,1,0:T(8,128)(2,1)} %shard_map.62.prev_ref), custom_call_target="tpu_custom_call", output_to_operand_aliasing={{}: (3, {})} | custom-call | flops 2147483648 | bytes 6815744 | tf_op jit(solution)/shard_map/pallas_call | solution.py:174
  144.3 161.0 %all-gather.4.cloned.1.call-done = f32[128,2,2048]{2,1,0:T(2,128)} async-done(((f32[1,2,2048]{2,1,0:T(2,128)}), f32[128,2,2048]{2,1,0:T(2,128)}) %all-gather.4.cloned.1.call-update) | async-done | bytes 2097168 | tf_op jit(solution)/shard_map/all_gather | solution.py:219
  305.3 1.1 constant_dynamic-slice_fusion
  306.5 0.7 copy.37
  (116 shorter events, 6.0 us)
Async XLA Ops:
  11.3 10.2 %copy-start.1 = (s32[16]{0:T(128)S(1)}, s32[16]{0:T(128)}, u32[]{:S(2)}) copy-start(s32[16]{0:T(128)} %param.5) | copy-start | bytes 196
  37.6 41.0 %all-to-all-start.1 = ((bf16[128,16,512]{2,1,0:T(8,128)(2,1)}), bf16[128,16,512]{2,1,0:T(8,128)(2,1)S(1)}, u32[]{:S(2)}, u32[]{:S(2)}) async-start(bf16[128,16,512]{2,1,0:T(8,128)(2,1)} %shard_map.59), calls=%async_computation.1 | async-start | bytes 4194304 | tf_op jit(solution)/shard_map/all_to_all | solution.py:201
  78.7 30.8 %copy-start = (bf16[128,16,512]{2,1,0:T(8,128)(2,1)}, bf16[128,16,512]{2,1,0:T(8,128)(2,1)S(1)}, u32[]{:S(2)}) copy-start(bf16[128,16,512]{2,1,0:T(8,128)(2,1)S(1)} %all-to-all-done.1) | copy-start | bytes 6291460
  78.7 35.1 %all-to-all-start = ((bf16[128,16,512]{2,1,0:T(8,128)(2,1)}), bf16[128,16,512]{2,1,0:T(8,128)(2,1)}, u32[]{:S(2)}, u32[]{:S(2)}) async-start(bf16[128,16,512]{2,1,0:T(8,128)(2,1)} %bitcast.539), calls=%async_computation | async-start | bytes 4194304 | tf_op jit(solution)/shard_map/all_to_all | solution.py:201
  84.5 220.8 %all-gather.4.cloned.1.call-start = ((), (), s32[]{:S(2)}) async-start(), calls=%async_computation.2 | async-start | bytes 2113536 | tf_op jit(solution)/shard_map/all_gather | solution.py:219
  109.5 21.4 %collective-permute-start.1 = (bf16[128,16,512]{2,1,0:T(8,128)(2,1)S(1)}, bf16[128,16,512]{2,1,0:T(8,128)(2,1)}, u32[]{:S(2)}, u32[]{:S(2)}) collective-permute-start(bf16[128,16,512]{2,1,0:T(8,128)(2,1)S(1)} %all-to-all-done.1), channel_id=1, source_target_pairs={{0,1},{1,0},{2,3},{3,2},{4,5},{5,4},{6,7},{7,6},{8,9},{9,8},{10,11... | collective-permute-start | bytes 6291464 | tf_op jit(solution)/shard_map/ppermute | solution.py:209
  113.8 23.8 %collective-permute-start = (bf16[128,16,512]{2,1,0:T(8,128)(2,1)}, bf16[128,16,512]{2,1,0:T(8,128)(2,1)}, u32[]{:S(2)}, u32[]{:S(2)}) collective-permute-start(bf16[128,16,512]{2,1,0:T(8,128)(2,1)} %all-to-all-done), channel_id=1, source_target_pairs={{0,1},{1,0},{2,3},{3,2},{4,5},{5,4},{6,7},{7,6},{8,9},{9,8},{10,11... | collective-permute-start | bytes 6291464 | tf_op jit(solution)/shard_map/ppermute | solution.py:217
Sparse Core Ops, SparseCore 0:
  109.6 195.6 all-gather.3

commit v12 on v11

--- a/solution.py
+++ b/solution.py
@@ -215,26 +215,29 @@
     full_im = amp * jnp.sin(phase)
     other = turn(second_send)
     other_partner = lax.ppermute(other, "blk", perm=swap)
-    solved = jnp.stack(solve_gains(own.reshape(all_inputs, -1), full_re, full_im))
-    everyone = lax.all_gather(solved, ("chan", "blk"), axis=0, tiled=False)
-    me = lax.axis_index("chan") * blk_count + block_index
-    gains = lax.dynamic_slice_in_dim(everyone, me * input_count, input_count, 2)
-    gains = gains.reshape(chan_count, 2, 2, 2, input_count)
-    gains = jnp.transpose(gains, (3, 0, 2, 1, 4)).reshape(2, -1, input_count)
-
     local_chans = 4
     shape = (devices, 1, input_count, 2 * SPECTRA)
-    visibility = None
+
+    def correlate_into(visibility, data, chan):
+        scalars = jnp.stack([block_index, chan]).astype(jnp.int32)
+        return correlate(
+            data.reshape(shape), scalars, row_count, out=visibility, total_chans=local_chans
+        )
+
+    visibility = correlate_into(None, own, 2 * core + level)
+    own, visibility = lax.optimization_barrier((own, visibility))
+    solved = jnp.stack(solve_gains(own.reshape(all_inputs, -1), full_re, full_im))
+    owners = solved.reshape(2, devices, 1, input_count)
+    gains = lax.all_to_all(owners, ("chan", "blk"), split_axis=1, concat_axis=1, tiled=True)
+    gains = gains.reshape(2, chan_count, 2, 2, input_count)
+    gains = jnp.swapaxes(gains, 2, 3).reshape(2, -1, input_count)
+
     for data, chan in (
-        (own, 2 * core + level),
         (other, 2 * core + 1 - level),
         (own_partner, 2 - 2 * core + level),
         (other_partner, 3 - 2 * core - level),
     ):
-        scalars = jnp.stack([block_index, chan]).astype(jnp.int32)
-        visibility = correlate(
-            data.reshape(shape), scalars, row_count, out=visibility, total_chans=local_chans
-        )
+        visibility = correlate_into(visibility, data, chan)
     return (visibility, gains)
 
 

time: 315 us -> 147 us (0.47)
  waiting for transfers between devices: 188 us -> 24.8 us
  between operations: 21.3 us -> 7.96 us
  starting transfers between devices: 20.2 us -> 27.8 us
    all_gather x1 -> x0, waiting for transfers between devices: 161 us -> none  [shards(): everyone = lax.all_gather(solved, ('chan', 'blk'), axis=0, tiled=False)]
    all_to_all x0 -> x1, starting transfers between devices: none -> 8.82 us  [shards(): lax.all_to_all(owners, ('chan', 'blk'), split_axis=1, concat_axis=1, tile...]
    all_to_all x2, waiting for transfers between devices: 26.8 us -> 21.4 us  [turn(): lax.all_to_all(send, ('chan', 'blk'), split_axis=0, concat_axis=0, tiled=...]
    all_to_all x0 -> x1, waiting for transfers between devices: none -> 3.36 us  [shards(): lax.all_to_all(owners, ('chan', 'blk'), split_axis=1, concat_axis=1, tile...]
  transfers between devices with their start and end apart: 5 -> 5, of which waited for: 3 -> 2; matrix products, arithmetic and copies ran while one was open for 8% -> 18% of each run, Pallas kernels for 9% -> 14%
where the time goes in v12:
time: 147 us; the launch traced here: 146 us
  Pallas kernels  42.5 us (29%)
  starting transfers between devices  27.8 us (19%)
  waiting for transfers between devices  24.8 us (17%)
  local copies, waits for them, and re-layouts  18.7 us (13%)
  other arithmetic  14.1 us (10%)
  matrix products  10.1 us (7%)
  between operations  7.96 us (5%)
    pallas_call x4, Pallas kernels, correlate(): pl.pallas_call(kernel, grid_spec=spec, out_shape=jax.ShapeDtypeStruct((2,...  27 us
    all_to_all x2, waiting for transfers between devices, turn(): lax.all_to_all(send, ('chan', 'blk'), split_axis=0, concat_axis=0, tiled=...  21.4 us
    all_to_all x2, starting transfers between devices, turn(): lax.all_to_all(send, ('chan', 'blk'), split_axis=0, concat_axis=0, tiled=...  17.3 us
    pallas_call x1, Pallas kernels, channelize(): pl.pallas_call(transform_kernel, grid=(count // group,), in_specs=[pl.Blo...  15.5 us
    reshape x1, local copies, waits for them, and re-layouts, channelize(): samples = voltages.reshape(count, SPECTRA + TAPS - 1, FRAME)  10.1 us
    dot_general x20, matrix products, exact_dot(): lax.dot_general(lhs, split3(rhs_f32), (dims, ((), ())), preferred_element...  10.1 us
    all_to_all x1, starting transfers between devices, shards(): lax.all_to_all(owners, ('chan', 'blk'), split_axis=1, concat_axis=1, tile...  8.82 us
    reduce_sum x10, other arithmetic, sweep(): power = jnp.sum(probe_re * probe_re + probe_im * probe_im)  6.22 us
  transfers between devices with their start and end apart: 5, of which 2 were waited for; matrix products, arithmetic and copies ran while one was open for 18% of the time, Pallas kernels for 14%

profile of v12, /device:TPU:1, one launch (start us, length us, event | category | flops | bytes accessed | tf_op | source)
XLA Modules:
  0.0 145.9 jit_solution(15099126595483614153)
XLA Ops:
  0.7 0.7 fusion.70.window_ref
  1.4 1.1 cosine_convert_fusion
  2.9 1.1 gather_fusion
  4.0 0.7 copy.41
  4.7 10.1 %reshape.490.samples_ref = s32[16,263,512]{2,1,0:T(8,128)} reshape(s32[16,134656]{1,0:T(8,128)} %param.4) | data formatting | bytes 17235968 | tf_op jit(solution)/shard_map/reshape | solution.py:56
  14.9 0.5 subtract_convert_fusion.20.keep_ref
  15.4 15.5 %shard_map.59 = bf16[128,16,512]{2,1,0:T(8,128)(2,1)} custom-call(f32[16]{0:T(128)} %subtract_convert_fusion.20.keep_ref, f32[8,512]{1,0:T(8,128)} %fusion.70.window_ref, bf16[256,512]{1,0:T(8,128)(2,1)} %bitcast.558, s32[16,263,512]{2,1,0:T(8,128)} %reshape.490.samples_ref), custom_call_target="tpu_custom_call" | custom-call | flops 1107296256 | bytes 10747904 | tf_op jit(solution)/shard_map/pallas_call | solution.py:60
  31.0 11.5 %all-to-all-start.1 = ((bf16[128,16,512]{2,1,0:T(8,128)(2,1)}), bf16[128,16,512]{2,1,0:T(8,128)(2,1)S(1)}, u32[]{:S(2)}, u32[]{:S(2)}) async-start(bf16[128,16,512]{2,1,0:T(8,128)(2,1)} %shard_map.59), calls=%async_computation.1 | async-start | bytes 4194304 | tf_op jit(solution)/shard_map/all_to_all | solution.py:201
  42.5 3.3 %rev.3 = bf16[32,2,2,16,512]{4,3,2,1,0:T(8,128)(2,1)} reverse(bf16[32,2,2,16,512]{4,3,2,1,0:T(8,128)(2,1)} %bitcast.536), dimensions={1} | reverse | bytes 4194304 | tf_op jit(solution)/shard_map/rev | solution.py:196
  45.8 1.0 fusion.163
  46.8 0.6 add_reduce_fusion.9
  48.1 0.6 pad_add_fusion.3.block_ref
  48.7 0.6 pad_add_fusion.2.block_ref
  49.3 0.6 pad_add_fusion.1.block_ref
  49.9 0.6 pad_add_fusion.block_ref
  50.6 21.4 %all-to-all-done.1 = bf16[128,16,512]{2,1,0:T(8,128)(2,1)S(1)} async-done(((bf16[128,16,512]{2,1,0:T(8,128)(2,1)}), bf16[128,16,512]{2,1,0:T(8,128)(2,1)S(1)}, u32[]{:S(2)}, u32[]{:S(2)}) %all-to-all-start.1) | async-done | bytes 2097184 | tf_op jit(solution)/shard_map/all_to_all | solution.py:201
  72.0 1.4 copy-done
  73.4 5.8 %all-to-all-start = ((bf16[128,16,512]{2,1,0:T(8,128)(2,1)}), bf16[128,16,512]{2,1,0:T(8,128)(2,1)}, u32[]{:S(2)}, u32[]{:S(2)}) async-start(bf16[128,16,512]{2,1,0:T(8,128)(2,1)} %bitcast.537), calls=%async_computation | async-start | bytes 4194304 | tf_op jit(solution)/shard_map/all_to_all | solution.py:201
  79.2 6.8 %shard_map.60.prev_ref = bf16[2,4,512,2048]{3,2,1,0:T(8,128)(2,1)} custom-call(s32[2]{0:T(128)} %pad_add_fusion.3.block_ref, bf16[128,1,16,512]{3,2,1,0:T(8,128)(2,1)} %bitcast.514, bf16[128,1,16,512]{3,2,1,0:T(8,128)(2,1)} %bitcast.515), custom_call_target="tpu_custom_call" | custom-call | flops 2147483648 | bytes 6815744 | tf_op jit(solution)/shard_map/pallas_call | solution.py:174
  86.4 0.6 fusion.99
  87.3 0.4 fusion.12
  87.7 0.6 fusion.105
  88.4 0.6 add_reduce_fusion.8
  90.3 0.6 fusion.111
  90.9 0.6 add_reduce_fusion.7
  92.4 0.4 fusion.24
  92.8 0.6 fusion.117
  93.5 0.6 add_reduce_fusion.6
  95.3 0.6 fusion.123
  96.0 0.6 add_reduce_fusion.5
  97.9 0.6 fusion.129
  98.6 0.6 add_reduce_fusion.4
  100.4 0.6 fusion.135
  101.1 0.6 add_reduce_fusion.3
  103.0 0.6 fusion.141
  103.7 0.6 add_reduce_fusion.2
  105.5 0.6 add_reduce_fusion.1
  106.8 0.6 fusion.147
  107.4 1.6 %collective-permute-start.1 = (bf16[128,16,512]{2,1,0:T(8,128)(2,1)S(1)}, bf16[128,16,512]{2,1,0:T(8,128)(2,1)}, u32[]{:S(2)}, u32[]{:S(2)}) collective-permute-start(bf16[128,16,512]{2,1,0:T(8,128)(2,1)S(1)} %copy-done.1), channel_id=1, source_target_pairs={{0,1},{1,0},{2,3},{3,2},{4,5},{5,4},{6,7},{7,6},{8,9},{9,8},{10,11... | collective-permute-start | bytes 6291464 | tf_op jit(solution)/shard_map/ppermute | solution.py:209
  109.6 0.6 add_reduce_fusion
  111.0 0.6 fusion.153
  112.0 0.8 copy.46
  112.8 8.8 %all-to-all-start.2 = ((f32[2,128,1,16]{3,2,0,1:T(1,128)}), f32[2,128,1,16]{3,2,0,1:T(1,128)S(1)}, u32[]{:S(2)}, u32[]{:S(2)}) async-start(f32[2,128,1,16]{3,2,0,1:T(1,128)} %copy.46), calls=%async_computation.2 | async-start | bytes 262144 | tf_op jit(solution)/shard_map/all_to_all | solution.py:231
  121.6 6.7 %shard_map.61.prev_ref = bf16[2,4,512,2048]{3,2,1,0:T(8,128)(2,1)} custom-call(s32[2]{0:T(128)} %pad_add_fusion.2.block_ref, bf16[128,1,16,512]{3,2,1,0:T(8,128)(2,1)} %bitcast.13.rows_ref.cols_ref, bf16[128,1,16,512]{3,2,1,0:T(8,128)(2,1)} %bitcast.13.rows_ref.cols_ref, bf16[2,4,512,2048]{3,2,1,0:T(8,128)(2,1)} %shard_map.60.prev_ref), custom_call_target="tpu_custom_call", output_to_operand_aliasing={{}: (3, {})} | custom-call | flops 2147483648 | bytes 6815744 | tf_op jit(solution)/shard_map/pallas_call | solution.py:174
  128.3 3.4 %all-to-all-done.2 = f32[2,128,1,16]{3,2,0,1:T(1,128)S(1)} async-done(((f32[2,128,1,16]{3,2,0,1:T(1,128)}), f32[2,128,1,16]{3,2,0,1:T(1,128)S(1)}, u32[]{:S(2)}, u32[]{:S(2)}) %all-to-all-start.2) | async-done | bytes 16416 | tf_op jit(solution)/shard_map/all_to_all | solution.py:231
  131.8 0.7 copy.49
  132.4 6.7 %shard_map.62.prev_ref = bf16[2,4,512,2048]{3,2,1,0:T(8,128)(2,1)} custom-call(s32[2]{0:T(128)} %pad_add_fusion.1.block_ref, bf16[128,1,16,512]{3,2,1,0:T(8,128)(2,1)} %bitcast.10.rows_ref.cols_ref, bf16[128,1,16,512]{3,2,1,0:T(8,128)(2,1)} %bitcast.10.rows_ref.cols_ref, bf16[2,4,512,2048]{3,2,1,0:T(8,128)(2,1)} %shard_map.61.prev_ref), custom_call_target="tpu_custom_call", output_to_operand_aliasing={{}: (3, {})} | custom-call | flops 2147483648 | bytes 6815744 | tf_op jit(solution)/shard_map/pallas_call | solution.py:174
  139.2 6.7 %shard_map.63 = bf16[2,4,512,2048]{3,2,1,0:T(8,128)(2,1)} custom-call(s32[2]{0:T(128)} %pad_add_fusion.block_ref, bf16[128,1,16,512]{3,2,1,0:T(8,128)(2,1)} %bitcast.8.rows_ref.cols_ref, bf16[128,1,16,512]{3,2,1,0:T(8,128)(2,1)} %bitcast.8.rows_ref.cols_ref, bf16[2,4,512,2048]{3,2,1,0:T(8,128)(2,1)} %shard_map.62.prev_ref), custom_call_target="tpu_custom_call", output_to_operand_aliasing={{}: (3, {})} | custom-call | flops 2147483648 | bytes 6815744 | tf_op jit(solution)/shard_map/pallas_call | solution.py:174
  (119 shorter events, 5.7 us)
Async XLA Ops:
  4.7 10.2 %copy-start.2 = (s32[16]{0:T(128)S(1)}, s32[16]{0:T(128)}, u32[]{:S(2)}) copy-start(s32[16]{0:T(128)} %param.5) | copy-start | bytes 196
  31.0 41.0 %all-to-all-start.1 = ((bf16[128,16,512]{2,1,0:T(8,128)(2,1)}), bf16[128,16,512]{2,1,0:T(8,128)(2,1)S(1)}, u32[]{:S(2)}, u32[]{:S(2)}) async-start(bf16[128,16,512]{2,1,0:T(8,128)(2,1)} %shard_map.59), calls=%async_computation.1 | async-start | bytes 4194304 | tf_op jit(solution)/shard_map/all_to_all | solution.py:201
  72.0 1.4 copy-start
  73.4 37.5 %all-to-all-start = ((bf16[128,16,512]{2,1,0:T(8,128)(2,1)}), bf16[128,16,512]{2,1,0:T(8,128)(2,1)}, u32[]{:S(2)}, u32[]{:S(2)}) async-start(bf16[128,16,512]{2,1,0:T(8,128)(2,1)} %bitcast.537), calls=%async_computation | async-start | bytes 4194304 | tf_op jit(solution)/shard_map/all_to_all | solution.py:201
  79.2 6.9 %copy-start.1 = (bf16[128,16,512]{2,1,0:T(8,128)(2,1)S(1)}, bf16[128,16,512]{2,1,0:T(8,128)(2,1)}, u32[]{:S(2)}) copy-start(bf16[128,16,512]{2,1,0:T(8,128)(2,1)} %copy-done) | copy-start | bytes 6291460
  107.4 25.0 %collective-permute-start.1 = (bf16[128,16,512]{2,1,0:T(8,128)(2,1)S(1)}, bf16[128,16,512]{2,1,0:T(8,128)(2,1)}, u32[]{:S(2)}, u32[]{:S(2)}) collective-permute-start(bf16[128,16,512]{2,1,0:T(8,128)(2,1)S(1)} %copy-done.1), channel_id=1, source_target_pairs={{0,1},{1,0},{2,3},{3,2},{4,5},{5,4},{6,7},{7,6},{8,9},{9,8},{10,11... | collective-permute-start | bytes 6291464 | tf_op jit(solution)/shard_map/ppermute | solution.py:209
  110.8 28.3 %collective-permute-start = (bf16[128,16,512]{2,1,0:T(8,128)(2,1)}, bf16[128,16,512]{2,1,0:T(8,128)(2,1)}, u32[]{:S(2)}, u32[]{:S(2)}) collective-permute-start(bf16[128,16,512]{2,1,0:T(8,128)(2,1)} %all-to-all-done), channel_id=1, source_target_pairs={{0,1},{1,0},{2,3},{3,2},{4,5},{5,4},{6,7},{7,6},{8,9},{9,8},{10,11... | collective-permute-start | bytes 6291464 | tf_op jit(solution)/shard_map/ppermute | solution.py:217
  112.8 18.9 %all-to-all-start.2 = ((f32[2,128,1,16]{3,2,0,1:T(1,128)}), f32[2,128,1,16]{3,2,0,1:T(1,128)S(1)}, u32[]{:S(2)}, u32[]{:S(2)}) async-start(f32[2,128,1,16]{3,2,0,1:T(1,128)} %copy.46), calls=%async_computation.2 | async-start | bytes 262144 | tf_op jit(solution)/shard_map/all_to_all | solution.py:231

commit v13 on v12

--- a/solution.py
+++ b/solution.py
@@ -224,15 +224,15 @@
             data.reshape(shape), scalars, row_count, out=visibility, total_chans=local_chans
         )
 
-    visibility = correlate_into(None, own, 2 * core + level)
-    own, visibility = lax.optimization_barrier((own, visibility))
     solved = jnp.stack(solve_gains(own.reshape(all_inputs, -1), full_re, full_im))
     owners = solved.reshape(2, devices, 1, input_count)
     gains = lax.all_to_all(owners, ("chan", "blk"), split_axis=1, concat_axis=1, tiled=True)
     gains = gains.reshape(2, chan_count, 2, 2, input_count)
     gains = jnp.swapaxes(gains, 2, 3).reshape(2, -1, input_count)
 
+    visibility = None
     for data, chan in (
+        (own, 2 * core + level),
         (other, 2 * core + 1 - level),
         (own_partner, 2 - 2 * core + level),
         (other_partner, 3 - 2 * core - level),

time: 147 us -> 143 us (0.973)
  starting transfers between devices: 27.8 us -> 23.8 us
    all_to_all x1, starting transfers between devices: 8.82 us -> 3.7 us  [shards(): lax.all_to_all(owners, ('chan', 'blk'), split_axis=1, concat_axis=1, tile...]
    all_to_all x2, waiting for transfers between devices: 21.4 us -> 25.9 us  [turn(): lax.all_to_all(send, ('chan', 'blk'), split_axis=0, concat_axis=0, tiled=...]
    all_to_all x1, waiting for transfers between devices: 3.36 us -> 0.01 us  [shards(): lax.all_to_all(owners, ('chan', 'blk'), split_axis=1, concat_axis=1, tile...]
  transfers between devices with their start and end apart: 5 -> 5, of which waited for: 2 -> 2; matrix products, arithmetic and copies ran while one was open for 18% -> 19% of each run, Pallas kernels for 14% -> 14%
where the time goes in v13:
time: 143 us; the launch traced here: 142 us
  Pallas kernels  42.4 us (30%)
  waiting for transfers between devices  25.9 us (18%)
  starting transfers between devices  23.8 us (17%)
  local copies, waits for them, and re-layouts  17.3 us (12%)
  other arithmetic  14 us (10%)
  matrix products  10.1 us (7%)
  between operations  7.99 us (6%)
    pallas_call x4, Pallas kernels, correlate(): pl.pallas_call(kernel, grid_spec=spec, out_shape=jax.ShapeDtypeStruct((2,...  26.8 us
    all_to_all x2, waiting for transfers between devices, turn(): lax.all_to_all(send, ('chan', 'blk'), split_axis=0, concat_axis=0, tiled=...  25.9 us
    all_to_all x2, starting transfers between devices, turn(): lax.all_to_all(send, ('chan', 'blk'), split_axis=0, concat_axis=0, tiled=...  17.3 us
    pallas_call x1, Pallas kernels, channelize(): pl.pallas_call(transform_kernel, grid=(count // group,), in_specs=[pl.Blo...  15.6 us
    reshape x1, local copies, waits for them, and re-layouts, channelize(): samples = voltages.reshape(count, SPECTRA + TAPS - 1, FRAME)  10.1 us
    dot_general x20, matrix products, exact_dot(): lax.dot_general(lhs, split3(rhs_f32), (dims, ((), ())), preferred_element...  10.1 us
    reduce_sum x10, other arithmetic, sweep(): power = jnp.sum(probe_re * probe_re + probe_im * probe_im)  6.27 us
    all_to_all x1, starting transfers between devices, shards(): lax.all_to_all(owners, ('chan', 'blk'), split_axis=1, concat_axis=1, tile...  3.7 us
  transfers between devices with their start and end apart: 5, of which 2 were waited for; matrix products, arithmetic and copies ran while one was open for 19% of the time, Pallas kernels for 14%

profile of v13, /device:TPU:1, one launch (start us, length us, event | category | flops | bytes accessed | tf_op | source)
XLA Modules:
  0.0 141.6 jit_solution(16726781151331443405)
XLA Ops:
  0.7 0.7 fusion.70.window_ref
  1.4 1.1 cosine_convert_fusion
  2.9 1.1 gather_fusion
  4.0 0.7 copy.41
  4.8 10.1 %reshape.490.samples_ref = s32[16,263,512]{2,1,0:T(8,128)} reshape(s32[16,134656]{1,0:T(8,128)} %param.4) | data formatting | bytes 17235968 | tf_op jit(solution)/shard_map/reshape | solution.py:56
  14.9 0.5 subtract_convert_fusion.20.keep_ref
  15.4 15.6 %shard_map.59 = bf16[128,16,512]{2,1,0:T(8,128)(2,1)} custom-call(f32[16]{0:T(128)} %subtract_convert_fusion.20.keep_ref, f32[8,512]{1,0:T(8,128)} %fusion.70.window_ref, bf16[256,512]{1,0:T(8,128)(2,1)} %bitcast.558, s32[16,263,512]{2,1,0:T(8,128)} %reshape.490.samples_ref), custom_call_target="tpu_custom_call" | custom-call | flops 1107296256 | bytes 10747904 | tf_op jit(solution)/shard_map/pallas_call | solution.py:60
  31.0 11.5 %all-to-all-start.1 = ((bf16[128,16,512]{2,1,0:T(8,128)(2,1)}), bf16[128,16,512]{2,1,0:T(8,128)(2,1)S(1)}, u32[]{:S(2)}, u32[]{:S(2)}) async-start(bf16[128,16,512]{2,1,0:T(8,128)(2,1)} %shard_map.59), calls=%async_computation.1 | async-start | bytes 4194304 | tf_op jit(solution)/shard_map/all_to_all | solution.py:201
  42.6 3.3 %rev.3 = bf16[32,2,2,16,512]{4,3,2,1,0:T(8,128)(2,1)} reverse(bf16[32,2,2,16,512]{4,3,2,1,0:T(8,128)(2,1)} %bitcast.536), dimensions={1} | reverse | bytes 4194304 | tf_op jit(solution)/shard_map/rev | solution.py:196
  45.8 1.0 fusion.163
  46.9 0.7 add_reduce_fusion.9
  48.2 0.6 pad_add_fusion.3.block_ref
  48.8 0.6 pad_add_fusion.2.block_ref
  49.4 0.6 pad_add_fusion.1.block_ref
  50.0 0.6 pad_add_fusion.block_ref
  50.7 21.4 %all-to-all-done.1 = bf16[128,16,512]{2,1,0:T(8,128)(2,1)S(1)} async-done(((bf16[128,16,512]{2,1,0:T(8,128)(2,1)}), bf16[128,16,512]{2,1,0:T(8,128)(2,1)S(1)}, u32[]{:S(2)}, u32[]{:S(2)}) %all-to-all-start.1) | async-done | bytes 2097184 | tf_op jit(solution)/shard_map/all_to_all | solution.py:201
  72.1 5.8 %all-to-all-start = ((bf16[128,16,512]{2,1,0:T(8,128)(2,1)}), bf16[128,16,512]{2,1,0:T(8,128)(2,1)}, u32[]{:S(2)}, u32[]{:S(2)}) async-start(bf16[128,16,512]{2,1,0:T(8,128)(2,1)} %bitcast.537), calls=%async_computation | async-start | bytes 4194304 | tf_op jit(solution)/shard_map/all_to_all | solution.py:201
  78.3 0.6 fusion.99
  79.2 0.4 fusion.12
  79.6 0.6 fusion.105
  80.3 0.6 add_reduce_fusion.8
  81.7 0.4 fusion.18
  82.1 0.6 fusion.111
  82.8 0.6 add_reduce_fusion.7
  84.7 0.6 fusion.117
  85.4 0.6 add_reduce_fusion.6
  87.2 0.6 fusion.123
  87.9 0.6 add_reduce_fusion.5
  89.8 0.6 fusion.129
  90.5 0.6 add_reduce_fusion.4
  92.3 0.6 fusion.135
  93.0 0.6 add_reduce_fusion.3
  94.9 0.6 fusion.141
  95.5 0.6 add_reduce_fusion.2
  97.4 0.6 add_reduce_fusion.1
  98.7 0.6 fusion.147
  99.4 0.6 add_reduce_fusion
  100.7 1.5 %collective-permute-start.1 = (bf16[128,16,512]{2,1,0:T(8,128)(2,1)S(1)}, bf16[128,16,512]{2,1,0:T(8,128)(2,1)}, u32[]{:S(2)}, u32[]{:S(2)}) collective-permute-start(bf16[128,16,512]{2,1,0:T(8,128)(2,1)S(1)} %all-to-all-done.1), channel_id=1, source_target_pairs={{0,1},{1,0},{2,3},{3,2},{4,5},{5,4},{6,7},{7,6},{8,9},{9,8},{10,11... | collective-permute-start | bytes 6291464 | tf_op jit(solution)/shard_map/ppermute | solution.py:209
  102.7 4.5 %all-to-all-done = bf16[128,16,512]{2,1,0:T(8,128)(2,1)} async-done(((bf16[128,16,512]{2,1,0:T(8,128)(2,1)}), bf16[128,16,512]{2,1,0:T(8,128)(2,1)}, u32[]{:S(2)}, u32[]{:S(2)}) %all-to-all-start) | async-done | bytes 2097184 | tf_op jit(solution)/shard_map/all_to_all | solution.py:201
  107.2 1.3 collective-permute-start
  108.5 0.6 fusion.153
  109.5 0.8 copy.46
  110.3 3.7 %all-to-all-start.2 = ((f32[2,128,1,16]{3,2,0,1:T(1,128)}), f32[2,128,1,16]{3,2,0,1:T(1,128)S(1)}, u32[]{:S(2)}, u32[]{:S(2)}) async-start(f32[2,128,1,16]{3,2,0,1:T(1,128)} %copy.46), calls=%async_computation.2 | async-start | bytes 262144 | tf_op jit(solution)/shard_map/all_to_all | solution.py:229
  114.0 6.7 %shard_map.60.prev_ref = bf16[2,4,512,2048]{3,2,1,0:T(8,128)(2,1)} custom-call(s32[2]{0:T(128)} %pad_add_fusion.3.block_ref, bf16[128,1,16,512]{3,2,1,0:T(8,128)(2,1)} %bitcast.534, bf16[128,1,16,512]{3,2,1,0:T(8,128)(2,1)} %bitcast.535), custom_call_target="tpu_custom_call" | custom-call | flops 2147483648 | bytes 6815744 | tf_op jit(solution)/shard_map/pallas_call | solution.py:174
  120.7 6.7 %shard_map.61.prev_ref = bf16[2,4,512,2048]{3,2,1,0:T(8,128)(2,1)} custom-call(s32[2]{0:T(128)} %pad_add_fusion.2.block_ref, bf16[128,1,16,512]{3,2,1,0:T(8,128)(2,1)} %bitcast.13.rows_ref.cols_ref, bf16[128,1,16,512]{3,2,1,0:T(8,128)(2,1)} %bitcast.13.rows_ref.cols_ref, bf16[2,4,512,2048]{3,2,1,0:T(8,128)(2,1)} %shard_map.60.prev_ref), custom_call_target="tpu_custom_call", output_to_operand_aliasing={{}: (3, {})} | custom-call | flops 2147483648 | bytes 6815744 | tf_op jit(solution)/shard_map/pallas_call | solution.py:174
  127.5 0.7 copy.49
  128.2 6.7 %shard_map.62.prev_ref = bf16[2,4,512,2048]{3,2,1,0:T(8,128)(2,1)} custom-call(s32[2]{0:T(128)} %pad_add_fusion.1.block_ref, bf16[128,1,16,512]{3,2,1,0:T(8,128)(2,1)} %bitcast.10.rows_ref.cols_ref, bf16[128,1,16,512]{3,2,1,0:T(8,128)(2,1)} %bitcast.10.rows_ref.cols_ref, bf16[2,4,512,2048]{3,2,1,0:T(8,128)(2,1)} %shard_map.61.prev_ref), custom_call_target="tpu_custom_call", output_to_operand_aliasing={{}: (3, {})} | custom-call | flops 2147483648 | bytes 6815744 | tf_op jit(solution)/shard_map/pallas_call | solution.py:174
  134.9 6.7 %shard_map.63 = bf16[2,4,512,2048]{3,2,1,0:T(8,128)(2,1)} custom-call(s32[2]{0:T(128)} %pad_add_fusion.block_ref, bf16[128,1,16,512]{3,2,1,0:T(8,128)(2,1)} %bitcast.8.rows_ref.cols_ref, bf16[128,1,16,512]{3,2,1,0:T(8,128)(2,1)} %bitcast.8.rows_ref.cols_ref, bf16[2,4,512,2048]{3,2,1,0:T(8,128)(2,1)} %shard_map.62.prev_ref), custom_call_target="tpu_custom_call", output_to_operand_aliasing={{}: (3, {})} | custom-call | flops 2147483648 | bytes 6815744 | tf_op jit(solution)/shard_map/pallas_call | solution.py:174
  (117 shorter events, 5.6 us)
Async XLA Ops:
  4.8 10.2 %copy-start.1 = (s32[16]{0:T(128)S(1)}, s32[16]{0:T(128)}, u32[]{:S(2)}) copy-start(s32[16]{0:T(128)} %param.5) | copy-start | bytes 196
  31.0 41.0 %all-to-all-start.1 = ((bf16[128,16,512]{2,1,0:T(8,128)(2,1)}), bf16[128,16,512]{2,1,0:T(8,128)(2,1)S(1)}, u32[]{:S(2)}, u32[]{:S(2)}) async-start(bf16[128,16,512]{2,1,0:T(8,128)(2,1)} %shard_map.59), calls=%async_computation.1 | async-start | bytes 4194304 | tf_op jit(solution)/shard_map/all_to_all | solution.py:201
  72.1 36.4 %copy-start = (bf16[128,16,512]{2,1,0:T(8,128)(2,1)}, bf16[128,16,512]{2,1,0:T(8,128)(2,1)S(1)}, u32[]{:S(2)}) copy-start(bf16[128,16,512]{2,1,0:T(8,128)(2,1)S(1)} %all-to-all-done.1) | copy-start | bytes 6291460
  72.1 35.1 %all-to-all-start = ((bf16[128,16,512]{2,1,0:T(8,128)(2,1)}), bf16[128,16,512]{2,1,0:T(8,128)(2,1)}, u32[]{:S(2)}, u32[]{:S(2)}) async-start(bf16[128,16,512]{2,1,0:T(8,128)(2,1)} %bitcast.537), calls=%async_computation | async-start | bytes 4194304 | tf_op jit(solution)/shard_map/all_to_all | solution.py:201
  100.7 27.5 %collective-permute-start.1 = (bf16[128,16,512]{2,1,0:T(8,128)(2,1)S(1)}, bf16[128,16,512]{2,1,0:T(8,128)(2,1)}, u32[]{:S(2)}, u32[]{:S(2)}) collective-permute-start(bf16[128,16,512]{2,1,0:T(8,128)(2,1)S(1)} %all-to-all-done.1), channel_id=1, source_target_pairs={{0,1},{1,0},{2,3},{3,2},{4,5},{5,4},{6,7},{7,6},{8,9},{9,8},{10,11... | collective-permute-start | bytes 6291464 | tf_op jit(solution)/shard_map/ppermute | solution.py:209
  107.2 27.7 %collective-permute-start = (bf16[128,16,512]{2,1,0:T(8,128)(2,1)}, bf16[128,16,512]{2,1,0:T(8,128)(2,1)}, u32[]{:S(2)}, u32[]{:S(2)}) collective-permute-start(bf16[128,16,512]{2,1,0:T(8,128)(2,1)} %all-to-all-done), channel_id=1, source_target_pairs={{0,1},{1,0},{2,3},{3,2},{4,5},{5,4},{6,7},{7,6},{8,9},{9,8},{10,11... | collective-permute-start | bytes 6291464 | tf_op jit(solution)/shard_map/ppermute | solution.py:217
  110.3 17.1 %all-to-all-start.2 = ((f32[2,128,1,16]{3,2,0,1:T(1,128)}), f32[2,128,1,16]{3,2,0,1:T(1,128)S(1)}, u32[]{:S(2)}, u32[]{:S(2)}) async-start(f32[2,128,1,16]{3,2,0,1:T(1,128)} %copy.46), calls=%async_computation.2 | async-start | bytes 262144 | tf_op jit(solution)/shard_map/all_to_all | solution.py:229

commit v14 on v13

--- a/solution.py
+++ b/solution.py
@@ -31,15 +31,26 @@
     return jnp.stack([jnp.cos(angle), -jnp.sin(angle)], axis=1).astype(jnp.bfloat16)
 
 
-def transform_kernel(keep_ref, window_ref, table_ref, samples_ref, out_ref, wide_ref):
-    group = samples_ref.shape[0]
+def transform_kernel(keep_ref, window_ref, table_ref, samples_ref, out_ref, frames_ref):
+    group = samples_ref.shape[1]
     base = pl.program_id(0) * group
     scale = 1.0 / (64.0 * math.sqrt(FRAME))
+
+    def frame(step, carry):
+        acc = window_ref[0:1, :] * samples_ref[step].astype(jnp.float32)
+        for tap in range(1, TAPS):
+            acc = acc + window_ref[tap : tap + 1, :] * samples_ref[step + tap].astype(jnp.float32)
+        rows = pl.ds(pl.multiple_of(step * group, group), group)
+        for lane in range(FRAME // 128):
+            frames_ref[lane, rows, :] = acc[:, lane * 128 : (lane + 1) * 128]
+        return carry
+
+    lax.fori_loop(0, SPECTRA, frame, 0)
     for item in range(group):
-        wide_ref[0 : SPECTRA + TAPS - 1, :] = samples_ref[item].astype(jnp.float32)
-        frames = window_ref[0:1, :] * wide_ref[0:SPECTRA, :]
-        for tap in range(1, TAPS):
-            frames = frames + window_ref[tap : tap + 1, :] * wide_ref[tap : tap + SPECTRA, :]
+        frames = jnp.concatenate(
+            [frames_ref[lane, pl.ds(item, SPECTRA, stride=group), :] for lane in range(FRAME // 128)],
+            axis=1,
+        )
         result = lax.dot_general(
             table_ref[...], frames.astype(jnp.bfloat16), (((1,), (1,)), ((), ())),
             preferred_element_type=jnp.float32,
@@ -53,7 +64,7 @@
     window = window_table()
     table = transform_table()
     count = voltages.shape[0]
-    samples = voltages.reshape(count, SPECTRA + TAPS - 1, FRAME)
+    samples = jnp.transpose(voltages.reshape(count, SPECTRA + TAPS - 1, FRAME), (1, 0, 2))
     order = jnp.arange(CHANS).reshape(-1, 2, 2).transpose(0, 2, 1).reshape(-1)
     table_t = jnp.transpose(table[:, :, order].reshape(FRAME, 2 * CHANS))
     group = 8
@@ -64,11 +75,11 @@
             pl.BlockSpec(memory_space=pltpu.SMEM),
             pl.BlockSpec((TAPS, FRAME), lambda g: (0, 0)),
             pl.BlockSpec((2 * CHANS, FRAME), lambda g: (0, 0)),
-            pl.BlockSpec((group, SPECTRA + TAPS - 1, FRAME), lambda g: (g, 0, 0)),
+            pl.BlockSpec((SPECTRA + TAPS - 1, group, FRAME), lambda g: (0, g, 0)),
         ],
         out_specs=pl.BlockSpec((CHANS, group, 2 * SPECTRA), lambda g: (0, g, 0)),
         out_shape=jax.ShapeDtypeStruct((CHANS, count, 2 * SPECTRA), jnp.bfloat16),
-        scratch_shapes=[pltpu.VMEM((SPECTRA + 2 * TAPS, FRAME), jnp.float32)],
+        scratch_shapes=[pltpu.VMEM((FRAME // 128, SPECTRA * group, 128), jnp.float32)],
         cost_estimate=pl.CostEstimate(
             flops=2 * count * SPECTRA * FRAME * (2 * CHANS + TAPS),
             transcendentals=0,

time: 143 us -> 144 us (level)
  Pallas kernels: 42.4 us -> 45 us
  local copies, waits for them, and re-layouts: 17.3 us -> 15.6 us
    pallas_call x1, Pallas kernels: 15.6 us -> 18.2 us  [channelize(): pl.pallas_call(transform_kernel, grid=(count // group,), in_specs=[pl.Blo...]
    reshape x1, local copies, waits for them, and re-layouts: 10.1 us -> 8.43 us  [channelize(): voltages.reshape(count, SPECTRA + TAPS - 1, FRAME)]
where the time goes in v14:
time: 144 us; the launch traced here: 142 us
  Pallas kernels  45 us (31%)
  waiting for transfers between devices  25.9 us (18%)
  starting transfers between devices  23.8 us (17%)
  local copies, waits for them, and re-layouts  15.6 us (11%)
  other arithmetic  14 us (10%)
  matrix products  10.1 us (7%)
  between operations  7.99 us (6%)
    pallas_call x4, Pallas kernels, correlate(): pl.pallas_call(kernel, grid_spec=spec, out_shape=jax.ShapeDtypeStruct((2,...  26.8 us
    all_to_all x2, waiting for transfers between devices, turn(): lax.all_to_all(send, ('chan', 'blk'), split_axis=0, concat_axis=0, tiled=...  25.9 us
    pallas_call x1, Pallas kernels, channelize(): pl.pallas_call(transform_kernel, grid=(count // group,), in_specs=[pl.Blo...  18.2 us
    all_to_all x2, starting transfers between devices, turn(): lax.all_to_all(send, ('chan', 'blk'), split_axis=0, concat_axis=0, tiled=...  17.3 us
    dot_general x20, matrix products, exact_dot(): lax.dot_general(lhs, split3(rhs_f32), (dims, ((), ())), preferred_element...  10.1 us
    reshape x1, local copies, waits for them, and re-layouts, channelize(): voltages.reshape(count, SPECTRA + TAPS - 1, FRAME)  8.43 us
    reduce_sum x10, other arithmetic, sweep(): power = jnp.sum(probe_re * probe_re + probe_im * probe_im)  6.27 us
    all_to_all x1, starting transfers between devices, shards(): lax.all_to_all(owners, ('chan', 'blk'), split_axis=1, concat_axis=1, tile...  3.7 us
  transfers between devices with their start and end apart: 5, of which 2 were waited for; matrix products, arithmetic and copies ran while one was open for 19% of the time, Pallas kernels for 14%

profile of v14, /device:TPU:1, one launch (start us, length us, event | category | flops | bytes accessed | tf_op | source)
XLA Modules:
  0.0 142.5 jit_solution(13040947989362394771)
XLA Ops:
  0.7 0.7 fusion.70.window_ref
  1.4 1.1 cosine_convert_fusion
  2.9 1.1 gather_fusion
  4.0 0.7 copy.44
  4.8 8.4 %copy.56 = s32[2,263,8,512]{3,2,0,1:T(8,128)} copy(s32[2,263,8,512]{3,2,1,0:T(8,128)} %bitcast.545) | data formatting | bytes 17235968 | tf_op jit(solution)/shard_map/reshape | solution.py:67
  13.2 0.5 subtract_convert_fusion.20.keep_ref
  13.7 18.2 %shard_map.59 = bf16[128,16,512]{2,1,0:T(8,128)(2,1)} custom-call(f32[16]{0:T(128)} %subtract_convert_fusion.20.keep_ref, f32[8,512]{1,0:T(8,128)} %fusion.70.window_ref, bf16[256,512]{1,0:T(8,128)(2,1)} %bitcast.567, s32[263,16,512]{2,1,0:T(8,128)} %bitcast.543), custom_call_target="tpu_custom_call" | custom-call | flops 1107296256 | bytes 10747904 | tf_op jit(solution)/shard_map/pallas_call | solution.py:71
  31.9 11.5 %all-to-all-start.1 = ((bf16[128,16,512]{2,1,0:T(8,128)(2,1)}), bf16[128,16,512]{2,1,0:T(8,128)(2,1)S(1)}, u32[]{:S(2)}, u32[]{:S(2)}) async-start(bf16[128,16,512]{2,1,0:T(8,128)(2,1)} %shard_map.59), calls=%async_computation.1 | async-start | bytes 4194304 | tf_op jit(solution)/shard_map/all_to_all | solution.py:212
  43.5 3.3 %rev.3 = bf16[32,2,2,16,512]{4,3,2,1,0:T(8,128)(2,1)} reverse(bf16[32,2,2,16,512]{4,3,2,1,0:T(8,128)(2,1)} %bitcast.544), dimensions={1} | reverse | bytes 4194304 | tf_op jit(solution)/shard_map/rev | solution.py:207
  46.7 1.0 fusion.163
  47.8 0.7 add_reduce_fusion.9
  49.1 0.6 pad_add_fusion.3.block_ref
  49.7 0.6 pad_add_fusion.2.block_ref
  50.3 0.6 pad_add_fusion.1.block_ref
  50.9 0.6 pad_add_fusion.block_ref
  51.6 21.4 %all-to-all-done.1 = bf16[128,16,512]{2,1,0:T(8,128)(2,1)S(1)} async-done(((bf16[128,16,512]{2,1,0:T(8,128)(2,1)}), bf16[128,16,512]{2,1,0:T(8,128)(2,1)S(1)}, u32[]{:S(2)}, u32[]{:S(2)}) %all-to-all-start.1) | async-done | bytes 2097184 | tf_op jit(solution)/shard_map/all_to_all | solution.py:212
  72.9 5.8 %all-to-all-start = ((bf16[128,16,512]{2,1,0:T(8,128)(2,1)}), bf16[128,16,512]{2,1,0:T(8,128)(2,1)}, u32[]{:S(2)}, u32[]{:S(2)}) async-start(bf16[128,16,512]{2,1,0:T(8,128)(2,1)} %bitcast.546), calls=%async_computation | async-start | bytes 4194304 | tf_op jit(solution)/shard_map/all_to_all | solution.py:212
  79.2 0.6 fusion.99
  80.0 0.4 fusion.12
  80.5 0.6 fusion.105
  81.2 0.6 add_reduce_fusion.8
  83.0 0.6 fusion.111
  83.7 0.6 add_reduce_fusion.7
  85.1 0.4 fusion.24
  85.6 0.6 fusion.117
  86.3 0.6 add_reduce_fusion.6
  88.1 0.6 fusion.123
  88.8 0.6 add_reduce_fusion.5
  90.7 0.6 fusion.129
  91.3 0.6 add_reduce_fusion.4
  93.2 0.6 fusion.135
  93.9 0.6 add_reduce_fusion.3
  95.8 0.6 fusion.141
  96.4 0.6 add_reduce_fusion.2
  98.3 0.6 add_reduce_fusion.1
  99.6 0.6 fusion.147
  100.3 0.6 add_reduce_fusion
  101.6 1.5 %collective-permute-start.1 = (bf16[128,16,512]{2,1,0:T(8,128)(2,1)S(1)}, bf16[128,16,512]{2,1,0:T(8,128)(2,1)}, u32[]{:S(2)}, u32[]{:S(2)}) collective-permute-start(bf16[128,16,512]{2,1,0:T(8,128)(2,1)S(1)} %all-to-all-done.1), channel_id=1, source_target_pairs={{0,1},{1,0},{2,3},{3,2},{4,5},{5,4},{6,7},{7,6},{8,9},{9,8},{10,11... | collective-permute-start | bytes 6291464 | tf_op jit(solution)/shard_map/ppermute | solution.py:220
  103.6 4.5 %all-to-all-done = bf16[128,16,512]{2,1,0:T(8,128)(2,1)} async-done(((bf16[128,16,512]{2,1,0:T(8,128)(2,1)}), bf16[128,16,512]{2,1,0:T(8,128)(2,1)}, u32[]{:S(2)}, u32[]{:S(2)}) %all-to-all-start) | async-done | bytes 2097184 | tf_op jit(solution)/shard_map/all_to_all | solution.py:212
  108.1 1.3 collective-permute-start
  109.4 0.6 fusion.153
  110.4 0.8 copy.50
  111.2 3.7 %all-to-all-start.2 = ((f32[2,128,1,16]{3,2,0,1:T(1,128)}), f32[2,128,1,16]{3,2,0,1:T(1,128)S(1)}, u32[]{:S(2)}, u32[]{:S(2)}) async-start(f32[2,128,1,16]{3,2,0,1:T(1,128)} %copy.50), calls=%async_computation.2 | async-start | bytes 262144 | tf_op jit(solution)/shard_map/all_to_all | solution.py:240
  114.9 6.7 %shard_map.60.prev_ref = bf16[2,4,512,2048]{3,2,1,0:T(8,128)(2,1)} custom-call(s32[2]{0:T(128)} %pad_add_fusion.3.block_ref, bf16[128,1,16,512]{3,2,1,0:T(8,128)(2,1)} %bitcast.541, bf16[128,1,16,512]{3,2,1,0:T(8,128)(2,1)} %bitcast.542), custom_call_target="tpu_custom_call" | custom-call | flops 2147483648 | bytes 6815744 | tf_op jit(solution)/shard_map/pallas_call | solution.py:185
  121.6 6.7 %shard_map.61.prev_ref = bf16[2,4,512,2048]{3,2,1,0:T(8,128)(2,1)} custom-call(s32[2]{0:T(128)} %pad_add_fusion.2.block_ref, bf16[128,1,16,512]{3,2,1,0:T(8,128)(2,1)} %bitcast.14.rows_ref.cols_ref, bf16[128,1,16,512]{3,2,1,0:T(8,128)(2,1)} %bitcast.14.rows_ref.cols_ref, bf16[2,4,512,2048]{3,2,1,0:T(8,128)(2,1)} %shard_map.60.prev_ref), custom_call_target="tpu_custom_call", output_to_operand_aliasing={{}: (3, {})} | custom-call | flops 2147483648 | bytes 6815744 | tf_op jit(solution)/shard_map/pallas_call | solution.py:185
  128.4 0.7 copy.53
  129.1 6.7 %shard_map.62.prev_ref = bf16[2,4,512,2048]{3,2,1,0:T(8,128)(2,1)} custom-call(s32[2]{0:T(128)} %pad_add_fusion.1.block_ref, bf16[128,1,16,512]{3,2,1,0:T(8,128)(2,1)} %bitcast.11.rows_ref.cols_ref, bf16[128,1,16,512]{3,2,1,0:T(8,128)(2,1)} %bitcast.11.rows_ref.cols_ref, bf16[2,4,512,2048]{3,2,1,0:T(8,128)(2,1)} %shard_map.61.prev_ref), custom_call_target="tpu_custom_call", output_to_operand_aliasing={{}: (3, {})} | custom-call | flops 2147483648 | bytes 6815744 | tf_op jit(solution)/shard_map/pallas_call | solution.py:185
  135.8 6.7 %shard_map.63 = bf16[2,4,512,2048]{3,2,1,0:T(8,128)(2,1)} custom-call(s32[2]{0:T(128)} %pad_add_fusion.block_ref, bf16[128,1,16,512]{3,2,1,0:T(8,128)(2,1)} %bitcast.9.rows_ref.cols_ref, bf16[128,1,16,512]{3,2,1,0:T(8,128)(2,1)} %bitcast.9.rows_ref.cols_ref, bf16[2,4,512,2048]{3,2,1,0:T(8,128)(2,1)} %shard_map.62.prev_ref), custom_call_target="tpu_custom_call", output_to_operand_aliasing={{}: (3, {})} | custom-call | flops 2147483648 | bytes 6815744 | tf_op jit(solution)/shard_map/pallas_call | solution.py:185
  (117 shorter events, 5.6 us)
Async XLA Ops:
  4.8 8.4 %copy-start.1 = (s32[16]{0:T(128)S(1)}, s32[16]{0:T(128)}, u32[]{:S(2)}) copy-start(s32[16]{0:T(128)} %param.5) | copy-start | bytes 196
  31.9 41.0 %all-to-all-start.1 = ((bf16[128,16,512]{2,1,0:T(8,128)(2,1)}), bf16[128,16,512]{2,1,0:T(8,128)(2,1)S(1)}, u32[]{:S(2)}, u32[]{:S(2)}) async-start(bf16[128,16,512]{2,1,0:T(8,128)(2,1)} %shard_map.59), calls=%async_computation.1 | async-start | bytes 4194304 | tf_op jit(solution)/shard_map/all_to_all | solution.py:212
  72.9 36.4 %copy-start = (bf16[128,16,512]{2,1,0:T(8,128)(2,1)}, bf16[128,16,512]{2,1,0:T(8,128)(2,1)S(1)}, u32[]{:S(2)}) copy-start(bf16[128,16,512]{2,1,0:T(8,128)(2,1)S(1)} %all-to-all-done.1) | copy-start | bytes 6291460
  72.9 35.1 %all-to-all-start = ((bf16[128,16,512]{2,1,0:T(8,128)(2,1)}), bf16[128,16,512]{2,1,0:T(8,128)(2,1)}, u32[]{:S(2)}, u32[]{:S(2)}) async-start(bf16[128,16,512]{2,1,0:T(8,128)(2,1)} %bitcast.546), calls=%async_computation | async-start | bytes 4194304 | tf_op jit(solution)/shard_map/all_to_all | solution.py:212
  101.6 27.5 %collective-permute-start.1 = (bf16[128,16,512]{2,1,0:T(8,128)(2,1)S(1)}, bf16[128,16,512]{2,1,0:T(8,128)(2,1)}, u32[]{:S(2)}, u32[]{:S(2)}) collective-permute-start(bf16[128,16,512]{2,1,0:T(8,128)(2,1)S(1)} %all-to-all-done.1), channel_id=1, source_target_pairs={{0,1},{1,0},{2,3},{3,2},{4,5},{5,4},{6,7},{7,6},{8,9},{9,8},{10,11... | collective-permute-start | bytes 6291464 | tf_op jit(solution)/shard_map/ppermute | solution.py:220
  108.1 27.7 %collective-permute-start = (bf16[128,16,512]{2,1,0:T(8,128)(2,1)}, bf16[128,16,512]{2,1,0:T(8,128)(2,1)}, u32[]{:S(2)}, u32[]{:S(2)}) collective-permute-start(bf16[128,16,512]{2,1,0:T(8,128)(2,1)} %all-to-all-done), channel_id=1, source_target_pairs={{0,1},{1,0},{2,3},{3,2},{4,5},{5,4},{6,7},{7,6},{8,9},{9,8},{10,11... | collective-permute-start | bytes 6291464 | tf_op jit(solution)/shard_map/ppermute | solution.py:228
  111.2 17.1 %all-to-all-start.2 = ((f32[2,128,1,16]{3,2,0,1:T(1,128)}), f32[2,128,1,16]{3,2,0,1:T(1,128)S(1)}, u32[]{:S(2)}, u32[]{:S(2)}) async-start(f32[2,128,1,16]{3,2,0,1:T(1,128)} %copy.50), calls=%async_computation.2 | async-start | bytes 262144 | tf_op jit(solution)/shard_map/all_to_all | solution.py:240

commit v15 on v13

--- a/solution.py
+++ b/solution.py
@@ -145,7 +145,7 @@
     correlate_kernel(block_ref, rows_ref, cols_ref, out_ref, turned_ref)
 
 
-def correlate(data, scalars, row_count, out=None, total_chans=None, col_block=512):
+def correlate(data, scalars, row_count, out=None, total_chans=None, col_block=1024):
     devices, chans, per, width = data.shape
     inputs = devices * per
     total_chans = chans if total_chans is None else total_chans

time: 143 us -> 141 us (0.986)
  Pallas kernels: 42.4 us -> 39.8 us
    pallas_call x4, Pallas kernels: 26.8 us -> 24.2 us  [correlate(): pl.pallas_call(kernel, grid_spec=spec, out_shape=jax.ShapeDtypeStruct((2,...]
  transfers between devices with their start and end apart: 5 -> 5, of which waited for: 2 -> 2; matrix products, arithmetic and copies ran while one was open for 19% -> 19% of each run, Pallas kernels for 14% -> 13%
where the time goes in v15:
time: 141 us; the launch traced here: 139 us
  Pallas kernels  39.8 us (28%)
  waiting for transfers between devices  25.9 us (18%)
  starting transfers between devices  23.9 us (17%)
  local copies, waits for them, and re-layouts  17.3 us (12%)
  other arithmetic  14 us (10%)
  matrix products  10.1 us (7%)
  between operations  7.99 us (6%)
    all_to_all x2, waiting for transfers between devices, turn(): lax.all_to_all(send, ('chan', 'blk'), split_axis=0, concat_axis=0, tiled=...  25.9 us
    pallas_call x4, Pallas kernels, correlate(): pl.pallas_call(kernel, grid_spec=spec, out_shape=jax.ShapeDtypeStruct((2,...  24.2 us
    all_to_all x2, starting transfers between devices, turn(): lax.all_to_all(send, ('chan', 'blk'), split_axis=0, concat_axis=0, tiled=...  17.3 us
    pallas_call x1, Pallas kernels, channelize(): pl.pallas_call(transform_kernel, grid=(count // group,), in_specs=[pl.Blo...  15.6 us
    reshape x1, local copies, waits for them, and re-layouts, channelize(): samples = voltages.reshape(count, SPECTRA + TAPS - 1, FRAME)  10.1 us
    dot_general x20, matrix products, exact_dot(): lax.dot_general(lhs, split3(rhs_f32), (dims, ((), ())), preferred_element...  10.1 us
    reduce_sum x10, other arithmetic, sweep(): power = jnp.sum(probe_re * probe_re + probe_im * probe_im)  6.27 us
    all_to_all x1, starting transfers between devices, shards(): lax.all_to_all(owners, ('chan', 'blk'), split_axis=1, concat_axis=1, tile...  3.75 us
  transfers between devices with their start and end apart: 5, of which 2 were waited for; matrix products, arithmetic and copies ran while one was open for 19% of the time, Pallas kernels for 13%

profile of v15, /device:TPU:1, one launch (start us, length us, event | category | flops | bytes accessed | tf_op | source)
XLA Modules:
  0.0 139.0 jit_solution(18300213275967479098)
XLA Ops:
  0.7 0.7 fusion.70.window_ref
  1.4 1.1 cosine_convert_fusion
  2.9 1.1 gather_fusion
  4.0 0.7 copy.41
  4.8 10.1 %reshape.490.samples_ref = s32[16,263,512]{2,1,0:T(8,128)} reshape(s32[16,134656]{1,0:T(8,128)} %param.4) | data formatting | bytes 17235968 | tf_op jit(solution)/shard_map/reshape | solution.py:56
  14.9 0.5 subtract_convert_fusion.20.keep_ref
  15.4 15.6 %shard_map.59 = bf16[128,16,512]{2,1,0:T(8,128)(2,1)} custom-call(f32[16]{0:T(128)} %subtract_convert_fusion.20.keep_ref, f32[8,512]{1,0:T(8,128)} %fusion.70.window_ref, bf16[256,512]{1,0:T(8,128)(2,1)} %bitcast.558, s32[16,263,512]{2,1,0:T(8,128)} %reshape.490.samples_ref), custom_call_target="tpu_custom_call" | custom-call | flops 1107296256 | bytes 10747904 | tf_op jit(solution)/shard_map/pallas_call | solution.py:60
  31.0 11.5 %all-to-all-start.1 = ((bf16[128,16,512]{2,1,0:T(8,128)(2,1)}), bf16[128,16,512]{2,1,0:T(8,128)(2,1)S(1)}, u32[]{:S(2)}, u32[]{:S(2)}) async-start(bf16[128,16,512]{2,1,0:T(8,128)(2,1)} %shard_map.59), calls=%async_computation.1 | async-start | bytes 4194304 | tf_op jit(solution)/shard_map/all_to_all | solution.py:201
  42.6 3.3 %rev.3 = bf16[32,2,2,16,512]{4,3,2,1,0:T(8,128)(2,1)} reverse(bf16[32,2,2,16,512]{4,3,2,1,0:T(8,128)(2,1)} %bitcast.536), dimensions={1} | reverse | bytes 4194304 | tf_op jit(solution)/shard_map/rev | solution.py:196
  45.8 1.0 fusion.163
  46.9 0.7 add_reduce_fusion.9
  48.2 0.6 pad_add_fusion.3.block_ref
  48.8 0.6 pad_add_fusion.2.block_ref
  49.4 0.6 pad_add_fusion.1.block_ref
  50.0 0.6 pad_add_fusion.block_ref
  50.7 21.4 %all-to-all-done.1 = bf16[128,16,512]{2,1,0:T(8,128)(2,1)S(1)} async-done(((bf16[128,16,512]{2,1,0:T(8,128)(2,1)}), bf16[128,16,512]{2,1,0:T(8,128)(2,1)S(1)}, u32[]{:S(2)}, u32[]{:S(2)}) %all-to-all-start.1) | async-done | bytes 2097184 | tf_op jit(solution)/shard_map/all_to_all | solution.py:201
  72.1 5.8 %all-to-all-start = ((bf16[128,16,512]{2,1,0:T(8,128)(2,1)}), bf16[128,16,512]{2,1,0:T(8,128)(2,1)}, u32[]{:S(2)}, u32[]{:S(2)}) async-start(bf16[128,16,512]{2,1,0:T(8,128)(2,1)} %bitcast.537), calls=%async_computation | async-start | bytes 4194304 | tf_op jit(solution)/shard_map/all_to_all | solution.py:201
  78.3 0.6 fusion.99
  79.2 0.4 fusion.12
  79.6 0.6 fusion.105
  80.3 0.6 add_reduce_fusion.8
  81.7 0.4 fusion.18
  82.1 0.6 fusion.111
  82.8 0.6 add_reduce_fusion.7
  84.7 0.6 fusion.117
  85.4 0.6 add_reduce_fusion.6
  87.2 0.6 fusion.123
  87.9 0.6 add_reduce_fusion.5
  89.8 0.6 fusion.129
  90.5 0.6 add_reduce_fusion.4
  92.3 0.6 fusion.135
  93.0 0.6 add_reduce_fusion.3
  94.9 0.6 fusion.141
  95.5 0.6 add_reduce_fusion.2
  97.4 0.6 add_reduce_fusion.1
  98.7 0.6 fusion.147
  99.4 0.6 add_reduce_fusion
  100.7 1.5 %collective-permute-start.1 = (bf16[128,16,512]{2,1,0:T(8,128)(2,1)S(1)}, bf16[128,16,512]{2,1,0:T(8,128)(2,1)}, u32[]{:S(2)}, u32[]{:S(2)}) collective-permute-start(bf16[128,16,512]{2,1,0:T(8,128)(2,1)S(1)} %all-to-all-done.1), channel_id=1, source_target_pairs={{0,1},{1,0},{2,3},{3,2},{4,5},{5,4},{6,7},{7,6},{8,9},{9,8},{10,11... | collective-permute-start | bytes 6291464 | tf_op jit(solution)/shard_map/ppermute | solution.py:209
  102.7 4.5 %all-to-all-done = bf16[128,16,512]{2,1,0:T(8,128)(2,1)} async-done(((bf16[128,16,512]{2,1,0:T(8,128)(2,1)}), bf16[128,16,512]{2,1,0:T(8,128)(2,1)}, u32[]{:S(2)}, u32[]{:S(2)}) %all-to-all-start) | async-done | bytes 2097184 | tf_op jit(solution)/shard_map/all_to_all | solution.py:201
  107.2 1.3 collective-permute-start
  108.5 0.6 fusion.153
  109.5 0.8 copy.46
  110.3 3.8 %all-to-all-start.2 = ((f32[2,128,1,16]{3,2,0,1:T(1,128)}), f32[2,128,1,16]{3,2,0,1:T(1,128)S(1)}, u32[]{:S(2)}, u32[]{:S(2)}) async-start(f32[2,128,1,16]{3,2,0,1:T(1,128)} %copy.46), calls=%async_computation.2 | async-start | bytes 262144 | tf_op jit(solution)/shard_map/all_to_all | solution.py:229
  114.0 6.1 %shard_map.60.prev_ref = bf16[2,4,512,2048]{3,2,1,0:T(8,128)(2,1)} custom-call(s32[2]{0:T(128)} %pad_add_fusion.3.block_ref, bf16[128,1,16,512]{3,2,1,0:T(8,128)(2,1)} %bitcast.534, bf16[128,1,16,512]{3,2,1,0:T(8,128)(2,1)} %bitcast.535), custom_call_target="tpu_custom_call" | custom-call | flops 2147483648 | bytes 6815744 | tf_op jit(solution)/shard_map/pallas_call | solution.py:174
  120.1 6.1 %shard_map.61.prev_ref = bf16[2,4,512,2048]{3,2,1,0:T(8,128)(2,1)} custom-call(s32[2]{0:T(128)} %pad_add_fusion.2.block_ref, bf16[128,1,16,512]{3,2,1,0:T(8,128)(2,1)} %bitcast.13.rows_ref.cols_ref, bf16[128,1,16,512]{3,2,1,0:T(8,128)(2,1)} %bitcast.13.rows_ref.cols_ref, bf16[2,4,512,2048]{3,2,1,0:T(8,128)(2,1)} %shard_map.60.prev_ref), custom_call_target="tpu_custom_call", output_to_operand_aliasing={{}: (3, {})} | custom-call | flops 2147483648 | bytes 6815744 | tf_op jit(solution)/shard_map/pallas_call | solution.py:174
  126.2 0.7 copy.49
  126.9 6.1 %shard_map.62.prev_ref = bf16[2,4,512,2048]{3,2,1,0:T(8,128)(2,1)} custom-call(s32[2]{0:T(128)} %pad_add_fusion.1.block_ref, bf16[128,1,16,512]{3,2,1,0:T(8,128)(2,1)} %bitcast.10.rows_ref.cols_ref, bf16[128,1,16,512]{3,2,1,0:T(8,128)(2,1)} %bitcast.10.rows_ref.cols_ref, bf16[2,4,512,2048]{3,2,1,0:T(8,128)(2,1)} %shard_map.61.prev_ref), custom_call_target="tpu_custom_call", output_to_operand_aliasing={{}: (3, {})} | custom-call | flops 2147483648 | bytes 6815744 | tf_op jit(solution)/shard_map/pallas_call | solution.py:174
  133.0 6.1 %shard_map.63 = bf16[2,4,512,2048]{3,2,1,0:T(8,128)(2,1)} custom-call(s32[2]{0:T(128)} %pad_add_fusion.block_ref, bf16[128,1,16,512]{3,2,1,0:T(8,128)(2,1)} %bitcast.8.rows_ref.cols_ref, bf16[128,1,16,512]{3,2,1,0:T(8,128)(2,1)} %bitcast.8.rows_ref.cols_ref, bf16[2,4,512,2048]{3,2,1,0:T(8,128)(2,1)} %shard_map.62.prev_ref), custom_call_target="tpu_custom_call", output_to_operand_aliasing={{}: (3, {})} | custom-call | flops 2147483648 | bytes 6815744 | tf_op jit(solution)/shard_map/pallas_call | solution.py:174
  (117 shorter events, 5.6 us)
Async XLA Ops:
  4.8 10.2 %copy-start.1 = (s32[16]{0:T(128)S(1)}, s32[16]{0:T(128)}, u32[]{:S(2)}) copy-start(s32[16]{0:T(128)} %param.5) | copy-start | bytes 196
  31.0 41.0 %all-to-all-start.1 = ((bf16[128,16,512]{2,1,0:T(8,128)(2,1)}), bf16[128,16,512]{2,1,0:T(8,128)(2,1)S(1)}, u32[]{:S(2)}, u32[]{:S(2)}) async-start(bf16[128,16,512]{2,1,0:T(8,128)(2,1)} %shard_map.59), calls=%async_computation.1 | async-start | bytes 4194304 | tf_op jit(solution)/shard_map/all_to_all | solution.py:201
  72.1 36.4 %copy-start = (bf16[128,16,512]{2,1,0:T(8,128)(2,1)}, bf16[128,16,512]{2,1,0:T(8,128)(2,1)S(1)}, u32[]{:S(2)}) copy-start(bf16[128,16,512]{2,1,0:T(8,128)(2,1)S(1)} %all-to-all-done.1) | copy-start | bytes 6291460
  72.1 35.1 %all-to-all-start = ((bf16[128,16,512]{2,1,0:T(8,128)(2,1)}), bf16[128,16,512]{2,1,0:T(8,128)(2,1)}, u32[]{:S(2)}, u32[]{:S(2)}) async-start(bf16[128,16,512]{2,1,0:T(8,128)(2,1)} %bitcast.537), calls=%async_computation | async-start | bytes 4194304 | tf_op jit(solution)/shard_map/all_to_all | solution.py:201
  100.7 26.2 %collective-permute-start.1 = (bf16[128,16,512]{2,1,0:T(8,128)(2,1)S(1)}, bf16[128,16,512]{2,1,0:T(8,128)(2,1)}, u32[]{:S(2)}, u32[]{:S(2)}) collective-permute-start(bf16[128,16,512]{2,1,0:T(8,128)(2,1)S(1)} %all-to-all-done.1), channel_id=1, source_target_pairs={{0,1},{1,0},{2,3},{3,2},{4,5},{5,4},{6,7},{7,6},{8,9},{9,8},{10,11... | collective-permute-start | bytes 6291464 | tf_op jit(solution)/shard_map/ppermute | solution.py:209
  107.2 25.8 %collective-permute-start = (bf16[128,16,512]{2,1,0:T(8,128)(2,1)}, bf16[128,16,512]{2,1,0:T(8,128)(2,1)}, u32[]{:S(2)}, u32[]{:S(2)}) collective-permute-start(bf16[128,16,512]{2,1,0:T(8,128)(2,1)} %all-to-all-done), channel_id=1, source_target_pairs={{0,1},{1,0},{2,3},{3,2},{4,5},{5,4},{6,7},{7,6},{8,9},{9,8},{10,11... | collective-permute-start | bytes 6291464 | tf_op jit(solution)/shard_map/ppermute | solution.py:217
  110.3 15.9 %all-to-all-start.2 = ((f32[2,128,1,16]{3,2,0,1:T(1,128)}), f32[2,128,1,16]{3,2,0,1:T(1,128)S(1)}, u32[]{:S(2)}, u32[]{:S(2)}) async-start(f32[2,128,1,16]{3,2,0,1:T(1,128)} %copy.46), calls=%async_computation.2 | async-start | bytes 262144 | tf_op jit(solution)/shard_map/all_to_all | solution.py:229

commit v16 on v15

--- a/solution.py
+++ b/solution.py
@@ -145,7 +145,7 @@
     correlate_kernel(block_ref, rows_ref, cols_ref, out_ref, turned_ref)
 
 
-def correlate(data, scalars, row_count, out=None, total_chans=None, col_block=1024):
+def correlate(data, scalars, row_count, out=None, total_chans=None, col_block=2048):
     devices, chans, per, width = data.shape
     inputs = devices * per
     total_chans = chans if total_chans is None else total_chans

time: 141 us -> 143 us (1.014)
  Pallas kernels: 39.8 us -> 42.9 us
    pallas_call x4, Pallas kernels: 24.2 us -> 27.3 us  [correlate(): pl.pallas_call(kernel, grid_spec=spec, out_shape=jax.ShapeDtypeStruct((2,...]
  transfers between devices with their start and end apart: 5 -> 5, of which waited for: 2 -> 2; matrix products, arithmetic and copies ran while one was open for 19% -> 19% of each run, Pallas kernels for 13% -> 14%
where the time goes in v16:
time: 143 us; the launch traced here: 142 us
  Pallas kernels  42.9 us (30%)
  waiting for transfers between devices  25.9 us (18%)
  starting transfers between devices  23.9 us (17%)
  local copies, waits for them, and re-layouts  17.3 us (12%)
  other arithmetic  14 us (10%)
  matrix products  10.1 us (7%)
  between operations  7.99 us (6%)
    pallas_call x4, Pallas kernels, correlate(): pl.pallas_call(kernel, grid_spec=spec, out_shape=jax.ShapeDtypeStruct((2,...  27.3 us
    all_to_all x2, waiting for transfers between devices, turn(): lax.all_to_all(send, ('chan', 'blk'), split_axis=0, concat_axis=0, tiled=...  25.9 us
    all_to_all x2, starting transfers between devices, turn(): lax.all_to_all(send, ('chan', 'blk'), split_axis=0, concat_axis=0, tiled=...  17.3 us
    pallas_call x1, Pallas kernels, channelize(): pl.pallas_call(transform_kernel, grid=(count // group,), in_specs=[pl.Blo...  15.6 us
    reshape x1, local copies, waits for them, and re-layouts, channelize(): samples = voltages.reshape(count, SPECTRA + TAPS - 1, FRAME)  10.1 us
    dot_general x20, matrix products, exact_dot(): lax.dot_general(lhs, split3(rhs_f32), (dims, ((), ())), preferred_element...  10.1 us
    reduce_sum x10, other arithmetic, sweep(): power = jnp.sum(probe_re * probe_re + probe_im * probe_im)  6.27 us
    all_to_all x1, starting transfers between devices, shards(): lax.all_to_all(owners, ('chan', 'blk'), split_axis=1, concat_axis=1, tile...  3.75 us
  transfers between devices with their start and end apart: 5, of which 2 were waited for; matrix products, arithmetic and copies ran while one was open for 19% of the time, Pallas kernels for 14%

profile of v16, /device:TPU:1, one launch (start us, length us, event | category | flops | bytes accessed | tf_op | source)
XLA Modules:
  0.0 142.1 jit_solution(868250884294780187)
XLA Ops:
  0.7 0.7 fusion.70.window_ref
  1.4 1.1 cosine_convert_fusion
  2.9 1.1 gather_fusion
  4.0 0.7 copy.41
  4.8 10.1 %reshape.490.samples_ref = s32[16,263,512]{2,1,0:T(8,128)} reshape(s32[16,134656]{1,0:T(8,128)} %param.4) | data formatting | bytes 17235968 | tf_op jit(solution)/shard_map/reshape | solution.py:56
  14.9 0.5 subtract_convert_fusion.20.keep_ref
  15.4 15.6 %shard_map.59 = bf16[128,16,512]{2,1,0:T(8,128)(2,1)} custom-call(f32[16]{0:T(128)} %subtract_convert_fusion.20.keep_ref, f32[8,512]{1,0:T(8,128)} %fusion.70.window_ref, bf16[256,512]{1,0:T(8,128)(2,1)} %bitcast.558, s32[16,263,512]{2,1,0:T(8,128)} %reshape.490.samples_ref), custom_call_target="tpu_custom_call" | custom-call | flops 1107296256 | bytes 10747904 | tf_op jit(solution)/shard_map/pallas_call | solution.py:60
  31.0 11.5 %all-to-all-start.1 = ((bf16[128,16,512]{2,1,0:T(8,128)(2,1)}), bf16[128,16,512]{2,1,0:T(8,128)(2,1)S(1)}, u32[]{:S(2)}, u32[]{:S(2)}) async-start(bf16[128,16,512]{2,1,0:T(8,128)(2,1)} %shard_map.59), calls=%async_computation.1 | async-start | bytes 4194304 | tf_op jit(solution)/shard_map/all_to_all | solution.py:201
  42.6 3.3 %rev.3 = bf16[32,2,2,16,512]{4,3,2,1,0:T(8,128)(2,1)} reverse(bf16[32,2,2,16,512]{4,3,2,1,0:T(8,128)(2,1)} %bitcast.536), dimensions={1} | reverse | bytes 4194304 | tf_op jit(solution)/shard_map/rev | solution.py:196
  45.8 1.0 fusion.163
  46.9 0.7 add_reduce_fusion.9
  48.2 0.6 pad_add_fusion.3.block_ref
  48.8 0.6 pad_add_fusion.2.block_ref
  49.4 0.6 pad_add_fusion.1.block_ref
  50.0 0.6 pad_add_fusion.block_ref
  50.7 21.4 %all-to-all-done.1 = bf16[128,16,512]{2,1,0:T(8,128)(2,1)S(1)} async-done(((bf16[128,16,512]{2,1,0:T(8,128)(2,1)}), bf16[128,16,512]{2,1,0:T(8,128)(2,1)S(1)}, u32[]{:S(2)}, u32[]{:S(2)}) %all-to-all-start.1) | async-done | bytes 2097184 | tf_op jit(solution)/shard_map/all_to_all | solution.py:201
  72.1 5.8 %all-to-all-start = ((bf16[128,16,512]{2,1,0:T(8,128)(2,1)}), bf16[128,16,512]{2,1,0:T(8,128)(2,1)}, u32[]{:S(2)}, u32[]{:S(2)}) async-start(bf16[128,16,512]{2,1,0:T(8,128)(2,1)} %bitcast.537), calls=%async_computation | async-start | bytes 4194304 | tf_op jit(solution)/shard_map/all_to_all | solution.py:201
  78.3 0.6 fusion.99
  79.2 0.4 fusion.12
  79.6 0.6 fusion.105
  80.3 0.6 add_reduce_fusion.8
  81.7 0.4 fusion.18
  82.1 0.6 fusion.111
  82.8 0.6 add_reduce_fusion.7
  84.7 0.6 fusion.117
  85.4 0.6 add_reduce_fusion.6
  87.2 0.6 fusion.123
  87.9 0.6 add_reduce_fusion.5
  89.8 0.6 fusion.129
  90.5 0.6 add_reduce_fusion.4
  92.3 0.6 fusion.135
  93.0 0.6 add_reduce_fusion.3
  94.9 0.6 fusion.141
  95.5 0.6 add_reduce_fusion.2
  97.4 0.6 add_reduce_fusion.1
  98.7 0.6 fusion.147
  99.4 0.6 add_reduce_fusion
  100.7 1.5 %collective-permute-start.1 = (bf16[128,16,512]{2,1,0:T(8,128)(2,1)S(1)}, bf16[128,16,512]{2,1,0:T(8,128)(2,1)}, u32[]{:S(2)}, u32[]{:S(2)}) collective-permute-start(bf16[128,16,512]{2,1,0:T(8,128)(2,1)S(1)} %all-to-all-done.1), channel_id=1, source_target_pairs={{0,1},{1,0},{2,3},{3,2},{4,5},{5,4},{6,7},{7,6},{8,9},{9,8},{10,11... | collective-permute-start | bytes 6291464 | tf_op jit(solution)/shard_map/ppermute | solution.py:209
  102.7 4.5 %all-to-all-done = bf16[128,16,512]{2,1,0:T(8,128)(2,1)} async-done(((bf16[128,16,512]{2,1,0:T(8,128)(2,1)}), bf16[128,16,512]{2,1,0:T(8,128)(2,1)}, u32[]{:S(2)}, u32[]{:S(2)}) %all-to-all-start) | async-done | bytes 2097184 | tf_op jit(solution)/shard_map/all_to_all | solution.py:201
  107.2 1.3 collective-permute-start
  108.5 0.6 fusion.153
  109.5 0.8 copy.46
  110.3 3.8 %all-to-all-start.2 = ((f32[2,128,1,16]{3,2,0,1:T(1,128)}), f32[2,128,1,16]{3,2,0,1:T(1,128)S(1)}, u32[]{:S(2)}, u32[]{:S(2)}) async-start(f32[2,128,1,16]{3,2,0,1:T(1,128)} %copy.46), calls=%async_computation.2 | async-start | bytes 262144 | tf_op jit(solution)/shard_map/all_to_all | solution.py:229
  114.0 6.8 %shard_map.60.prev_ref = bf16[2,4,512,2048]{3,2,1,0:T(8,128)(2,1)} custom-call(s32[2]{0:T(128)} %pad_add_fusion.3.block_ref, bf16[128,1,16,512]{3,2,1,0:T(8,128)(2,1)} %bitcast.534, bf16[128,1,16,512]{3,2,1,0:T(8,128)(2,1)} %bitcast.535), custom_call_target="tpu_custom_call" | custom-call | flops 2147483648 | bytes 6815744 | tf_op jit(solution)/shard_map/pallas_call | solution.py:174
  120.9 6.8 %shard_map.61.prev_ref = bf16[2,4,512,2048]{3,2,1,0:T(8,128)(2,1)} custom-call(s32[2]{0:T(128)} %pad_add_fusion.2.block_ref, bf16[128,1,16,512]{3,2,1,0:T(8,128)(2,1)} %bitcast.13.rows_ref.cols_ref, bf16[128,1,16,512]{3,2,1,0:T(8,128)(2,1)} %bitcast.13.rows_ref.cols_ref, bf16[2,4,512,2048]{3,2,1,0:T(8,128)(2,1)} %shard_map.60.prev_ref), custom_call_target="tpu_custom_call", output_to_operand_aliasing={{}: (3, {})} | custom-call | flops 2147483648 | bytes 6815744 | tf_op jit(solution)/shard_map/pallas_call | solution.py:174
  127.8 0.7 copy.49
  128.5 6.8 %shard_map.62.prev_ref = bf16[2,4,512,2048]{3,2,1,0:T(8,128)(2,1)} custom-call(s32[2]{0:T(128)} %pad_add_fusion.1.block_ref, bf16[128,1,16,512]{3,2,1,0:T(8,128)(2,1)} %bitcast.10.rows_ref.cols_ref, bf16[128,1,16,512]{3,2,1,0:T(8,128)(2,1)} %bitcast.10.rows_ref.cols_ref, bf16[2,4,512,2048]{3,2,1,0:T(8,128)(2,1)} %shard_map.61.prev_ref), custom_call_target="tpu_custom_call", output_to_operand_aliasing={{}: (3, {})} | custom-call | flops 2147483648 | bytes 6815744 | tf_op jit(solution)/shard_map/pallas_call | solution.py:174
  135.3 6.8 %shard_map.63 = bf16[2,4,512,2048]{3,2,1,0:T(8,128)(2,1)} custom-call(s32[2]{0:T(128)} %pad_add_fusion.block_ref, bf16[128,1,16,512]{3,2,1,0:T(8,128)(2,1)} %bitcast.8.rows_ref.cols_ref, bf16[128,1,16,512]{3,2,1,0:T(8,128)(2,1)} %bitcast.8.rows_ref.cols_ref, bf16[2,4,512,2048]{3,2,1,0:T(8,128)(2,1)} %shard_map.62.prev_ref), custom_call_target="tpu_custom_call", output_to_operand_aliasing={{}: (3, {})} | custom-call | flops 2147483648 | bytes 6815744 | tf_op jit(solution)/shard_map/pallas_call | solution.py:174
  (117 shorter events, 5.6 us)
Async XLA Ops:
  4.8 10.2 %copy-start.1 = (s32[16]{0:T(128)S(1)}, s32[16]{0:T(128)}, u32[]{:S(2)}) copy-start(s32[16]{0:T(128)} %param.5) | copy-start | bytes 196
  31.0 41.0 %all-to-all-start.1 = ((bf16[128,16,512]{2,1,0:T(8,128)(2,1)}), bf16[128,16,512]{2,1,0:T(8,128)(2,1)S(1)}, u32[]{:S(2)}, u32[]{:S(2)}) async-start(bf16[128,16,512]{2,1,0:T(8,128)(2,1)} %shard_map.59), calls=%async_computation.1 | async-start | bytes 4194304 | tf_op jit(solution)/shard_map/all_to_all | solution.py:201
  72.1 36.4 %copy-start = (bf16[128,16,512]{2,1,0:T(8,128)(2,1)}, bf16[128,16,512]{2,1,0:T(8,128)(2,1)S(1)}, u32[]{:S(2)}) copy-start(bf16[128,16,512]{2,1,0:T(8,128)(2,1)S(1)} %all-to-all-done.1) | copy-start | bytes 6291460
  72.1 35.1 %all-to-all-start = ((bf16[128,16,512]{2,1,0:T(8,128)(2,1)}), bf16[128,16,512]{2,1,0:T(8,128)(2,1)}, u32[]{:S(2)}, u32[]{:S(2)}) async-start(bf16[128,16,512]{2,1,0:T(8,128)(2,1)} %bitcast.537), calls=%async_computation | async-start | bytes 4194304 | tf_op jit(solution)/shard_map/all_to_all | solution.py:201
  100.7 27.8 %collective-permute-start.1 = (bf16[128,16,512]{2,1,0:T(8,128)(2,1)S(1)}, bf16[128,16,512]{2,1,0:T(8,128)(2,1)}, u32[]{:S(2)}, u32[]{:S(2)}) collective-permute-start(bf16[128,16,512]{2,1,0:T(8,128)(2,1)S(1)} %all-to-all-done.1), channel_id=1, source_target_pairs={{0,1},{1,0},{2,3},{3,2},{4,5},{5,4},{6,7},{7,6},{8,9},{9,8},{10,11... | collective-permute-start | bytes 6291464 | tf_op jit(solution)/shard_map/ppermute | solution.py:209
  107.2 28.1 %collective-permute-start = (bf16[128,16,512]{2,1,0:T(8,128)(2,1)}, bf16[128,16,512]{2,1,0:T(8,128)(2,1)}, u32[]{:S(2)}, u32[]{:S(2)}) collective-permute-start(bf16[128,16,512]{2,1,0:T(8,128)(2,1)} %all-to-all-done), channel_id=1, source_target_pairs={{0,1},{1,0},{2,3},{3,2},{4,5},{5,4},{6,7},{7,6},{8,9},{9,8},{10,11... | collective-permute-start | bytes 6291464 | tf_op jit(solution)/shard_map/ppermute | solution.py:217
  110.3 17.4 %all-to-all-start.2 = ((f32[2,128,1,16]{3,2,0,1:T(1,128)}), f32[2,128,1,16]{3,2,0,1:T(1,128)S(1)}, u32[]{:S(2)}, u32[]{:S(2)}) async-start(f32[2,128,1,16]{3,2,0,1:T(1,128)} %copy.46), calls=%async_computation.2 | async-start | bytes 262144 | tf_op jit(solution)/shard_map/all_to_all | solution.py:229

commit v17 on v15

--- a/solution.py
+++ b/solution.py
@@ -36,10 +36,11 @@
     base = pl.program_id(0) * group
     scale = 1.0 / (64.0 * math.sqrt(FRAME))
     for item in range(group):
-        wide_ref[0 : SPECTRA + TAPS - 1, :] = samples_ref[item].astype(jnp.float32)
-        frames = window_ref[0:1, :] * wide_ref[0:SPECTRA, :]
+        frames = window_ref[0:1, :] * samples_ref[item, 0:SPECTRA, :].astype(jnp.float32)
         for tap in range(1, TAPS):
-            frames = frames + window_ref[tap : tap + 1, :] * wide_ref[tap : tap + SPECTRA, :]
+            frames = frames + window_ref[tap : tap + 1, :] * samples_ref[
+                item, tap : tap + SPECTRA, :
+            ].astype(jnp.float32)
         result = lax.dot_general(
             table_ref[...], frames.astype(jnp.bfloat16), (((1,), (1,)), ((), ())),
             preferred_element_type=jnp.float32,

time: 141 us -> 141 us (level)
  no operation moved by 1% of the time
where the time goes in v17:
time: 141 us; the launch traced here: 139 us
  Pallas kernels  40.3 us (29%)
  waiting for transfers between devices  25.9 us (18%)
  starting transfers between devices  23.9 us (17%)
  local copies, waits for them, and re-layouts  17.3 us (12%)
  other arithmetic  14 us (10%)
  matrix products  10.1 us (7%)
  between operations  7.99 us (6%)
    all_to_all x2, waiting for transfers between devices, turn(): lax.all_to_all(send, ('chan', 'blk'), split_axis=0, concat_axis=0, tiled=...  25.9 us
    pallas_call x4, Pallas kernels, correlate(): pl.pallas_call(kernel, grid_spec=spec, out_shape=jax.ShapeDtypeStruct((2,...  24.2 us
    all_to_all x2, starting transfers between devices, turn(): lax.all_to_all(send, ('chan', 'blk'), split_axis=0, concat_axis=0, tiled=...  17.3 us
    pallas_call x1, Pallas kernels, channelize(): pl.pallas_call(transform_kernel, grid=(count // group,), in_specs=[pl.Blo...  16.1 us
    reshape x1, local copies, waits for them, and re-layouts, channelize(): samples = voltages.reshape(count, SPECTRA + TAPS - 1, FRAME)  10.1 us
    dot_general x20, matrix products, exact_dot(): lax.dot_general(lhs, split3(rhs_f32), (dims, ((), ())), preferred_element...  10.1 us
    reduce_sum x10, other arithmetic, sweep(): power = jnp.sum(probe_re * probe_re + probe_im * probe_im)  6.27 us
    all_to_all x1, starting transfers between devices, shards(): lax.all_to_all(owners, ('chan', 'blk'), split_axis=1, concat_axis=1, tile...  3.75 us
  transfers between devices with their start and end apart: 5, of which 2 were waited for; matrix products, arithmetic and copies ran while one was open for 19% of the time, Pallas kernels for 13%

profile of v17, /device:TPU:1, one launch (start us, length us, event | category | flops | bytes accessed | tf_op | source)
XLA Modules:
  0.0 139.5 jit_solution(15968495274845522200)
XLA Ops:
  0.7 0.7 fusion.70.window_ref
  1.4 1.1 cosine_convert_fusion
  2.9 1.1 gather_fusion
  4.0 0.7 copy.41
  4.8 10.1 %reshape.490.samples_ref = s32[16,263,512]{2,1,0:T(8,128)} reshape(s32[16,134656]{1,0:T(8,128)} %param.4) | data formatting | bytes 17235968 | tf_op jit(solution)/shard_map/reshape | solution.py:57
  14.9 0.5 subtract_convert_fusion.20.keep_ref
  15.4 16.1 %shard_map.59 = bf16[128,16,512]{2,1,0:T(8,128)(2,1)} custom-call(f32[16]{0:T(128)} %subtract_convert_fusion.20.keep_ref, f32[8,512]{1,0:T(8,128)} %fusion.70.window_ref, bf16[256,512]{1,0:T(8,128)(2,1)} %bitcast.558, s32[16,263,512]{2,1,0:T(8,128)} %reshape.490.samples_ref), custom_call_target="tpu_custom_call" | custom-call | flops 1107296256 | bytes 10747904 | tf_op jit(solution)/shard_map/pallas_call | solution.py:61
  31.5 11.5 %all-to-all-start.1 = ((bf16[128,16,512]{2,1,0:T(8,128)(2,1)}), bf16[128,16,512]{2,1,0:T(8,128)(2,1)S(1)}, u32[]{:S(2)}, u32[]{:S(2)}) async-start(bf16[128,16,512]{2,1,0:T(8,128)(2,1)} %shard_map.59), calls=%async_computation.1 | async-start | bytes 4194304 | tf_op jit(solution)/shard_map/all_to_all | solution.py:202
  43.0 3.3 %rev.3 = bf16[32,2,2,16,512]{4,3,2,1,0:T(8,128)(2,1)} reverse(bf16[32,2,2,16,512]{4,3,2,1,0:T(8,128)(2,1)} %bitcast.536), dimensions={1} | reverse | bytes 4194304 | tf_op jit(solution)/shard_map/rev | solution.py:197
  46.3 1.0 fusion.163
  47.3 0.7 add_reduce_fusion.9
  48.7 0.6 pad_add_fusion.3.block_ref
  49.3 0.6 pad_add_fusion.2.block_ref
  49.8 0.6 pad_add_fusion.1.block_ref
  50.4 0.6 pad_add_fusion.block_ref
  51.1 21.4 %all-to-all-done.1 = bf16[128,16,512]{2,1,0:T(8,128)(2,1)S(1)} async-done(((bf16[128,16,512]{2,1,0:T(8,128)(2,1)}), bf16[128,16,512]{2,1,0:T(8,128)(2,1)S(1)}, u32[]{:S(2)}, u32[]{:S(2)}) %all-to-all-start.1) | async-done | bytes 2097184 | tf_op jit(solution)/shard_map/all_to_all | solution.py:202
  72.5 5.8 %all-to-all-start = ((bf16[128,16,512]{2,1,0:T(8,128)(2,1)}), bf16[128,16,512]{2,1,0:T(8,128)(2,1)}, u32[]{:S(2)}, u32[]{:S(2)}) async-start(bf16[128,16,512]{2,1,0:T(8,128)(2,1)} %bitcast.537), calls=%async_computation | async-start | bytes 4194304 | tf_op jit(solution)/shard_map/all_to_all | solution.py:202
  78.8 0.6 fusion.99
  79.6 0.4 fusion.12
  80.0 0.6 fusion.105
  80.7 0.6 add_reduce_fusion.8
  82.1 0.4 fusion.18
  82.6 0.6 fusion.111
  83.3 0.6 add_reduce_fusion.7
  85.1 0.6 fusion.117
  85.8 0.6 add_reduce_fusion.6
  87.7 0.6 fusion.123
  88.4 0.6 add_reduce_fusion.5
  90.2 0.6 fusion.129
  90.9 0.6 add_reduce_fusion.4
  92.8 0.6 fusion.135
  93.4 0.6 add_reduce_fusion.3
  95.3 0.6 fusion.141
  96.0 0.6 add_reduce_fusion.2
  97.9 0.6 add_reduce_fusion.1
  99.1 0.6 fusion.147
  99.9 0.6 add_reduce_fusion
  101.1 1.5 %collective-permute-start.1 = (bf16[128,16,512]{2,1,0:T(8,128)(2,1)S(1)}, bf16[128,16,512]{2,1,0:T(8,128)(2,1)}, u32[]{:S(2)}, u32[]{:S(2)}) collective-permute-start(bf16[128,16,512]{2,1,0:T(8,128)(2,1)S(1)} %all-to-all-done.1), channel_id=1, source_target_pairs={{0,1},{1,0},{2,3},{3,2},{4,5},{5,4},{6,7},{7,6},{8,9},{9,8},{10,11... | collective-permute-start | bytes 6291464 | tf_op jit(solution)/shard_map/ppermute | solution.py:210
  103.1 4.5 %all-to-all-done = bf16[128,16,512]{2,1,0:T(8,128)(2,1)} async-done(((bf16[128,16,512]{2,1,0:T(8,128)(2,1)}), bf16[128,16,512]{2,1,0:T(8,128)(2,1)}, u32[]{:S(2)}, u32[]{:S(2)}) %all-to-all-start) | async-done | bytes 2097184 | tf_op jit(solution)/shard_map/all_to_all | solution.py:202
  107.6 1.3 collective-permute-start
  109.0 0.6 fusion.153
  109.9 0.8 copy.46
  110.7 3.8 %all-to-all-start.2 = ((f32[2,128,1,16]{3,2,0,1:T(1,128)}), f32[2,128,1,16]{3,2,0,1:T(1,128)S(1)}, u32[]{:S(2)}, u32[]{:S(2)}) async-start(f32[2,128,1,16]{3,2,0,1:T(1,128)} %copy.46), calls=%async_computation.2 | async-start | bytes 262144 | tf_op jit(solution)/shard_map/all_to_all | solution.py:230
  114.5 6.1 %shard_map.60.prev_ref = bf16[2,4,512,2048]{3,2,1,0:T(8,128)(2,1)} custom-call(s32[2]{0:T(128)} %pad_add_fusion.3.block_ref, bf16[128,1,16,512]{3,2,1,0:T(8,128)(2,1)} %bitcast.534, bf16[128,1,16,512]{3,2,1,0:T(8,128)(2,1)} %bitcast.535), custom_call_target="tpu_custom_call" | custom-call | flops 2147483648 | bytes 6815744 | tf_op jit(solution)/shard_map/pallas_call | solution.py:175
  120.5 6.1 %shard_map.61.prev_ref = bf16[2,4,512,2048]{3,2,1,0:T(8,128)(2,1)} custom-call(s32[2]{0:T(128)} %pad_add_fusion.2.block_ref, bf16[128,1,16,512]{3,2,1,0:T(8,128)(2,1)} %bitcast.13.rows_ref.cols_ref, bf16[128,1,16,512]{3,2,1,0:T(8,128)(2,1)} %bitcast.13.rows_ref.cols_ref, bf16[2,4,512,2048]{3,2,1,0:T(8,128)(2,1)} %shard_map.60.prev_ref), custom_call_target="tpu_custom_call", output_to_operand_aliasing={{}: (3, {})} | custom-call | flops 2147483648 | bytes 6815744 | tf_op jit(solution)/shard_map/pallas_call | solution.py:175
  126.7 0.7 copy.49
  127.4 6.1 %shard_map.62.prev_ref = bf16[2,4,512,2048]{3,2,1,0:T(8,128)(2,1)} custom-call(s32[2]{0:T(128)} %pad_add_fusion.1.block_ref, bf16[128,1,16,512]{3,2,1,0:T(8,128)(2,1)} %bitcast.10.rows_ref.cols_ref, bf16[128,1,16,512]{3,2,1,0:T(8,128)(2,1)} %bitcast.10.rows_ref.cols_ref, bf16[2,4,512,2048]{3,2,1,0:T(8,128)(2,1)} %shard_map.61.prev_ref), custom_call_target="tpu_custom_call", output_to_operand_aliasing={{}: (3, {})} | custom-call | flops 2147483648 | bytes 6815744 | tf_op jit(solution)/shard_map/pallas_call | solution.py:175
  133.4 6.1 %shard_map.63 = bf16[2,4,512,2048]{3,2,1,0:T(8,128)(2,1)} custom-call(s32[2]{0:T(128)} %pad_add_fusion.block_ref, bf16[128,1,16,512]{3,2,1,0:T(8,128)(2,1)} %bitcast.8.rows_ref.cols_ref, bf16[128,1,16,512]{3,2,1,0:T(8,128)(2,1)} %bitcast.8.rows_ref.cols_ref, bf16[2,4,512,2048]{3,2,1,0:T(8,128)(2,1)} %shard_map.62.prev_ref), custom_call_target="tpu_custom_call", output_to_operand_aliasing={{}: (3, {})} | custom-call | flops 2147483648 | bytes 6815744 | tf_op jit(solution)/shard_map/pallas_call | solution.py:175
  (117 shorter events, 5.6 us)
Async XLA Ops:
  4.8 10.2 %copy-start.1 = (s32[16]{0:T(128)S(1)}, s32[16]{0:T(128)}, u32[]{:S(2)}) copy-start(s32[16]{0:T(128)} %param.5) | copy-start | bytes 196
  31.5 41.0 %all-to-all-start.1 = ((bf16[128,16,512]{2,1,0:T(8,128)(2,1)}), bf16[128,16,512]{2,1,0:T(8,128)(2,1)S(1)}, u32[]{:S(2)}, u32[]{:S(2)}) async-start(bf16[128,16,512]{2,1,0:T(8,128)(2,1)} %shard_map.59), calls=%async_computation.1 | async-start | bytes 4194304 | tf_op jit(solution)/shard_map/all_to_all | solution.py:202
  72.5 36.4 %copy-start = (bf16[128,16,512]{2,1,0:T(8,128)(2,1)}, bf16[128,16,512]{2,1,0:T(8,128)(2,1)S(1)}, u32[]{:S(2)}) copy-start(bf16[128,16,512]{2,1,0:T(8,128)(2,1)S(1)} %all-to-all-done.1) | copy-start | bytes 6291460
  72.5 35.1 %all-to-all-start = ((bf16[128,16,512]{2,1,0:T(8,128)(2,1)}), bf16[128,16,512]{2,1,0:T(8,128)(2,1)}, u32[]{:S(2)}, u32[]{:S(2)}) async-start(bf16[128,16,512]{2,1,0:T(8,128)(2,1)} %bitcast.537), calls=%async_computation | async-start | bytes 4194304 | tf_op jit(solution)/shard_map/all_to_all | solution.py:202
  101.1 26.2 %collective-permute-start.1 = (bf16[128,16,512]{2,1,0:T(8,128)(2,1)S(1)}, bf16[128,16,512]{2,1,0:T(8,128)(2,1)}, u32[]{:S(2)}, u32[]{:S(2)}) collective-permute-start(bf16[128,16,512]{2,1,0:T(8,128)(2,1)S(1)} %all-to-all-done.1), channel_id=1, source_target_pairs={{0,1},{1,0},{2,3},{3,2},{4,5},{5,4},{6,7},{7,6},{8,9},{9,8},{10,11... | collective-permute-start | bytes 6291464 | tf_op jit(solution)/shard_map/ppermute | solution.py:210
  107.6 25.8 %collective-permute-start = (bf16[128,16,512]{2,1,0:T(8,128)(2,1)}, bf16[128,16,512]{2,1,0:T(8,128)(2,1)}, u32[]{:S(2)}, u32[]{:S(2)}) collective-permute-start(bf16[128,16,512]{2,1,0:T(8,128)(2,1)} %all-to-all-done), channel_id=1, source_target_pairs={{0,1},{1,0},{2,3},{3,2},{4,5},{5,4},{6,7},{7,6},{8,9},{9,8},{10,11... | collective-permute-start | bytes 6291464 | tf_op jit(solution)/shard_map/ppermute | solution.py:218
  110.7 15.9 %all-to-all-start.2 = ((f32[2,128,1,16]{3,2,0,1:T(1,128)}), f32[2,128,1,16]{3,2,0,1:T(1,128)S(1)}, u32[]{:S(2)}, u32[]{:S(2)}) async-start(f32[2,128,1,16]{3,2,0,1:T(1,128)} %copy.46), calls=%async_computation.2 | async-start | bytes 262144 | tf_op jit(solution)/shard_map/all_to_all | solution.py:230

commit v18 on v15

--- a/solution.py
+++ b/solution.py
@@ -226,13 +226,14 @@
 
     solved = jnp.stack(solve_gains(own.reshape(all_inputs, -1), full_re, full_im))
     owners = solved.reshape(2, devices, 1, input_count)
+    first = correlate_into(None, own, 2 * core + level)
+    owners, first = lax.optimization_barrier((owners, first))
     gains = lax.all_to_all(owners, ("chan", "blk"), split_axis=1, concat_axis=1, tiled=True)
     gains = gains.reshape(2, chan_count, 2, 2, input_count)
     gains = jnp.swapaxes(gains, 2, 3).reshape(2, -1, input_count)
 
-    visibility = None
+    visibility = first
     for data, chan in (
-        (own, 2 * core + level),
         (other, 2 * core + 1 - level),
         (own_partner, 2 - 2 * core + level),
         (other_partner, 3 - 2 * core - level),

time: 141 us -> 144 us (1.021)
  waiting for transfers between devices: 25.9 us -> 29.6 us
    all_to_all x1, waiting for transfers between devices: 0.01 us -> 4 us  [shards(): lax.all_to_all(owners, ('chan', 'blk'), split_axis=1, concat_axis=1, tile...]
  transfers between devices with their start and end apart: 5 -> 5, of which waited for: 2 -> 3; matrix products, arithmetic and copies ran while one was open for 19% -> 19% of each run, Pallas kernels for 13% -> 13%
where the time goes in v18:
time: 144 us; the launch traced here: 143 us
  Pallas kernels  39.9 us (28%)
  waiting for transfers between devices  29.6 us (21%)
  starting transfers between devices  24.1 us (17%)
  local copies, waits for them, and re-layouts  17.4 us (12%)
  other arithmetic  14.3 us (10%)
  matrix products  10.1 us (7%)
  between operations  7.98 us (6%)
    all_to_all x2, waiting for transfers between devices, turn(): lax.all_to_all(send, ('chan', 'blk'), split_axis=0, concat_axis=0, tiled=...  25.6 us
    pallas_call x4, Pallas kernels, correlate(): pl.pallas_call(kernel, grid_spec=spec, out_shape=jax.ShapeDtypeStruct((2,...  24.3 us
    all_to_all x2, starting transfers between devices, turn(): lax.all_to_all(send, ('chan', 'blk'), split_axis=0, concat_axis=0, tiled=...  17.3 us
    pallas_call x1, Pallas kernels, channelize(): pl.pallas_call(transform_kernel, grid=(count // group,), in_specs=[pl.Blo...  15.6 us
    reshape x1, local copies, waits for them, and re-layouts, channelize(): samples = voltages.reshape(count, SPECTRA + TAPS - 1, FRAME)  10.1 us
    dot_general x20, matrix products, exact_dot(): lax.dot_general(lhs, split3(rhs_f32), (dims, ((), ())), preferred_element...  10.1 us
    reduce_sum x10, other arithmetic, sweep(): power = jnp.sum(probe_re * probe_re + probe_im * probe_im)  6.27 us
    all_to_all x1, waiting for transfers between devices, shards(): lax.all_to_all(owners, ('chan', 'blk'), split_axis=1, concat_axis=1, tile...  4 us
  transfers between devices with their start and end apart: 5, of which 3 were waited for; matrix products, arithmetic and copies ran while one was open for 19% of the time, Pallas kernels for 13%

profile of v18, /device:TPU:1, one launch (start us, length us, event | category | flops | bytes accessed | tf_op | source)
XLA Modules:
  0.0 143.3 jit_solution(18042057327315355702)
XLA Ops:
  0.7 0.7 fusion.70.window_ref
  1.4 1.1 cosine_convert_fusion
  2.9 1.1 gather_fusion
  4.0 0.7 copy.32
  4.8 10.1 %reshape.490.samples_ref = s32[16,263,512]{2,1,0:T(8,128)} reshape(s32[16,134656]{1,0:T(8,128)} %param.4) | data formatting | bytes 17235968 | tf_op jit(solution)/shard_map/reshape | solution.py:56
  14.9 0.5 subtract_convert_fusion.20.keep_ref
  15.4 15.6 %shard_map.59 = bf16[128,16,512]{2,1,0:T(8,128)(2,1)} custom-call(f32[16]{0:T(128)} %subtract_convert_fusion.20.keep_ref, f32[8,512]{1,0:T(8,128)} %fusion.70.window_ref, bf16[256,512]{1,0:T(8,128)(2,1)} %bitcast.558, s32[16,263,512]{2,1,0:T(8,128)} %reshape.490.samples_ref), custom_call_target="tpu_custom_call" | custom-call | flops 1107296256 | bytes 10747904 | tf_op jit(solution)/shard_map/pallas_call | solution.py:60
  31.0 11.5 %all-to-all-start.1 = ((bf16[128,16,512]{2,1,0:T(8,128)(2,1)}), bf16[128,16,512]{2,1,0:T(8,128)(2,1)S(1)}, u32[]{:S(2)}, u32[]{:S(2)}) async-start(bf16[128,16,512]{2,1,0:T(8,128)(2,1)} %shard_map.59), calls=%async_computation.1 | async-start | bytes 4194304 | tf_op jit(solution)/shard_map/all_to_all | solution.py:201
  42.6 3.3 %rev.3 = bf16[32,2,2,16,512]{4,3,2,1,0:T(8,128)(2,1)} reverse(bf16[32,2,2,16,512]{4,3,2,1,0:T(8,128)(2,1)} %bitcast.536), dimensions={1} | reverse | bytes 4194304 | tf_op jit(solution)/shard_map/rev | solution.py:196
  45.8 1.0 fusion.163
  46.9 0.7 add_reduce_fusion.9
  48.2 0.7 pad_add_fusion.3.block_ref
  48.9 0.6 pad_add_fusion.2.block_ref
  49.5 0.7 pad_add_fusion.1.block_ref
  50.2 0.7 pad_add_fusion.block_ref
  50.9 21.1 %all-to-all-done.1 = bf16[128,16,512]{2,1,0:T(8,128)(2,1)S(1)} async-done(((bf16[128,16,512]{2,1,0:T(8,128)(2,1)}), bf16[128,16,512]{2,1,0:T(8,128)(2,1)S(1)}, u32[]{:S(2)}, u32[]{:S(2)}) %all-to-all-start.1) | async-done | bytes 2097184 | tf_op jit(solution)/shard_map/all_to_all | solution.py:201
  72.1 5.8 %all-to-all-start = ((bf16[128,16,512]{2,1,0:T(8,128)(2,1)}), bf16[128,16,512]{2,1,0:T(8,128)(2,1)}, u32[]{:S(2)}, u32[]{:S(2)}) async-start(bf16[128,16,512]{2,1,0:T(8,128)(2,1)} %bitcast.537), calls=%async_computation | async-start | bytes 4194304 | tf_op jit(solution)/shard_map/all_to_all | solution.py:201
  78.3 0.6 fusion.99
  79.2 0.4 fusion.12
  79.6 0.6 fusion.105
  80.3 0.6 add_reduce_fusion.8
  82.1 0.6 fusion.111
  82.8 0.6 add_reduce_fusion.7
  84.7 0.6 fusion.117
  85.4 0.6 add_reduce_fusion.6
  87.2 0.6 fusion.123
  87.9 0.6 add_reduce_fusion.5
  89.8 0.6 fusion.129
  90.5 0.6 add_reduce_fusion.4
  92.3 0.6 fusion.135
  93.0 0.6 add_reduce_fusion.3
  94.9 0.6 fusion.141
  95.5 0.6 add_reduce_fusion.2
  97.4 0.6 add_reduce_fusion.1
  98.7 0.6 fusion.147
  99.4 0.6 add_reduce_fusion
  100.7 1.5 %collective-permute-start.1 = (bf16[128,16,512]{2,1,0:T(8,128)(2,1)S(1)}, bf16[128,16,512]{2,1,0:T(8,128)(2,1)}, u32[]{:S(2)}, u32[]{:S(2)}) collective-permute-start(bf16[128,16,512]{2,1,0:T(8,128)(2,1)S(1)} %all-to-all-done.1), channel_id=1, source_target_pairs={{0,1},{1,0},{2,3},{3,2},{4,5},{5,4},{6,7},{7,6},{8,9},{9,8},{10,11... | collective-permute-start | bytes 6291464 | tf_op jit(solution)/shard_map/ppermute | solution.py:209
  102.7 4.5 %all-to-all-done = bf16[128,16,512]{2,1,0:T(8,128)(2,1)} async-done(((bf16[128,16,512]{2,1,0:T(8,128)(2,1)}), bf16[128,16,512]{2,1,0:T(8,128)(2,1)}, u32[]{:S(2)}, u32[]{:S(2)}) %all-to-all-start) | async-done | bytes 2097184 | tf_op jit(solution)/shard_map/all_to_all | solution.py:201
  107.2 1.3 collective-permute-start
  108.5 0.6 fusion.153
  109.6 6.1 %shard_map.60.prev_ref = bf16[2,4,512,2048]{3,2,1,0:T(8,128)(2,1)} custom-call(s32[2]{0:T(128)} %pad_add_fusion.3.block_ref, bf16[128,1,16,512]{3,2,1,0:T(8,128)(2,1)} %bitcast.534, bf16[128,1,16,512]{3,2,1,0:T(8,128)(2,1)} %bitcast.535), custom_call_target="tpu_custom_call" | custom-call | flops 2147483648 | bytes 6815744 | tf_op jit(solution)/shard_map/pallas_call | solution.py:174
  115.7 0.8 copy.39
  116.4 3.9 %all-to-all-start.2 = ((f32[2,128,1,16]{3,2,0,1:T(1,128)}), f32[2,128,1,16]{3,2,0,1:T(1,128)S(1)}, u32[]{:S(2)}, u32[]{:S(2)}) async-start(f32[2,128,1,16]{3,2,0,1:T(1,128)} %copy.39), calls=%async_computation.2 | async-start | bytes 262144 | tf_op jit(solution)/shard_map/all_to_all | solution.py:231
  120.4 6.1 %shard_map.61.prev_ref = bf16[2,4,512,2048]{3,2,1,0:T(8,128)(2,1)} custom-call(s32[2]{0:T(128)} %pad_add_fusion.2.block_ref, bf16[128,1,16,512]{3,2,1,0:T(8,128)(2,1)} %bitcast.13.rows_ref.cols_ref, bf16[128,1,16,512]{3,2,1,0:T(8,128)(2,1)} %bitcast.13.rows_ref.cols_ref, bf16[2,4,512,2048]{3,2,1,0:T(8,128)(2,1)} %shard_map.60.prev_ref), custom_call_target="tpu_custom_call", output_to_operand_aliasing={{}: (3, {})} | custom-call | flops 2147483648 | bytes 6815744 | tf_op jit(solution)/shard_map/pallas_call | solution.py:174
  126.4 4.0 %all-to-all-done.2 = f32[2,128,1,16]{3,2,0,1:T(1,128)S(1)} async-done(((f32[2,128,1,16]{3,2,0,1:T(1,128)}), f32[2,128,1,16]{3,2,0,1:T(1,128)S(1)}, u32[]{:S(2)}, u32[]{:S(2)}) %all-to-all-start.2) | async-done | bytes 16416 | tf_op jit(solution)/shard_map/all_to_all | solution.py:231
  130.5 0.7 copy.42
  131.2 6.1 %shard_map.62.prev_ref = bf16[2,4,512,2048]{3,2,1,0:T(8,128)(2,1)} custom-call(s32[2]{0:T(128)} %pad_add_fusion.1.block_ref, bf16[128,1,16,512]{3,2,1,0:T(8,128)(2,1)} %bitcast.10.rows_ref.cols_ref, bf16[128,1,16,512]{3,2,1,0:T(8,128)(2,1)} %bitcast.10.rows_ref.cols_ref, bf16[2,4,512,2048]{3,2,1,0:T(8,128)(2,1)} %shard_map.61.prev_ref), custom_call_target="tpu_custom_call", output_to_operand_aliasing={{}: (3, {})} | custom-call | flops 2147483648 | bytes 6815744 | tf_op jit(solution)/shard_map/pallas_call | solution.py:174
  137.3 6.1 %shard_map.63 = bf16[2,4,512,2048]{3,2,1,0:T(8,128)(2,1)} custom-call(s32[2]{0:T(128)} %pad_add_fusion.block_ref, bf16[128,1,16,512]{3,2,1,0:T(8,128)(2,1)} %bitcast.8.rows_ref.cols_ref, bf16[128,1,16,512]{3,2,1,0:T(8,128)(2,1)} %bitcast.8.rows_ref.cols_ref, bf16[2,4,512,2048]{3,2,1,0:T(8,128)(2,1)} %shard_map.62.prev_ref), custom_call_target="tpu_custom_call", output_to_operand_aliasing={{}: (3, {})} | custom-call | flops 2147483648 | bytes 6815744 | tf_op jit(solution)/shard_map/pallas_call | solution.py:174
  (119 shorter events, 6.1 us)
Async XLA Ops:
  4.8 10.2 %copy-start.1 = (s32[16]{0:T(128)S(1)}, s32[16]{0:T(128)}, u32[]{:S(2)}) copy-start(s32[16]{0:T(128)} %param.5) | copy-start | bytes 196
  31.0 41.0 %all-to-all-start.1 = ((bf16[128,16,512]{2,1,0:T(8,128)(2,1)}), bf16[128,16,512]{2,1,0:T(8,128)(2,1)S(1)}, u32[]{:S(2)}, u32[]{:S(2)}) async-start(bf16[128,16,512]{2,1,0:T(8,128)(2,1)} %shard_map.59), calls=%async_computation.1 | async-start | bytes 4194304 | tf_op jit(solution)/shard_map/all_to_all | solution.py:201
  72.1 36.4 %copy-start = (bf16[128,16,512]{2,1,0:T(8,128)(2,1)}, bf16[128,16,512]{2,1,0:T(8,128)(2,1)S(1)}, u32[]{:S(2)}) copy-start(bf16[128,16,512]{2,1,0:T(8,128)(2,1)S(1)} %all-to-all-done.1) | copy-start | bytes 6291460
  72.1 35.1 %all-to-all-start = ((bf16[128,16,512]{2,1,0:T(8,128)(2,1)}), bf16[128,16,512]{2,1,0:T(8,128)(2,1)}, u32[]{:S(2)}, u32[]{:S(2)}) async-start(bf16[128,16,512]{2,1,0:T(8,128)(2,1)} %bitcast.537), calls=%async_computation | async-start | bytes 4194304 | tf_op jit(solution)/shard_map/all_to_all | solution.py:201
  100.7 30.5 %collective-permute-start.1 = (bf16[128,16,512]{2,1,0:T(8,128)(2,1)S(1)}, bf16[128,16,512]{2,1,0:T(8,128)(2,1)}, u32[]{:S(2)}, u32[]{:S(2)}) collective-permute-start(bf16[128,16,512]{2,1,0:T(8,128)(2,1)S(1)} %all-to-all-done.1), channel_id=1, source_target_pairs={{0,1},{1,0},{2,3},{3,2},{4,5},{5,4},{6,7},{7,6},{8,9},{9,8},{10,11... | collective-permute-start | bytes 6291464 | tf_op jit(solution)/shard_map/ppermute | solution.py:209
  107.2 30.1 %collective-permute-start = (bf16[128,16,512]{2,1,0:T(8,128)(2,1)}, bf16[128,16,512]{2,1,0:T(8,128)(2,1)}, u32[]{:S(2)}, u32[]{:S(2)}) collective-permute-start(bf16[128,16,512]{2,1,0:T(8,128)(2,1)} %all-to-all-done), channel_id=1, source_target_pairs={{0,1},{1,0},{2,3},{3,2},{4,5},{5,4},{6,7},{7,6},{8,9},{9,8},{10,11... | collective-permute-start | bytes 6291464 | tf_op jit(solution)/shard_map/ppermute | solution.py:217
  116.4 14.0 %all-to-all-start.2 = ((f32[2,128,1,16]{3,2,0,1:T(1,128)}), f32[2,128,1,16]{3,2,0,1:T(1,128)S(1)}, u32[]{:S(2)}, u32[]{:S(2)}) async-start(f32[2,128,1,16]{3,2,0,1:T(1,128)} %copy.39), calls=%async_computation.2 | async-start | bytes 262144 | tf_op jit(solution)/shard_map/all_to_all | solution.py:231
